TPU v7x, 256 devices: a whole 4x4x8 slice. The times are simulated.
256 devices in a mesh: head: 8 (over z), ctx: 32 (over y, x, core).
Axes of the slice: x: 4, y: 4, z: 8, core: 2. Of those that a mesh axis runs over, the one named last changes fastest.
Arguments:
- queries: bfloat16 [16384, 4096], P('ctx', 'head'), may hold values from -6 to 6
- key_head_tensor: bfloat16 [16384, 2048], P('ctx', 'head'), may hold values from -6 to 6
- value_head_tensor: bfloat16 [16384, 2048], P('ctx', 'head'), may hold values from -6 to 6
- output_gradient: bfloat16 [16384, 4096], P('ctx', 'head'), may hold values from -6 to 6
- adapter_up_matrix: bfloat16 [16, 4096], P(None, 'head'), may hold values from -0.09375 to 0.09375
- document_block_counts: int32 [32], replicated, may hold values from 1 to 32, 128 in all
Outputs:
- attention_output: bfloat16 [16384, 4096], P('ctx', 'head')
- query_gradient: bfloat16 [16384, 4096], P('ctx', 'head')
- key_gradient: bfloat16 [16384, 2048], P('ctx', 'head')
- value_gradient: bfloat16 [16384, 2048], P('ctx', 'head')
- adapter_gradient: float32 [16384, 16], P('ctx')
Inputs may be any that keep to these rules, and one draw needn't show every extreme that they name: Document i holds document_block_counts[i] * 128 consecutive tokens; the documents fill all 128 blocks in order.
All inputs are finite; a program needn't handle non-finite values.
Results may differ from a plain program's by a relative error of at most 0.012.
Values may be sent and summed in bfloat16 or wider, within the bound.
No kernel may reach another device: no remote copies, remote signals or barrier semaphores. Data moves between devices by JAX's collectives and lax.ppermute only.
A program may use at most 128 MiB of HBM per device.

v0:
```python
import jax
import jax.numpy as jnp
from jax import lax
from jax.sharding import PartitionSpec as P

HEAD_SIZE = 128
WIN = 1024
BLK = 128


softmax_scale = 168.0 ** (-0.5)
masked_value = -1e30


def passed_along(block, axis, distance):
    devices = range(lax.axis_size(axis))
    route = [(i - distance, i) for i in devices if i - distance in devices]
    return lax.ppermute(block, axis, route)


def doc_index(positions, doc_ends):
    counted = jnp.sum((positions[:, None] >= doc_ends[None, :]).astype(jnp.int32), axis=1)
    return jnp.where(positions < 0, -1, counted)


def span_scores(query_tile, key_span, query_pos, key_pos, doc_ends):
    scores = (
        jnp.einsum("iged,jgd->geij", query_tile, key_span, preferred_element_type=jnp.float32)
        * softmax_scale
    )
    row_pos = query_pos + jnp.arange(query_tile.shape[0], dtype=jnp.int32)
    col_pos = key_pos + jnp.arange(key_span.shape[0], dtype=jnp.int32)
    offsets = row_pos[:, None] - col_pos[None, :]
    same_doc = doc_index(row_pos, doc_ends)[:, None] == doc_index(col_pos, doc_ends)[None, :]
    allowed = same_doc & (offsets >= 0) & (offsets < WIN)
    return (scores, allowed)


def attend_span(query_tile, grad_tile, key_span, value_span, query_pos, key_pos, doc_ends):
    scores, allowed = span_scores(query_tile, key_span, query_pos, key_pos, doc_ends)
    attended = None
    masked = jnp.where(allowed, scores, masked_value)
    row_max = jnp.max(masked, axis=-1)
    row_sum = jnp.sum(jnp.where(allowed, jnp.exp(masked - row_max[..., None]), 0.0), axis=-1)
    log_norm = row_max + jnp.log(row_sum)
    weights = jnp.where(allowed, jnp.exp(scores - log_norm[..., None]), 0.0)
    weights_low = weights.astype(jnp.bfloat16)
    attended = jnp.einsum(
        "geij,jgd->iged", weights_low, value_span, preferred_element_type=jnp.float32
    )
    row_dot = jnp.transpose(jnp.sum(grad_tile.astype(jnp.float32) * attended, axis=-1), (1, 2, 0))
    weight_grad = jnp.einsum(
        "iged,jgd->geij", grad_tile, value_span, preferred_element_type=jnp.float32
    )
    score_grad = (weights * (weight_grad - row_dot[..., None])).astype(jnp.bfloat16)
    key_part = softmax_scale * jnp.einsum(
        "geij,iged->jgd", score_grad, query_tile, preferred_element_type=jnp.float32
    )
    value_part = jnp.einsum(
        "geij,iged->jgd", weights_low, grad_tile, preferred_element_type=jnp.float32
    )
    return (attended, score_grad, log_norm, row_dot, key_part, value_part)


def add_rows(total, part):
    return total + part


def body(
    queries,
    key_head_tensor,
    value_head_tensor,
    output_gradient,
    adapter_up_matrix,
    document_block_counts,
):
    tokens_here = queries.shape[0]
    query_cols = queries.shape[1]
    key_cols = key_head_tensor.shape[1]
    group_count = key_cols // HEAD_SIZE
    edge_rows = min(WIN, tokens_here)
    hop_count = WIN // edge_rows
    block_rows = min(tokens_here, 512)
    blocks = tokens_here // block_rows
    first_pos = lax.axis_index("ctx") * tokens_here
    lowest = first_pos - WIN
    doc_ends = jnp.cumsum(document_block_counts) * BLK
    joined = jnp.concatenate([key_head_tensor, value_head_tensor], axis=1)
    arrived = []
    moving = joined
    for hop_num in range(hop_count):
        moving = passed_along(moving, "ctx", 1)
        arrived.append(moving)
    extended = jnp.concatenate(arrived[::-1] + [joined], axis=0)
    ext_keys = extended[:, :key_cols].reshape(WIN + tokens_here, group_count, HEAD_SIZE)
    ext_values = extended[:, key_cols:].reshape(WIN + tokens_here, group_count, HEAD_SIZE)
    query_heads = queries.reshape(tokens_here, group_count, 2, HEAD_SIZE)
    grad_heads = output_gradient.reshape(tokens_here, group_count, 2, HEAD_SIZE)

    def one_block(block_num, buffers):
        out_buf, query_buf, key_acc, value_acc, norm_buf, dot_buf = buffers
        row_first = block_num * block_rows
        attended, score_grad, log_norm, row_dot, key_part, value_part = attend_span(
            query_heads,
            grad_heads,
            ext_keys,
            ext_values,
            first_pos + row_first,
            lowest + row_first,
            doc_ends,
        )
        query_grad = softmax_scale * jnp.einsum(
            "geij,jgd->iged", score_grad, ext_keys, preferred_element_type=jnp.float32
        )
        key_acc = add_rows(key_acc, key_part)
        value_acc = add_rows(value_acc, value_part)
        out_buf = attended.astype(jnp.bfloat16)
        query_buf = query_grad.astype(jnp.bfloat16)
        norm_buf = log_norm.reshape(2 * group_count, block_rows)
        dot_buf = row_dot.reshape(2 * group_count, block_rows)
        return (out_buf, query_buf, key_acc, value_acc, norm_buf, dot_buf)

    start_bufs = (
        jnp.zeros((tokens_here, group_count, 2, HEAD_SIZE), jnp.bfloat16),
        jnp.zeros((tokens_here, group_count, 2, HEAD_SIZE), jnp.bfloat16),
        jnp.zeros((WIN + tokens_here, group_count, HEAD_SIZE), jnp.float32),
        jnp.zeros((WIN + tokens_here, group_count, HEAD_SIZE), jnp.float32),
        jnp.zeros((2 * group_count, tokens_here), jnp.float32),
        jnp.zeros((2 * group_count, tokens_here), jnp.float32),
    )
    out_buf, query_buf, key_acc, value_acc, norm_buf, dot_buf = lax.fori_loop(
        0, blocks, one_block, start_bufs
    )
    halo_grads = jnp.concatenate(
        [key_acc[:WIN].reshape(WIN, key_cols), value_acc[:WIN].reshape(WIN, key_cols)], axis=1
    )
    returned = jnp.zeros((edge_rows, 2 * key_cols), jnp.float32)
    for hop_num in range(hop_count):
        segment = halo_grads[
            (hop_count - 1 - hop_num) * edge_rows : (hop_count - hop_num) * edge_rows
        ]
        returned = returned + passed_along(
            segment.astype(jnp.bfloat16), "ctx", -(hop_num + 1)
        ).astype(segment.dtype)
    key_total = key_acc[WIN:].reshape(tokens_here, key_cols)
    value_total = value_acc[WIN:].reshape(tokens_here, key_cols)
    cut_row = tokens_here - edge_rows
    key_total = jnp.concatenate([key_total[:cut_row], key_total + returned[:, :key_cols]], axis=0)
    value_total = jnp.concatenate(
        [value_total[:cut_row], value_total + returned[:, key_cols:]], axis=0
    )
    flattened_query = query_buf.reshape(tokens_here, query_cols)
    adapter_portion = lax.dot_general(
        flattened_query,
        adapter_up_matrix,
        (((1,), (1,)), ((), ())),
        preferred_element_type=jnp.float32,
    )
    adapter_gradient = lax.psum(adapter_portion.astype(jnp.bfloat16), "head").astype(jnp.float32)
    return (
        out_buf.reshape(tokens_here, query_cols),
        flattened_query,
        key_total.astype(jnp.bfloat16),
        value_total.astype(jnp.bfloat16),
        adapter_gradient,
    )


def solution(mesh):
    in_specs = (
        P("ctx", "head"),
        P("ctx", "head"),
        P("ctx", "head"),
        P("ctx", "head"),
        P(None, "head"),
        P(),
    )
    out_specs = (
        P("ctx", "head"),
        P("ctx", "head"),
        P("ctx", "head"),
        P("ctx", "head"),
        P("ctx", None),
    )
    return jax.shard_map(body, mesh=mesh, in_specs=in_specs, out_specs=out_specs, check_vma=False)
```

profile of v0, /device:TPU:24, one launch (start us, length us, event | category | flops | bytes accessed | tf_op | source)
XLA Modules:
  0.0 110.1 jit_solution(6461842222806312211)
XLA Ops:
  0.6 0.0 copy-start
  0.6 1.1 copy.49
  1.7 1.1 copy.48
  2.9 1.9 %collective-permute-start = (bf16[512,512]{0,1:T(8,128)(2,1)S(1)}, bf16[512,512]{0,1:T(8,128)(2,1)S(1)}, u32[]{:S(2)}, u32[]{:S(2)}) collective-permute-start(bf16[512,512]{0,1:T(8,128)(2,1)S(1)} %pad_maximum_fusion), channel_id=1, source_target_pairs={{0,1},{1,2},{2,3},{3,4},{4,5},{5,6},{6,7},{7,8},{8,9},{9,10},{10,1... | collective-permute-start | bytes 1572872 | tf_op jit(solution)/shard_map/ppermute | solution.py:18
  4.8 0.7 copy.50
  5.6 0.1 reduce-window.8
  5.6 0.1 multiply_reduce_fusion.1
  5.8 0.1 convert_reduce_fusion.1
  5.8 0.1 convert_reduce_fusion
  6.0 9.5 %collective-permute-done = bf16[512,512]{0,1:T(8,128)(2,1)S(1)} collective-permute-done((bf16[512,512]{0,1:T(8,128)(2,1)S(1)}, bf16[512,512]{0,1:T(8,128)(2,1)S(1)}, u32[]{:S(2)}, u32[]{:S(2)}) %collective-permute-start) | collective-permute-done | bytes 524320 | tf_op jit(solution)/shard_map/ppermute | solution.py:18
  15.5 1.9 %collective-permute-start.1 = (bf16[512,512]{0,1:T(8,128)(2,1)S(1)}, bf16[512,512]{0,1:T(8,128)(2,1)S(1)}, u32[]{:S(2)}, u32[]{:S(2)}) collective-permute-start(bf16[512,512]{0,1:T(8,128)(2,1)S(1)} %collective-permute-done), channel_id=1, source_target_pairs={{0,1},{1,2},{2,3},{3,4},{4,5},{5,6},{6,7},{7,8},{8,9},{9,10},{10,1... | collective-permute-start | bytes 1572872 | tf_op jit(solution)/shard_map/ppermute | solution.py:18
  17.4 2.0 %copy.54 = bf16[512,512]{0,1:T(8,128)(2,1)} copy(bf16[512,512]{1,0:T(8,128)(2,1)} %param.9) | data formatting | bytes 1048576 | tf_op args[3]
  19.5 1.3 %copy.82 = bf16[512,512]{0,1:T(8,128)(2,1)S(1)} copy(bf16[512,512]{1,0:T(8,128)(2,1)} %param.6) | data formatting | bytes 1048576 | tf_op jit(solution)/shard_map/reshape | solution.py:97
  20.7 1.3 %fusion.7 = pred[512,1536]{0,1:T(8,128)(4,1)S(1)} fusion(s32[1536]{0:T(1024)S(1)} %iota_add_fusion, s32[512]{0:T(512)S(1)} %iota_add_fusion.1, s32[512]{0:T(512)S(1)} %compare_select_fusion.1, s32[1536]{0:T(1024)S(1)} %compare_select_fusion), kind=kLoop, calls=%fused_computation.13 | loop fusion | flops 4718592 | bytes 802816 | tf_op jit(solution)/shard_map/while/body/eval_jaxpr/and | solution.py:35
  22.1 6.0 %collective-permute-done.1 = bf16[512,512]{0,1:T(8,128)(2,1)S(1)} collective-permute-done((bf16[512,512]{0,1:T(8,128)(2,1)S(1)}, bf16[512,512]{0,1:T(8,128)(2,1)S(1)}, u32[]{:S(2)}, u32[]{:S(2)}) %collective-permute-start.1) | collective-permute-done | bytes 524320 | tf_op jit(solution)/shard_map/ppermute | solution.py:18
  28.1 0.1 maximum_maximum_fusion
  28.2 0.1 fusion.15
  28.3 2.5 %fusion.4 = (f32[2,2,512]{2,1,0:T(2,128)S(1)}, f32[2,1536,512,2]{2,1,3,0:T(8,128)S(1)}) fusion(pred[512,1536]{0,1:T(8,128)(4,1)S(1)} %fusion.7, bf16[1536,2,128,1]{0,2,3,1:T(8,128)(2,1)S(1)} %bitcast.84, bf16[512,2,2,128]{0,3,2,1:T(8,128)(2,1)S(1)} %bitcast.86), kind=kOutput, calls=%fused_computation.8 | convolution fusion | flops 814741504 | bytes 14688256 | tf_op jit(solution)/shard_map/while/body/eval_jaxpr/iged,jgd->geij/dot_general | solution.py:28
  30.8 0.0 copy-start.2
  30.8 0.0 copy-start.4
  30.8 3.1 %select_reduce_fusion = f32[2,2,512]{2,1,0:T(2,128)S(1)} fusion(f32[2,1536,512,2]{2,1,3,0:T(8,128)S(1)} %get-tuple-element.66, f32[2,2,512]{2,1,0:T(2,128)S(1)} %get-tuple-element.65, pred[512,1536]{0,1:T(8,128)(4,1)S(1)} %fusion.7), kind=kLoop, calls=%fused_computation.7 | loop fusion | flops 15726592 | bytes 13385728 | tf_op jit(solution)/shard_map/while/body/eval_jaxpr/reduce_sum | solution.py:44
  34.0 1.4 %copy-done.2 = f32[2,1536,512,2]{2,1,3,0:T(8,128)} copy-done((f32[2,1536,512,2]{2,1,3,0:T(8,128)}, f32[2,1536,512,2]{2,1,3,0:T(8,128)S(1)}, u32[]{:S(2)}) %copy-start.2) | copy-done | bytes 12582936
  35.4 0.0 copy-done.4
  35.4 6.2 %convolution_bitcast_fusion = f32[1536,2,128]{0,2,1:T(8,128)S(1)} fusion(bf16[512,2,2,128]{0,3,2,1:T(8,128)(2,1)S(1)} %bitcast.94, f32[2,1536,512,2]{2,1,3,0:T(8,128)} %copy-done.2, f32[2,2,512]{2,1,0:T(2,128)S(1)} %log_add_fusion, pred[512,1536]{0,1:T(8,128)(4,1)S(1)} %fusion.7), kind=kOutput, calls=%fused_computation.14 | convolution fusion | flops 817889280 | bytes 15474688 | tf_op jit(solution)/shard_map/while/body/eval_jaxpr/geij,iged->jgd/dot_general | solution.py:59
  41.6 0.0 copy-start.3
  41.6 0.1 slice.46
  41.7 8.9 %multiply_reduce_fusion = (f32[512,2,2]{0,2,1:T(2,128)S(1)}, bf16[512,2,2,128]{0,3,2,1:T(8,128)(2,1)}) fusion(bf16[512,512]{0,1:T(8,128)(2,1)S(1)} %copy-done.4, bf16[1536,2,128,1]{0,2,3,1:T(8,128)(2,1)S(1)} %bitcast.92, f32[2,1536,512,2]{2,1,3,0:T(8,128)} %copy-done.2, f32[2,2,512]{2,1,0:T(2,128)S(1)} %log_add_fusion, pred[512,1536]{0,1:T(8,128)(4,1)S(1)} %fusion.7), kind=kOutput, calls=%fused_computation.25 | convolution fusion | flops 818935808 | bytes 15220736 | tf_op jit(solution)/shard_map/while/body/eval_jaxpr/geij,jgd->iged/dot_general | solution.py:48
  50.6 0.0 copy-done.3
  50.6 7.4 %fusion.1 = bf16[2,2,512,1536]{2,3,1,0:T(8,128)(2,1)S(1)} fusion(f32[2,1536,512,2]{2,1,3,0:T(8,128)} %copy-done.2, bf16[1536,2,128,1]{0,2,3,1:T(8,128)(2,1)S(1)} %bitcast.93, bf16[512,2,2,128]{0,3,2,1:T(8,128)(2,1)S(1)} %bitcast.95, f32[2,2,512]{2,1,0:T(2,128)S(1)} %bitcast.98, f32[2,2,512]{2,1,0:T(2,128)S(1)} %log_add_fusion, pred[512,1536]{0,1:T(8,128)(4,1)S(1)} %fusion.7), kind=kOutput, calls=%fused_computation.2 | convolution fusion | flops 824180736 | bytes 20987904 | tf_op jit(solution)/shard_map/while/body/eval_jaxpr/iged,jgd->geij/dot_general | solution.py:52
  58.1 0.0 copy-start.1
  58.1 2.7 %copy-done.1 = bf16[2,2,512,1536]{2,3,1,0:T(8,128)(2,1)} copy-done((bf16[2,2,512,1536]{2,3,1,0:T(8,128)(2,1)}, bf16[2,2,512,1536]{2,3,1,0:T(8,128)(2,1)S(1)}, u32[]{:S(2)}) %copy-start.1) | copy-done | bytes 6291480
  60.7 0.0 copy-start.5
  60.7 2.1 %fusion.9 = f32[1536,2,128]{0,2,1:T(8,128)S(1)} fusion(bf16[2,2,512,1536]{2,3,1,0:T(8,128)(2,1)S(1)} %fusion.1, bf16[512,2,2,128]{0,3,2,1:T(8,128)(2,1)S(1)} %bitcast.87), kind=kOutput, calls=%fused_computation.17 | convolution fusion | flops 805699584 | bytes 8388608 | tf_op jit(solution)/shard_map/while/body/eval_jaxpr/geij,iged->jgd/dot_general | solution.py:56
  62.9 0.1 slice.45
  63.0 0.0 copy-done.5
  63.0 1.0 copy.65
  64.0 0.2 copy.62
  64.2 0.2 copy.61
  64.4 0.0 slice-start
  64.4 0.1 maximum_convert_fusion
  64.5 0.9 fusion.16
  65.4 1.9 %collective-permute-start.3 = (bf16[512,512]{1,0:T(8,128)(2,1)}, bf16[512,512]{1,0:T(8,128)(2,1)S(1)}, u32[]{:S(2)}, u32[]{:S(2)}) collective-permute-start(bf16[512,512]{1,0:T(8,128)(2,1)} %get-tuple-element.62), channel_id=1, source_target_pairs={{2,0},{3,1},{4,2},{5,3},{6,4},{7,5},{8,6},{9,7},{10,8},{11,9},{12,... | collective-permute-start | bytes 1572872 | tf_op jit(solution)/shard_map/ppermute | solution.py:18
  67.3 1.9 %collective-permute-start.2 = (bf16[512,512]{1,0:T(8,128)(2,1)S(1)}, bf16[512,512]{1,0:T(8,128)(2,1)}, u32[]{:S(2)}, u32[]{:S(2)}) collective-permute-start(bf16[512,512]{1,0:T(8,128)(2,1)S(1)} %get-tuple-element.61), channel_id=1, source_target_pairs={{1,0},{2,1},{3,2},{4,3},{5,4},{6,5},{7,6},{8,7},{9,8},{10,9},{11,1... | collective-permute-start | bytes 1572872 | tf_op jit(solution)/shard_map/ppermute | solution.py:18
  69.2 3.8 %fusion.10 = bf16[2,128,2,512]{3,1,2,0:T(8,128)(2,1)S(1)} fusion(bf16[1536,2,128,1]{0,2,3,1:T(8,128)(2,1)S(1)} %bitcast.85, bf16[2,2,512,1536]{2,3,1,0:T(8,128)(2,1)} %copy-done.1), kind=kOutput, calls=%fused_computation.22 | convolution fusion | flops 805830656 | bytes 7602176 | tf_op jit(solution)/shard_map/while/body/eval_jaxpr/geij,jgd->iged/dot_general | solution.py:112
  73.0 1.0 copy.66
  74.0 0.0 slice-done
  74.0 0.2 copy.64
  74.2 0.2 copy.63
  74.4 0.0 copy-done
  74.4 0.2 convolution_convert_fusion
  74.6 32.8 %psum.7 = bf16[512,16]{0,1:T(8,128)(2,1)S(1)} all-reduce(bf16[512,16]{0,1:T(8,128)(2,1)S(1)} %convolution_convert_fusion), channel_id=1, replica_groups=mesh['head'=8,'ctx'=32] {'head'}, use_global_device_ids=true, to_apply=%region_6.7 | all-reduce | flops 8192 | bytes 32768 | tf_op jit(solution)/shard_map/psum | solution.py:159
  107.4 0.6 convert_element_type.64
  108.0 0.0 collective-permute-done.3
  108.0 0.0 collective-permute-done.2
  108.0 1.2 %convert_add_fusion = f32[512,512]{1,0:T(8,128)S(1)} fusion(bf16[512,512]{1,0:T(8,128)(2,1)S(1)} %collective-permute-done.3, bf16[512,512]{1,0:T(8,128)(2,1)} %collective-permute-done.2), kind=kLoop, calls=%fused_computation.24 | loop fusion | flops 786432 | bytes 2097152 | tf_op jit(solution)/shard_map/add | solution.py:142
  109.2 0.9 fusion.11
  (7 shorter events, 0.1 us)
Async XLA Ops:
  0.6 73.8 %copy-start = (bf16[16,512]{1,0:T(8,128)(2,1)S(1)}, bf16[16,512]{1,0:T(8,128)(2,1)}, u32[]{:S(2)}) copy-start(bf16[16,512]{1,0:T(8,128)(2,1)} %param.10) | copy-start | bytes 49156
  2.9 12.6 %collective-permute-start = (bf16[512,512]{0,1:T(8,128)(2,1)S(1)}, bf16[512,512]{0,1:T(8,128)(2,1)S(1)}, u32[]{:S(2)}, u32[]{:S(2)}) collective-permute-start(bf16[512,512]{0,1:T(8,128)(2,1)S(1)} %pad_maximum_fusion), channel_id=1, source_target_pairs={{0,1},{1,2},{2,3},{3,4},{4,5},{5,6},{6,7},{7,8},{8,9},{9,10},{10,1... | collective-permute-start | bytes 1572872 | tf_op jit(solution)/shard_map/ppermute | solution.py:18
  15.5 12.6 %collective-permute-start.1 = (bf16[512,512]{0,1:T(8,128)(2,1)S(1)}, bf16[512,512]{0,1:T(8,128)(2,1)S(1)}, u32[]{:S(2)}, u32[]{:S(2)}) collective-permute-start(bf16[512,512]{0,1:T(8,128)(2,1)S(1)} %collective-permute-done), channel_id=1, source_target_pairs={{0,1},{1,2},{2,3},{3,4},{4,5},{5,6},{6,7},{7,8},{8,9},{9,10},{10,1... | collective-permute-start | bytes 1572872 | tf_op jit(solution)/shard_map/ppermute | solution.py:18
  30.8 4.6 %copy-start.2 = (f32[2,1536,512,2]{2,1,3,0:T(8,128)}, f32[2,1536,512,2]{2,1,3,0:T(8,128)S(1)}, u32[]{:S(2)}) copy-start(f32[2,1536,512,2]{2,1,3,0:T(8,128)S(1)} %get-tuple-element.66) | copy-start | bytes 37748740
  30.8 4.6 %copy-start.4 = (bf16[512,512]{0,1:T(8,128)(2,1)S(1)}, bf16[512,512]{0,1:T(8,128)(2,1)}, u32[]{:S(2)}) copy-start(bf16[512,512]{0,1:T(8,128)(2,1)} %copy.54) | copy-start | bytes 1572868
  41.6 9.0 %copy-start.3 = (f32[1536,2,128]{0,2,1:T(8,128)}, f32[1536,2,128]{0,2,1:T(8,128)S(1)}, u32[]{:S(2)}) copy-start(f32[1536,2,128]{0,2,1:T(8,128)S(1)} %convolution_bitcast_fusion) | copy-start | bytes 4718596
  58.1 2.7 %copy-start.1 = (bf16[2,2,512,1536]{2,3,1,0:T(8,128)(2,1)}, bf16[2,2,512,1536]{2,3,1,0:T(8,128)(2,1)S(1)}, u32[]{:S(2)}) copy-start(bf16[2,2,512,1536]{2,3,1,0:T(8,128)(2,1)S(1)} %fusion.1) | copy-start | bytes 18874372
  60.7 2.3 %copy-start.5 = (bf16[512,2,2,128]{0,3,2,1:T(8,128)(2,1)S(1)}, bf16[512,2,2,128]{0,3,2,1:T(8,128)(2,1)}, u32[]{:S(2)}) copy-start(bf16[512,2,2,128]{0,3,2,1:T(8,128)(2,1)} %get-tuple-element.64) | copy-start | bytes 1572868
  64.4 9.6 %slice-start = ((f32[1536,2,128]{0,2,1:T(8,128)}), f32[512,2,128]{0,2,1:T(8,128)S(1)}, s32[]{:S(2)}) async-start(f32[1536,2,128]{0,2,1:T(8,128)} %copy-done.3), calls=%async_computation | async-start | bytes 1048576 | tf_op jit(solution)/shard_map/slice | solution.py:146
  65.4 42.6 %collective-permute-start.3 = (bf16[512,512]{1,0:T(8,128)(2,1)}, bf16[512,512]{1,0:T(8,128)(2,1)S(1)}, u32[]{:S(2)}, u32[]{:S(2)}) collective-permute-start(bf16[512,512]{1,0:T(8,128)(2,1)} %get-tuple-element.62), channel_id=1, source_target_pairs={{2,0},{3,1},{4,2},{5,3},{6,4},{7,5},{8,6},{9,7},{10,8},{11,9},{12,... | collective-permute-start | bytes 1572872 | tf_op jit(solution)/shard_map/ppermute | solution.py:18
  67.3 40.7 %collective-permute-start.2 = (bf16[512,512]{1,0:T(8,128)(2,1)S(1)}, bf16[512,512]{1,0:T(8,128)(2,1)}, u32[]{:S(2)}, u32[]{:S(2)}) collective-permute-start(bf16[512,512]{1,0:T(8,128)(2,1)S(1)} %get-tuple-element.61), channel_id=1, source_target_pairs={{1,0},{2,1},{3,2},{4,3},{5,4},{6,5},{7,6},{8,7},{9,8},{10,9},{11,1... | collective-permute-start | bytes 1572872 | tf_op jit(solution)/shard_map/ppermute | solution.py:18
where the time goes:
time: 111 us; the launch traced here: 110 us
  blocking collectives  32.8 us (30%)
  matrix products  31.1 us (28%)
  waiting for transfers between devices  15.6 us (14%)
  local copies, waits for them, and re-layouts  14.3 us (13%)
  other arithmetic  7.76 us (7%)
  starting transfers between devices  7.66 us (7%)
    psum x1, blocking collectives, body(): lax.psum(adapter_portion.astype(jnp.bfloat16), 'head').astype(jnp.float32)  32.8 us
    ppermute x4, waiting for transfers between devices, passed_along(): return lax.ppermute(block, axis, route)  15.6 us
    unnamed x17, local copies, waits for them, and re-layouts  10.3 us
    dot_general x1, matrix products, attend_span(): jnp.einsum('geij,jgd->iged', weights_low, value_span, preferred_element_t...  8.91 us
    ppermute x4, starting transfers between devices, passed_along(): return lax.ppermute(block, axis, route)  7.66 us
    dot_general x1, matrix products, attend_span(): jnp.einsum('iged,jgd->geij', grad_tile, value_span, preferred_element_typ...  7.44 us
    dot_general x1, matrix products, attend_span(): jnp.einsum('geij,iged->jgd', weights_low, grad_tile, preferred_element_ty...  6.2 us
    dot_general x1, matrix products, one_block(): jnp.einsum('geij,jgd->iged', score_grad, ext_keys, preferred_element_type...  3.77 us
  transfers between devices with their start and end apart: 4, of which 2 were waited for; matrix products, arithmetic and copies ran while one was open for 11% of the time, Pallas kernels for 0%

commit v1 on v0

--- a/solution.py
+++ b/solution.py
@@ -16,6 +16,21 @@
     devices = range(lax.axis_size(axis))
     route = [(i - distance, i) for i in devices if i - distance in devices]
     return lax.ppermute(block, axis, route)
+
+
+def gathered_sum(part, axis):
+    count = lax.axis_size(axis)
+    received = [part]
+    for shift in range(1, count):
+        route = [(i, (i + shift) % count) for i in range(count)]
+        received.append(lax.ppermute(part, axis, route))
+    stacked = jnp.stack(received).astype(jnp.float32)
+    order = (lax.axis_index(axis) - jnp.arange(count, dtype=jnp.int32)) % count
+    in_order = jnp.take(stacked, order, axis=0)
+    total = in_order[0]
+    for j in range(1, count):
+        total = total + in_order[j]
+    return total
 
 
 def doc_index(positions, doc_ends):
@@ -87,10 +102,8 @@
     doc_ends = jnp.cumsum(document_block_counts) * BLK
     joined = jnp.concatenate([key_head_tensor, value_head_tensor], axis=1)
     arrived = []
-    moving = joined
     for hop_num in range(hop_count):
-        moving = passed_along(moving, "ctx", 1)
-        arrived.append(moving)
+        arrived.append(passed_along(joined, "ctx", hop_num + 1))
     extended = jnp.concatenate(arrived[::-1] + [joined], axis=0)
     ext_keys = extended[:, :key_cols].reshape(WIN + tokens_here, group_count, HEAD_SIZE)
     ext_values = extended[:, key_cols:].reshape(WIN + tokens_here, group_count, HEAD_SIZE)
@@ -156,7 +169,7 @@
         (((1,), (1,)), ((), ())),
         preferred_element_type=jnp.float32,
     )
-    adapter_gradient = lax.psum(adapter_portion.astype(jnp.bfloat16), "head").astype(jnp.float32)
+    adapter_gradient = gathered_sum(adapter_portion.astype(jnp.bfloat16), "head")
     return (
         out_buf.reshape(tokens_here, query_cols),
         flattened_query,

time: 111 us -> 108 us (0.973)
  the two profiles are of different devices: /device:TPU:24 before, /device:TPU:14 now
where the time goes in v1:
time: 108 us
  waiting for transfers between devices  28.8 us (27%)
  starting transfers between devices  28.4 us (26%)
  matrix products  25.6 us (24%)
  local copies, waits for them, and re-layouts  16 us (15%)
  other arithmetic  8.12 us (8%)
    ppermute x4, waiting for transfers between devices, passed_along(): return lax.ppermute(block, axis, route)  28.8 us
    ppermute x7, starting transfers between devices, gathered_sum(): received.append(lax.ppermute(part, axis, route))  18.4 us
    ppermute x4, starting transfers between devices, passed_along(): return lax.ppermute(block, axis, route)  9.96 us
    dot_general x1, matrix products, attend_span(): jnp.einsum('geij,iged->jgd', weights_low, grad_tile, preferred_element_ty...  8.65 us
    unnamed x17, local copies, waits for them, and re-layouts  7.87 us
    dot_general x1, matrix products, attend_span(): jnp.einsum('iged,jgd->geij', grad_tile, value_span, preferred_element_typ...  7.26 us
    dot_general x1, matrix products, attend_span(): jnp.einsum('geij,jgd->iged', weights_low, value_span, preferred_element_t...  3.83 us
    reduce_sum x1, other arithmetic, attend_span(): jnp.sum(jnp.where(allowed, jnp.exp(masked - row_max[..., None]), 0.0), ax...  3.18 us
  transfers between devices with their start and end apart: 11, of which 4 were waited for; matrix products, arithmetic and copies ran while one was open for 25% of the time, Pallas kernels for 0%

profile of v1, /device:TPU:14, one launch (start us, length us, event | category | flops | bytes accessed | tf_op | source)
XLA Modules:
  0.0 107.8 jit_solution(13486635347991202253)
XLA Ops:
  0.6 0.0 copy-start
  0.6 1.1 %copy.48 = bf16[512,256]{0,1:T(8,128)(2,1)S(1)} copy(bf16[512,256]{1,0:T(8,128)(2,1)} %param.7) | data formatting | bytes 524288 | tf_op args[1]
  1.7 1.1 %copy.49 = bf16[512,256]{0,1:T(8,128)(2,1)S(1)} copy(bf16[512,256]{1,0:T(8,128)(2,1)} %param.8) | data formatting | bytes 524288 | tf_op args[2]
  2.9 3.4 %collective-permute-start = (bf16[512,512]{0,1:T(8,128)(2,1)S(1)}, bf16[512,512]{0,1:T(8,128)(2,1)S(1)}, u32[]{:S(2)}, u32[]{:S(2)}) collective-permute-start(bf16[512,512]{0,1:T(8,128)(2,1)S(1)} %pad_maximum_fusion), channel_id=1, source_target_pairs={{0,2},{1,3},{2,4},{3,5},{4,6},{5,7},{6,8},{7,9},{8,10},{9,11},{10,... | collective-permute-start | bytes 1572872 | tf_op jit(solution)/shard_map/ppermute | solution.py:18
  6.3 1.9 %collective-permute-start.1 = (bf16[512,512]{0,1:T(8,128)(2,1)S(1)}, bf16[512,512]{0,1:T(8,128)(2,1)S(1)}, u32[]{:S(2)}, u32[]{:S(2)}) collective-permute-start(bf16[512,512]{0,1:T(8,128)(2,1)S(1)} %pad_maximum_fusion), channel_id=1, source_target_pairs={{0,1},{1,2},{2,3},{3,4},{4,5},{5,6},{6,7},{7,8},{8,9},{9,10},{10,1... | collective-permute-start | bytes 1572872 | tf_op jit(solution)/shard_map/ppermute | solution.py:18
  8.3 0.7 copy.50
  9.0 0.1 reduce-window.8
  9.1 0.1 multiply_reduce_fusion.1
  9.2 0.1 convert_reduce_fusion
  9.3 0.1 convert_reduce_fusion.1
  9.4 1.3 %copy.82 = bf16[512,512]{0,1:T(8,128)(2,1)S(1)} copy(bf16[512,512]{1,0:T(8,128)(2,1)} %param.6) | data formatting | bytes 1048576 | tf_op jit(solution)/shard_map/reshape | solution.py:110
  10.7 1.3 %copy.54 = bf16[512,512]{0,1:T(8,128)(2,1)S(1)} copy(bf16[512,512]{1,0:T(8,128)(2,1)} %param.9) | data formatting | bytes 1048576 | tf_op args[3]
  12.0 1.3 %fusion.7 = pred[512,1536]{0,1:T(8,128)(4,1)S(1)} fusion(s32[1536]{0:T(1024)S(1)} %iota_add_fusion, s32[512]{0:T(512)S(1)} %iota_add_fusion.1, s32[512]{0:T(512)S(1)} %compare_select_fusion.7, s32[1536]{0:T(1024)S(1)} %compare_select_fusion), kind=kLoop, calls=%fused_computation.14 | loop fusion | flops 4718592 | bytes 802816 | tf_op jit(solution)/shard_map/while/body/eval_jaxpr/and | solution.py:50
  13.3 6.3 %collective-permute-done = bf16[512,512]{0,1:T(8,128)(2,1)S(1)} collective-permute-done((bf16[512,512]{0,1:T(8,128)(2,1)S(1)}, bf16[512,512]{0,1:T(8,128)(2,1)S(1)}, u32[]{:S(2)}, u32[]{:S(2)}) %collective-permute-start) | collective-permute-done | bytes 524320 | tf_op jit(solution)/shard_map/ppermute | solution.py:18
  19.6 4.5 %collective-permute-done.1 = bf16[512,512]{0,1:T(8,128)(2,1)S(1)} collective-permute-done((bf16[512,512]{0,1:T(8,128)(2,1)S(1)}, bf16[512,512]{0,1:T(8,128)(2,1)S(1)}, u32[]{:S(2)}, u32[]{:S(2)}) %collective-permute-start.1) | collective-permute-done | bytes 524320 | tf_op jit(solution)/shard_map/ppermute | solution.py:18
  24.1 0.1 maximum_maximum_fusion
  24.2 0.1 fusion.19
  24.3 2.5 %fusion.4 = (f32[2,2,512]{2,1,0:T(2,128)S(1)}, f32[2,1536,512,2]{2,1,3,0:T(8,128)S(1)}) fusion(pred[512,1536]{0,1:T(8,128)(4,1)S(1)} %fusion.7, bf16[1536,2,128,1]{0,2,3,1:T(8,128)(2,1)S(1)} %bitcast.104, bf16[512,2,2,128]{0,3,2,1:T(8,128)(2,1)S(1)} %bitcast.106), kind=kOutput, calls=%fused_computation.9 | convolution fusion | flops 814741504 | bytes 14688256 | tf_op jit(solution)/shard_map/while/body/eval_jaxpr/iged,jgd->geij/dot_general | solution.py:43
  26.8 0.0 copy-start.1
  26.8 3.2 %select_reduce_fusion = f32[2,2,512]{2,1,0:T(2,128)S(1)} fusion(f32[2,1536,512,2]{2,1,3,0:T(8,128)S(1)} %get-tuple-element.66, f32[2,2,512]{2,1,0:T(2,128)S(1)} %get-tuple-element.65, pred[512,1536]{0,1:T(8,128)(4,1)S(1)} %fusion.7), kind=kLoop, calls=%fused_computation.8 | loop fusion | flops 15726592 | bytes 13385728 | tf_op jit(solution)/shard_map/while/body/eval_jaxpr/reduce_sum | solution.py:59
  30.0 1.3 %copy-done.1 = f32[2,1536,512,2]{2,1,3,0:T(8,128)} copy-done((f32[2,1536,512,2]{2,1,3,0:T(8,128)}, f32[2,1536,512,2]{2,1,3,0:T(8,128)S(1)}, u32[]{:S(2)}) %copy-start.1) | copy-done | bytes 12582936
  31.4 3.8 %multiply_reduce_fusion = (f32[512,2,2]{0,2,1:T(2,128)S(1)}, bf16[512,2,2,128]{0,3,2,1:T(8,128)(2,1)}) fusion(bf16[512,512]{0,1:T(8,128)(2,1)S(1)} %copy.54, bf16[1536,2,128,1]{0,2,3,1:T(8,128)(2,1)S(1)} %bitcast.112, f32[2,1536,512,2]{2,1,3,0:T(8,128)S(1)} %get-tuple-element.66, f32[2,2,512]{2,1,0:T(2,128)S(1)} %log_add_fusion, ...), kind=kOutput, calls=%fused_computation.26 | convolution fusion | flops 818935808 | bytes 15220736 | tf_op jit(solution)/shard_map/while/body/eval_jaxpr/geij,jgd->iged/dot_general | solution.py:63
  35.2 7.3 %fusion.1 = bf16[2,2,512,1536]{2,3,1,0:T(8,128)(2,1)S(1)} fusion(f32[2,1536,512,2]{2,1,3,0:T(8,128)} %copy-done.1, bf16[1536,2,128,1]{0,2,3,1:T(8,128)(2,1)S(1)} %bitcast.113, bf16[512,2,2,128]{0,3,2,1:T(8,128)(2,1)S(1)} %bitcast.114, f32[2,2,512]{2,1,0:T(2,128)S(1)} %bitcast.118, f32[2,2,512]{2,1,0:T(2,128)S(1)} %log_add_fusion, ...), kind=kOutput, calls=%fused_computation.3 | convolution fusion | flops 824180736 | bytes 20987904 | tf_op jit(solution)/shard_map/while/body/eval_jaxpr/iged,jgd->geij/dot_general | solution.py:67
  42.5 1.0 fusion.10
  43.5 0.0 copy-done
  43.5 0.2 constant_dynamic-update-slice_fusion.7
  43.6 1.9 %collective-permute-start.4 = (bf16[512,16]{0,1:T(8,128)(2,1)S(1)}, bf16[512,16]{0,1:T(8,128)(2,1)S(1)}, u32[]{:S(2)}, u32[]{:S(2)}) collective-permute-start(bf16[512,16]{0,1:T(8,128)(2,1)S(1)} %get-tuple-element.69), channel_id=1, source_target_pairs={{0,32},{32,64},{64,96},{96,128},{128,160},{160,192},{192,224},{224... | collective-permute-start | bytes 49160 | tf_op jit(solution)/shard_map/ppermute | solution.py:26
  45.6 3.3 %collective-permute-start.5 = (bf16[512,16]{0,1:T(8,128)(2,1)S(1)}, bf16[512,16]{0,1:T(8,128)(2,1)S(1)}, u32[]{:S(2)}, u32[]{:S(2)}) collective-permute-start(bf16[512,16]{0,1:T(8,128)(2,1)S(1)} %get-tuple-element.69), channel_id=1, source_target_pairs={{0,64},{32,96},{64,128},{96,160},{128,192},{160,224},{192,0},{224,... | collective-permute-start | bytes 49160 | tf_op jit(solution)/shard_map/ppermute | solution.py:26
  48.9 4.0 %collective-permute-start.6 = (bf16[512,16]{0,1:T(8,128)(2,1)S(1)}, bf16[512,16]{0,1:T(8,128)(2,1)S(1)}, u32[]{:S(2)}, u32[]{:S(2)}) collective-permute-start(bf16[512,16]{0,1:T(8,128)(2,1)S(1)} %get-tuple-element.69), channel_id=1, source_target_pairs={{0,96},{32,128},{64,160},{96,192},{128,224},{160,0},{192,32},{224,... | collective-permute-start | bytes 49160 | tf_op jit(solution)/shard_map/ppermute | solution.py:26
  52.9 0.5 collective-permute-start.7
  53.4 5.0 %collective-permute-start.8 = (bf16[512,16]{0,1:T(8,128)(2,1)S(1)}, bf16[512,16]{0,1:T(8,128)(2,1)S(1)}, u32[]{:S(2)}, u32[]{:S(2)}) collective-permute-start(bf16[512,16]{0,1:T(8,128)(2,1)S(1)} %get-tuple-element.69), channel_id=1, source_target_pairs={{0,160},{32,192},{64,224},{96,0},{128,32},{160,64},{192,96},{224,1... | collective-permute-start | bytes 49160 | tf_op jit(solution)/shard_map/ppermute | solution.py:26
  58.4 8.7 %convolution_bitcast_fusion = f32[1536,2,128]{0,2,1:T(8,128)} fusion(bf16[512,2,2,128]{0,3,2,1:T(8,128)(2,1)S(1)} %bitcast.115, f32[2,1536,512,2]{2,1,3,0:T(8,128)} %copy-done.1, f32[2,2,512]{2,1,0:T(2,128)S(1)} %log_add_fusion, pred[512,1536]{0,1:T(8,128)(4,1)S(1)} %fusion.7), kind=kOutput, calls=%fused_computation.15 | convolution fusion | flops 817889280 | bytes 15474688 | tf_op jit(solution)/shard_map/while/body/eval_jaxpr/geij,iged->jgd/dot_general | solution.py:74
  67.0 2.1 %fusion.9 = f32[1536,2,128]{0,2,1:T(8,128)S(1)} fusion(bf16[2,2,512,1536]{2,3,1,0:T(8,128)(2,1)S(1)} %fusion.1, bf16[512,2,2,128]{0,3,2,1:T(8,128)(2,1)S(1)} %bitcast.107), kind=kOutput, calls=%fused_computation.18 | convolution fusion | flops 805699584 | bytes 8388608 | tf_op jit(solution)/shard_map/while/body/eval_jaxpr/geij,iged->jgd/dot_general | solution.py:71
  69.2 0.0 copy-done.2
  69.2 0.0 slice-start
  69.2 0.1 slice.80
  69.3 1.0 copy.62
  70.3 0.1 slice.79
  70.3 1.0 copy.61
  71.3 1.3 %maximum_convert_fusion = bf16[1024,512]{1,0:T(8,128)(2,1)S(1)} fusion(bf16[1024,256]{1,0:T(8,128)(2,1)} %copy.62, bf16[1024,256]{1,0:T(8,128)(2,1)} %copy.61), kind=kLoop, calls=%fused_computation.19 | loop fusion | flops 2097152 | bytes 2097152 | tf_op jit(solution)/shard_map/convert.1
  72.6 1.0 fusion.20
  73.7 0.8 slice.78
  74.5 1.0 copy.66
  75.5 0.2 copy.64
  75.7 1.2 %copy.63 = f32[512,256]{1,0:T(8,128)S(1)} copy(f32[512,256]{0,1:T(8,128)} %bitcast.109) | data formatting | bytes 1048576 | tf_op jit(solution)/shard_map/reshape | solution.py:158
  77.0 2.0 %copy.65 = bf16[512,512]{1,0:T(8,128)(2,1)} copy(bf16[512,512]{0,1:T(8,128)(2,1)} %bitcast.116) | data formatting | bytes 1048576
  79.0 0.0 collective-permute-done.4
  79.0 2.7 %collective-permute-start.9 = (bf16[512,16]{0,1:T(8,128)(2,1)S(1)}, bf16[512,16]{0,1:T(8,128)(2,1)S(1)}, u32[]{:S(2)}, u32[]{:S(2)}) collective-permute-start(bf16[512,16]{0,1:T(8,128)(2,1)S(1)} %get-tuple-element.69), channel_id=1, source_target_pairs={{0,192},{32,224},{64,0},{96,32},{128,64},{160,96},{192,128},{224,1... | collective-permute-start | bytes 49160 | tf_op jit(solution)/shard_map/ppermute | solution.py:26
  81.7 0.0 collective-permute-done.5
  81.7 1.0 collective-permute-start.10
  82.7 0.0 collective-permute-done.6
  82.7 1.9 %collective-permute-start.2 = (bf16[512,512]{1,0:T(8,128)(2,1)}, bf16[512,512]{1,0:T(8,128)(2,1)S(1)}, u32[]{:S(2)}, u32[]{:S(2)}) collective-permute-start(bf16[512,512]{1,0:T(8,128)(2,1)} %get-tuple-element.61), channel_id=1, source_target_pairs={{1,0},{2,1},{3,2},{4,3},{5,4},{6,5},{7,6},{8,7},{9,8},{10,9},{11,1... | collective-permute-start | bytes 1572872 | tf_op jit(solution)/shard_map/ppermute | solution.py:18
  84.6 0.0 collective-permute-done.7
  84.6 2.7 %collective-permute-start.3 = (bf16[512,512]{1,0:T(8,128)(2,1)}, bf16[512,512]{1,0:T(8,128)(2,1)S(1)}, u32[]{:S(2)}, u32[]{:S(2)}) collective-permute-start(bf16[512,512]{1,0:T(8,128)(2,1)} %get-tuple-element.62), channel_id=1, source_target_pairs={{2,0},{3,1},{4,2},{5,3},{6,4},{7,5},{8,6},{9,7},{10,8},{11,9},{12,... | collective-permute-start | bytes 1572872 | tf_op jit(solution)/shard_map/ppermute | solution.py:18
  87.4 0.0 collective-permute-done.8
  87.4 0.0 collective-permute-done.9
  87.4 0.0 collective-permute-done.10
  87.5 0.6 gather_fusion
  88.0 0.1 broadcast_select_fusion
  88.1 0.6 fusion.13
  88.8 6.2 %collective-permute-done.2 = bf16[512,512]{1,0:T(8,128)(2,1)S(1)} collective-permute-done((bf16[512,512]{1,0:T(8,128)(2,1)}, bf16[512,512]{1,0:T(8,128)(2,1)S(1)}, u32[]{:S(2)}, u32[]{:S(2)}) %collective-permute-start.2) | collective-permute-done | bytes 524320 | tf_op jit(solution)/shard_map/ppermute | solution.py:18
  94.9 11.9 %collective-permute-done.3 = bf16[512,512]{1,0:T(8,128)(2,1)S(1)} collective-permute-done((bf16[512,512]{1,0:T(8,128)(2,1)}, bf16[512,512]{1,0:T(8,128)(2,1)S(1)}, u32[]{:S(2)}, u32[]{:S(2)}) %collective-permute-start.3) | collective-permute-done | bytes 524320 | tf_op jit(solution)/shard_map/ppermute | solution.py:18
  106.8 0.1 convert_add_fusion
  106.9 0.9 fusion.11
  (19 shorter events, 0.2 us)
Async XLA Ops:
  0.6 42.8 %copy-start = (bf16[16,512]{1,0:T(8,128)(2,1)S(1)}, bf16[16,512]{1,0:T(8,128)(2,1)}, u32[]{:S(2)}) copy-start(bf16[16,512]{1,0:T(8,128)(2,1)} %param.10) | copy-start | bytes 49156
  2.9 16.7 %collective-permute-start = (bf16[512,512]{0,1:T(8,128)(2,1)S(1)}, bf16[512,512]{0,1:T(8,128)(2,1)S(1)}, u32[]{:S(2)}, u32[]{:S(2)}) collective-permute-start(bf16[512,512]{0,1:T(8,128)(2,1)S(1)} %pad_maximum_fusion), channel_id=1, source_target_pairs={{0,2},{1,3},{2,4},{3,5},{4,6},{5,7},{6,8},{7,9},{8,10},{9,11},{10,... | collective-permute-start | bytes 1572872 | tf_op jit(solution)/shard_map/ppermute | solution.py:18
  6.3 17.8 %collective-permute-start.1 = (bf16[512,512]{0,1:T(8,128)(2,1)S(1)}, bf16[512,512]{0,1:T(8,128)(2,1)S(1)}, u32[]{:S(2)}, u32[]{:S(2)}) collective-permute-start(bf16[512,512]{0,1:T(8,128)(2,1)S(1)} %pad_maximum_fusion), channel_id=1, source_target_pairs={{0,1},{1,2},{2,3},{3,4},{4,5},{5,6},{6,7},{7,8},{8,9},{9,10},{10,1... | collective-permute-start | bytes 1572872 | tf_op jit(solution)/shard_map/ppermute | solution.py:18
  26.8 4.6 %copy-start.1 = (f32[2,1536,512,2]{2,1,3,0:T(8,128)}, f32[2,1536,512,2]{2,1,3,0:T(8,128)S(1)}, u32[]{:S(2)}) copy-start(f32[2,1536,512,2]{2,1,3,0:T(8,128)S(1)} %get-tuple-element.66) | copy-start | bytes 37748740
  43.6 35.4 %collective-permute-start.4 = (bf16[512,16]{0,1:T(8,128)(2,1)S(1)}, bf16[512,16]{0,1:T(8,128)(2,1)S(1)}, u32[]{:S(2)}, u32[]{:S(2)}) collective-permute-start(bf16[512,16]{0,1:T(8,128)(2,1)S(1)} %get-tuple-element.69), channel_id=1, source_target_pairs={{0,32},{32,64},{64,96},{96,128},{128,160},{160,192},{192,224},{224... | collective-permute-start | bytes 49160 | tf_op jit(solution)/shard_map/ppermute | solution.py:26
  45.6 36.1 %collective-permute-start.5 = (bf16[512,16]{0,1:T(8,128)(2,1)S(1)}, bf16[512,16]{0,1:T(8,128)(2,1)S(1)}, u32[]{:S(2)}, u32[]{:S(2)}) collective-permute-start(bf16[512,16]{0,1:T(8,128)(2,1)S(1)} %get-tuple-element.69), channel_id=1, source_target_pairs={{0,64},{32,96},{64,128},{96,160},{128,192},{160,224},{192,0},{224,... | collective-permute-start | bytes 49160 | tf_op jit(solution)/shard_map/ppermute | solution.py:26
  48.9 33.8 %collective-permute-start.6 = (bf16[512,16]{0,1:T(8,128)(2,1)S(1)}, bf16[512,16]{0,1:T(8,128)(2,1)S(1)}, u32[]{:S(2)}, u32[]{:S(2)}) collective-permute-start(bf16[512,16]{0,1:T(8,128)(2,1)S(1)} %get-tuple-element.69), channel_id=1, source_target_pairs={{0,96},{32,128},{64,160},{96,192},{128,224},{160,0},{192,32},{224,... | collective-permute-start | bytes 49160 | tf_op jit(solution)/shard_map/ppermute | solution.py:26
  52.9 31.7 %collective-permute-start.7 = (bf16[512,16]{0,1:T(8,128)(2,1)S(1)}, bf16[512,16]{0,1:T(8,128)(2,1)S(1)}, u32[]{:S(2)}, u32[]{:S(2)}) collective-permute-start(bf16[512,16]{0,1:T(8,128)(2,1)S(1)} %get-tuple-element.69), channel_id=1, source_target_pairs={{0,128},{32,160},{64,192},{96,224},{128,0},{160,32},{192,64},{224,... | collective-permute-start | bytes 49160 | tf_op jit(solution)/shard_map/ppermute | solution.py:26
  53.4 34.0 %collective-permute-start.8 = (bf16[512,16]{0,1:T(8,128)(2,1)S(1)}, bf16[512,16]{0,1:T(8,128)(2,1)S(1)}, u32[]{:S(2)}, u32[]{:S(2)}) collective-permute-start(bf16[512,16]{0,1:T(8,128)(2,1)S(1)} %get-tuple-element.69), channel_id=1, source_target_pairs={{0,160},{32,192},{64,224},{96,0},{128,32},{160,64},{192,96},{224,1... | collective-permute-start | bytes 49160 | tf_op jit(solution)/shard_map/ppermute | solution.py:26
  67.0 2.2 %copy-start.2 = (f32[1536,2,128]{0,2,1:T(8,128)S(1)}, f32[1536,2,128]{0,2,1:T(8,128)}, u32[]{:S(2)}) copy-start(f32[1536,2,128]{0,2,1:T(8,128)} %convolution_bitcast_fusion) | copy-start | bytes 4718596
  69.2 6.3 %slice-start = ((f32[1536,2,128]{0,2,1:T(8,128)}), f32[512,2,128]{0,2,1:T(8,128)S(1)}, s32[]{:S(2)}) async-start(f32[1536,2,128]{0,2,1:T(8,128)} %convolution_bitcast_fusion), calls=%async_computation | async-start | bytes 1048576 | tf_op jit(solution)/shard_map/slice | solution.py:159
  79.0 8.4 %collective-permute-start.9 = (bf16[512,16]{0,1:T(8,128)(2,1)S(1)}, bf16[512,16]{0,1:T(8,128)(2,1)S(1)}, u32[]{:S(2)}, u32[]{:S(2)}) collective-permute-start(bf16[512,16]{0,1:T(8,128)(2,1)S(1)} %get-tuple-element.69), channel_id=1, source_target_pairs={{0,192},{32,224},{64,0},{96,32},{128,64},{160,96},{192,128},{224,1... | collective-permute-start | bytes 49160 | tf_op jit(solution)/shard_map/ppermute | solution.py:26
  81.7 5.8 %collective-permute-start.10 = (bf16[512,16]{0,1:T(8,128)(2,1)S(1)}, bf16[512,16]{0,1:T(8,128)(2,1)S(1)}, u32[]{:S(2)}, u32[]{:S(2)}) collective-permute-start(bf16[512,16]{0,1:T(8,128)(2,1)S(1)} %get-tuple-element.69), channel_id=1, source_target_pairs={{0,224},{32,0},{64,32},{96,64},{128,96},{160,128},{192,160},{224,1... | collective-permute-start | bytes 49160 | tf_op jit(solution)/shard_map/ppermute | solution.py:26
  82.7 12.2 %collective-permute-start.2 = (bf16[512,512]{1,0:T(8,128)(2,1)}, bf16[512,512]{1,0:T(8,128)(2,1)S(1)}, u32[]{:S(2)}, u32[]{:S(2)}) collective-permute-start(bf16[512,512]{1,0:T(8,128)(2,1)} %get-tuple-element.61), channel_id=1, source_target_pairs={{1,0},{2,1},{3,2},{4,3},{5,4},{6,5},{7,6},{8,7},{9,8},{10,9},{11,1... | collective-permute-start | bytes 1572872 | tf_op jit(solution)/shard_map/ppermute | solution.py:18
  84.6 22.2 %collective-permute-start.3 = (bf16[512,512]{1,0:T(8,128)(2,1)}, bf16[512,512]{1,0:T(8,128)(2,1)S(1)}, u32[]{:S(2)}, u32[]{:S(2)}) collective-permute-start(bf16[512,512]{1,0:T(8,128)(2,1)} %get-tuple-element.62), channel_id=1, source_target_pairs={{2,0},{3,1},{4,2},{5,3},{6,4},{7,5},{8,6},{9,7},{10,8},{11,9},{12,... | collective-permute-start | bytes 1572872 | tf_op jit(solution)/shard_map/ppermute | solution.py:18

commit v2 on v1

v2 whole, which is shorter than its diff:
```python
import jax
import jax.numpy as jnp
from jax import lax
from jax.experimental import pallas as pl
from jax.experimental.pallas import tpu as pltpu
from jax.sharding import PartitionSpec as P

HEAD_SIZE = 128
WIN = 1024
BLK = 128


softmax_scale = 168.0 ** (-0.5)
masked_value = -1e30


def passed_along(block, axis, distance):
    devices = range(lax.axis_size(axis))
    route = [(i - distance, i) for i in devices if i - distance in devices]
    return lax.ppermute(block, axis, route)


def gathered_sum(part, axis):
    count = lax.axis_size(axis)
    received = [part]
    for shift in range(1, count):
        route = [(i, (i + shift) % count) for i in range(count)]
        received.append(lax.ppermute(part, axis, route))
    stacked = jnp.stack(received).astype(jnp.float32)
    order = (lax.axis_index(axis) - jnp.arange(count, dtype=jnp.int32)) % count
    in_order = jnp.take(stacked, order, axis=0)
    total = in_order[0]
    for j in range(1, count):
        total = total + in_order[j]
    return total


def doc_index(positions, doc_ends):
    counted = jnp.sum((positions[:, None] >= doc_ends[None, :]).astype(jnp.int32), axis=1)
    return jnp.where(positions < 0, -1, counted)


def attention_kernel(q_ref, k_ref, v_ref, do_ref, qdoc_ref, kdoc_ref,
                     o_ref, dq_ref, dk_ref, dv_ref):
    qb = pl.program_id(1)
    rows = q_ref.shape[0]
    span = rows + WIN
    key_first = pl.multiple_of(qb * rows, rows)

    @pl.when(qb == 0)
    def _():
        dk_ref[...] = jnp.zeros_like(dk_ref)
        dv_ref[...] = jnp.zeros_like(dv_ref)

    q = jnp.concatenate([q_ref[:, :HEAD_SIZE], q_ref[:, HEAD_SIZE:]], axis=0)
    do = jnp.concatenate([do_ref[:, :HEAD_SIZE], do_ref[:, HEAD_SIZE:]], axis=0)
    k = k_ref[pl.ds(key_first, span), :]
    v = v_ref[pl.ds(key_first, span), :]
    qdoc = qdoc_ref[...]
    qdoc = jnp.concatenate([qdoc, qdoc], axis=0)
    kdoc = kdoc_ref[:, pl.ds(key_first, span)]
    row = lax.broadcasted_iota(jnp.int32, (2 * rows, span), 0) % rows
    col = lax.broadcasted_iota(jnp.int32, (2 * rows, span), 1)
    offset = row + WIN - col
    live = (offset >= 0) & (offset < WIN) & (qdoc == kdoc)

    s = lax.dot_general(q, k, (((1,), (1,)), ((), ())),
                        preferred_element_type=jnp.float32) * softmax_scale
    masked = jnp.where(live, s, masked_value)
    row_max = jnp.max(masked, axis=1, keepdims=True)
    e = jnp.exp(masked - row_max)
    row_sum = jnp.sum(e, axis=1, keepdims=True)
    p = e * (1.0 / row_sum)
    p_low = p.astype(jnp.bfloat16)
    o = jnp.dot(p_low, v, preferred_element_type=jnp.float32)
    row_dot = jnp.sum(do.astype(jnp.float32) * o, axis=1, keepdims=True)
    dp = lax.dot_general(do, v, (((1,), (1,)), ((), ())),
                         preferred_element_type=jnp.float32)
    ds = (p * (dp - row_dot)).astype(jnp.bfloat16)
    dq = jnp.dot(ds, k, preferred_element_type=jnp.float32) * softmax_scale
    dk = lax.dot_general(ds, q, (((0,), (0,)), ((), ())),
                         preferred_element_type=jnp.float32) * softmax_scale
    dv = lax.dot_general(p_low, do, (((0,), (0,)), ((), ())),
                         preferred_element_type=jnp.float32)
    o_ref[:, :HEAD_SIZE] = o[:rows].astype(o_ref.dtype)
    o_ref[:, HEAD_SIZE:] = o[rows:].astype(o_ref.dtype)
    dq_ref[:, :HEAD_SIZE] = dq[:rows].astype(dq_ref.dtype)
    dq_ref[:, HEAD_SIZE:] = dq[rows:].astype(dq_ref.dtype)
    dk_ref[pl.ds(key_first, span), :] += dk
    dv_ref[pl.ds(key_first, span), :] += dv


def fused_attention(queries, extended, output_gradient, qdoc, kdoc, rows=BLK):
    tokens, query_cols = queries.shape
    ext_rows, joined_cols = extended.shape
    groups = joined_cols // (2 * HEAD_SIZE)
    blocks = tokens // rows
    span = rows + WIN
    pair = 2 * HEAD_SIZE
    flops = groups * blocks * 6 * 2 * (2 * rows) * span * HEAD_SIZE
    nbytes = 2 * (4 * tokens * query_cols + ext_rows * joined_cols) + 4 * ext_rows * joined_cols
    return pl.pallas_call(
        attention_kernel,
        grid=(groups, blocks),
        in_specs=[
            pl.BlockSpec((rows, pair), lambda g, b: (b, g)),
            pl.BlockSpec((ext_rows, HEAD_SIZE), lambda g, b: (0, g)),
            pl.BlockSpec((ext_rows, HEAD_SIZE), lambda g, b: (0, g + groups)),
            pl.BlockSpec((rows, pair), lambda g, b: (b, g)),
            pl.BlockSpec((rows, 1), lambda g, b: (b, 0)),
            pl.BlockSpec((1, ext_rows), lambda g, b: (0, 0)),
        ],
        out_specs=[
            pl.BlockSpec((rows, pair), lambda g, b: (b, g)),
            pl.BlockSpec((rows, pair), lambda g, b: (b, g)),
            pl.BlockSpec((ext_rows, HEAD_SIZE), lambda g, b: (0, g)),
            pl.BlockSpec((ext_rows, HEAD_SIZE), lambda g, b: (0, g)),
        ],
        out_shape=[
            jax.ShapeDtypeStruct((tokens, query_cols), jnp.bfloat16),
            jax.ShapeDtypeStruct((tokens, query_cols), jnp.bfloat16),
            jax.ShapeDtypeStruct((ext_rows, joined_cols // 2), jnp.float32),
            jax.ShapeDtypeStruct((ext_rows, joined_cols // 2), jnp.float32),
        ],
        compiler_params=pltpu.CompilerParams(
            dimension_semantics=("arbitrary", "arbitrary"),
            vmem_limit_bytes=48 * 1024 * 1024,
        ),
        cost_estimate=pl.CostEstimate(
            flops=flops, transcendentals=groups * blocks * 2 * rows * span,
            bytes_accessed=nbytes),
    )(queries, extended, extended, output_gradient, qdoc, kdoc)


def body(
    queries,
    key_head_tensor,
    value_head_tensor,
    output_gradient,
    adapter_up_matrix,
    document_block_counts,
):
    tokens_here = queries.shape[0]
    query_cols = queries.shape[1]
    key_cols = key_head_tensor.shape[1]
    edge_rows = min(WIN, tokens_here)
    hop_count = WIN // edge_rows
    first_pos = lax.axis_index("ctx") * tokens_here
    lowest = first_pos - WIN
    doc_ends = jnp.cumsum(document_block_counts) * BLK
    joined = jnp.concatenate([key_head_tensor, value_head_tensor], axis=1)
    arrived = []
    for hop_num in range(hop_count):
        arrived.append(passed_along(joined, "ctx", hop_num + 1))
    extended = jnp.concatenate(arrived[::-1] + [joined], axis=0)
    qdoc = doc_index(first_pos + jnp.arange(tokens_here, dtype=jnp.int32), doc_ends)
    kdoc = doc_index(lowest + jnp.arange(WIN + tokens_here, dtype=jnp.int32), doc_ends)
    attended, flattened_query, key_grads, value_grads = fused_attention(
        queries, extended, output_gradient, qdoc[:, None], kdoc[None, :]
    )
    halo_grads = jnp.concatenate([key_grads[:WIN], value_grads[:WIN]], axis=1)
    returned = jnp.zeros((edge_rows, 2 * key_cols), jnp.float32)
    for hop_num in range(hop_count):
        segment = halo_grads[
            (hop_count - 1 - hop_num) * edge_rows : (hop_count - hop_num) * edge_rows
        ]
        returned = returned + passed_along(
            segment.astype(jnp.bfloat16), "ctx", -(hop_num + 1)
        ).astype(segment.dtype)
    cut_row = tokens_here - edge_rows
    own = jnp.concatenate([key_grads[WIN:], value_grads[WIN:]], axis=1)
    total = jnp.concatenate([own[:cut_row], own[cut_row:] + returned], axis=0)
    key_total = total[:, :key_cols]
    value_total = total[:, key_cols:]
    adapter_portion = lax.dot_general(
        flattened_query,
        adapter_up_matrix,
        (((1,), (1,)), ((), ())),
        preferred_element_type=jnp.float32,
    )
    adapter_gradient = gathered_sum(adapter_portion.astype(jnp.bfloat16), "head")
    return (
        attended,
        flattened_query,
        key_total.astype(jnp.bfloat16),
        value_total.astype(jnp.bfloat16),
        adapter_gradient,
    )


def solution(mesh):
    in_specs = (
        P("ctx", "head"),
        P("ctx", "head"),
        P("ctx", "head"),
        P("ctx", "head"),
        P(None, "head"),
        P(),
    )
    out_specs = (
        P("ctx", "head"),
        P("ctx", "head"),
        P("ctx", "head"),
        P("ctx", "head"),
        P("ctx", None),
    )
    return jax.shard_map(body, mesh=mesh, in_specs=in_specs, out_specs=out_specs, check_vma=False)
```

time: 108 us -> 83.7 us (0.78)
  the two profiles are of different devices: /device:TPU:14 before, /device:TPU:23 now
where the time goes in v2:
time: 83.7 us; the launch traced here: 83.4 us
  waiting for transfers between devices  31.4 us (38%)
  starting transfers between devices  27.4 us (33%)
  Pallas kernels  15.7 us (19%)
  local copies, waits for them, and re-layouts  6.22 us (7%)
  other arithmetic  1.56 us (2%)
  between operations  0.93 us (1%)
    ppermute x4, waiting for transfers between devices, passed_along(): return lax.ppermute(block, axis, route)  31.4 us
    ppermute x7, starting transfers between devices, gathered_sum(): received.append(lax.ppermute(part, axis, route))  16.5 us
    pallas_call x1, Pallas kernels, fused_attention(): pl.pallas_call(attention_kernel, grid=(groups, blocks), in_specs=[pl.Bloc...  15.7 us
    ppermute x4, starting transfers between devices, passed_along(): return lax.ppermute(block, axis, route)  10.8 us
    unnamed x15, local copies, waits for them, and re-layouts  1.93 us
  transfers between devices with their start and end apart: 11, of which 4 were waited for; matrix products, arithmetic and copies ran while one was open for 4% of the time, Pallas kernels for 0%

profile of v2, /device:TPU:23, one launch (start us, length us, event | category | flops | bytes accessed | tf_op | source)
XLA Modules:
  0.0 83.4 jit_solution(8550055342513310487)
XLA Ops:
  0.6 0.0 copy-start
  0.6 1.0 %constant_dynamic-update-slice_fusion.1 = bf16[512,512]{1,0:T(8,128)(2,1)S(1)} fusion(bf16[512,256]{1,0:T(8,128)(2,1)} %param.7), kind=kLoop, calls=%fused_computation.21 | loop fusion | bytes 524288
  1.6 1.0 %constant_dynamic-update-slice_fusion = bf16[512,512]{1,0:T(8,128)(2,1)S(1)} fusion(bf16[512,512]{1,0:T(8,128)(2,1)S(1)} %constant_dynamic-update-slice_fusion.1, bf16[512,256]{1,0:T(8,128)(2,1)} %param.8), kind=kLoop, calls=%fused_computation.20 | loop fusion | bytes 524288 | tf_op jit(solution)/shard_map/concatenate | solution.py:151
  2.6 3.4 %collective-permute-start.1 = (bf16[512,512]{1,0:T(8,128)(2,1)S(1)}, bf16[512,512]{1,0:T(8,128)(2,1)S(1)}, u32[]{:S(2)}, u32[]{:S(2)}) collective-permute-start(bf16[512,512]{1,0:T(8,128)(2,1)S(1)} %constant_dynamic-update-slice_fusion), channel_id=1, source_target_pairs={{0,1},{1,2},{2,3},{3,4},{4,5},{5,6},{6,7},{7,8},{8,9},{9,10},{10,1... | collective-permute-start | bytes 1572872 | tf_op jit(solution)/shard_map/ppermute | solution.py:20
  6.0 3.1 %collective-permute-start = (bf16[512,512]{1,0:T(8,128)(2,1)S(1)}, bf16[512,512]{1,0:T(8,128)(2,1)S(1)}, u32[]{:S(2)}, u32[]{:S(2)}) collective-permute-start(bf16[512,512]{1,0:T(8,128)(2,1)S(1)} %constant_dynamic-update-slice_fusion), channel_id=1, source_target_pairs={{0,2},{1,3},{2,4},{3,5},{4,6},{5,7},{6,8},{7,9},{8,10},{9,11},{10,... | collective-permute-start | bytes 1572872 | tf_op jit(solution)/shard_map/ppermute | solution.py:20
  9.1 0.7 copy.14
  9.9 0.1 reduce-window.8
  9.9 0.1 multiply_reduce_fusion
  10.0 0.1 convert_reduce_fusion.1
  10.1 0.2 copy.15
  10.3 0.1 convert_reduce_fusion
  10.5 0.0 copy-start.1
  10.6 0.0 copy-start.2
  10.6 4.6 %collective-permute-done.1 = bf16[512,512]{1,0:T(8,128)(2,1)S(1)} collective-permute-done((bf16[512,512]{1,0:T(8,128)(2,1)S(1)}, bf16[512,512]{1,0:T(8,128)(2,1)S(1)}, u32[]{:S(2)}, u32[]{:S(2)}) %collective-permute-start.1) | collective-permute-done | bytes 524320 | tf_op jit(solution)/shard_map/ppermute | solution.py:20
  15.2 9.1 %collective-permute-done = bf16[512,512]{1,0:T(8,128)(2,1)S(1)} collective-permute-done((bf16[512,512]{1,0:T(8,128)(2,1)S(1)}, bf16[512,512]{1,0:T(8,128)(2,1)S(1)}, u32[]{:S(2)}, u32[]{:S(2)}) %collective-permute-start) | collective-permute-done | bytes 524320 | tf_op jit(solution)/shard_map/ppermute | solution.py:20
  24.3 0.1 pad_maximum_fusion.k_ref.v_ref
  24.4 0.0 copy-done.1
  24.4 0.0 copy-done.2
  24.4 15.7 %shard_map.101 = (bf16[512,512]{1,0:T(8,128)(2,1)}, bf16[512,512]{1,0:T(8,128)(2,1)}, f32[1536,256]{1,0:T(8,128)S(1)}, f32[1536,256]{1,0:T(8,128)S(1)}) custom-call(bf16[512,512]{1,0:T(8,128)(2,1)S(1)} %copy-done.1, bf16[1536,512]{1,0:T(8,128)(2,1)S(1)} %pad_maximum_fusion.k_ref.v_ref, bf16[1536,512]{1,0:T(8,128)(2,1)S(1)} %pad_maximum_fusion.k_ref.v_ref, ...), custom_call_target="tpu_custom_call" | custom-call | flops 3623878656 | bytes 6815744 | tf_op jit(solution)/shard_map/pallas_call | solution.py:102
  40.1 0.0 copy-start.3
  40.1 0.1 slice.55
  40.2 0.1 slice.54
  40.2 0.0 copy-done
  40.2 0.9 %copy-done.3 = bf16[512,512]{1,0:T(8,128)(2,1)S(1)} copy-done((bf16[512,512]{1,0:T(8,128)(2,1)S(1)}, bf16[512,512]{1,0:T(8,128)(2,1)}, u32[]{:S(2)}) %copy-start.3) | copy-done | bytes 524312
  41.1 0.2 constant_dynamic-update-slice_fusion.9
  41.4 1.7 %collective-permute-start.4 = (bf16[512,16]{0,1:T(8,128)(2,1)S(1)}, bf16[512,16]{0,1:T(8,128)(2,1)S(1)}, u32[]{:S(2)}, u32[]{:S(2)}) collective-permute-start(bf16[512,16]{0,1:T(8,128)(2,1)S(1)} %get-tuple-element.18), channel_id=1, source_target_pairs={{0,32},{32,64},{64,96},{96,128},{128,160},{160,192},{192,224},{224... | collective-permute-start | bytes 49160 | tf_op jit(solution)/shard_map/ppermute | solution.py:28
  43.1 0.1 maximum_convert_fusion
  43.1 0.9 %fusion.6 = (bf16[512,512]{1,0:T(8,128)(2,1)S(1)}, bf16[512,512]{1,0:T(8,128)(2,1)}) fusion(bf16[1024,512]{1,0:T(8,128)(2,1)S(1)} %maximum_convert_fusion), kind=kLoop, calls=%fused_computation.46 | loop fusion | bytes 2097152 | tf_op jit(solution)/shard_map/slice | solution.py:164
  44.1 3.1 %collective-permute-start.5 = (bf16[512,16]{0,1:T(8,128)(2,1)S(1)}, bf16[512,16]{0,1:T(8,128)(2,1)S(1)}, u32[]{:S(2)}, u32[]{:S(2)}) collective-permute-start(bf16[512,16]{0,1:T(8,128)(2,1)S(1)} %get-tuple-element.18), channel_id=1, source_target_pairs={{0,64},{32,96},{64,128},{96,160},{128,192},{160,224},{192,0},{224,... | collective-permute-start | bytes 49160 | tf_op jit(solution)/shard_map/ppermute | solution.py:28
  47.2 3.7 %collective-permute-start.6 = (bf16[512,16]{0,1:T(8,128)(2,1)S(1)}, bf16[512,16]{0,1:T(8,128)(2,1)S(1)}, u32[]{:S(2)}, u32[]{:S(2)}) collective-permute-start(bf16[512,16]{0,1:T(8,128)(2,1)S(1)} %get-tuple-element.18), channel_id=1, source_target_pairs={{0,96},{32,128},{64,160},{96,192},{128,224},{160,0},{192,32},{224,... | collective-permute-start | bytes 49160 | tf_op jit(solution)/shard_map/ppermute | solution.py:28
  50.9 0.5 collective-permute-start.7
  51.4 4.5 %collective-permute-start.8 = (bf16[512,16]{0,1:T(8,128)(2,1)S(1)}, bf16[512,16]{0,1:T(8,128)(2,1)S(1)}, u32[]{:S(2)}, u32[]{:S(2)}) collective-permute-start(bf16[512,16]{0,1:T(8,128)(2,1)S(1)} %get-tuple-element.18), channel_id=1, source_target_pairs={{0,160},{32,192},{64,224},{96,0},{128,32},{160,64},{192,96},{224,1... | collective-permute-start | bytes 49160 | tf_op jit(solution)/shard_map/ppermute | solution.py:28
  55.8 0.0 collective-permute-done.4
  55.8 2.4 %collective-permute-start.9 = (bf16[512,16]{0,1:T(8,128)(2,1)S(1)}, bf16[512,16]{0,1:T(8,128)(2,1)S(1)}, u32[]{:S(2)}, u32[]{:S(2)}) collective-permute-start(bf16[512,16]{0,1:T(8,128)(2,1)S(1)} %get-tuple-element.18), channel_id=1, source_target_pairs={{0,192},{32,224},{64,0},{96,32},{128,64},{160,96},{192,128},{224,1... | collective-permute-start | bytes 49160 | tf_op jit(solution)/shard_map/ppermute | solution.py:28
  58.2 0.0 collective-permute-done.5
  58.2 0.7 collective-permute-start.10
  59.0 0.0 collective-permute-done.6
  59.0 2.4 %collective-permute-start.3 = (bf16[512,512]{1,0:T(8,128)(2,1)}, bf16[512,512]{1,0:T(8,128)(2,1)S(1)}, u32[]{:S(2)}, u32[]{:S(2)}) collective-permute-start(bf16[512,512]{1,0:T(8,128)(2,1)} %get-tuple-element.14), channel_id=1, source_target_pairs={{2,0},{3,1},{4,2},{5,3},{6,4},{7,5},{8,6},{9,7},{10,8},{11,9},{12,... | collective-permute-start | bytes 1572872 | tf_op jit(solution)/shard_map/ppermute | solution.py:20
  61.4 0.0 collective-permute-done.7
  61.4 1.9 %collective-permute-start.2 = (bf16[512,512]{1,0:T(8,128)(2,1)S(1)}, bf16[512,512]{1,0:T(8,128)(2,1)S(1)}, u32[]{:S(2)}, u32[]{:S(2)}) collective-permute-start(bf16[512,512]{1,0:T(8,128)(2,1)S(1)} %get-tuple-element.13), channel_id=1, source_target_pairs={{1,0},{2,1},{3,2},{4,3},{5,4},{6,5},{7,6},{8,7},{9,8},{10,9},{11,1... | collective-permute-start | bytes 1572872 | tf_op jit(solution)/shard_map/ppermute | solution.py:20
  63.4 0.0 collective-permute-done.8
  63.4 0.0 collective-permute-done.9
  63.4 0.0 collective-permute-done.10
  63.5 0.6 gather_fusion
  64.0 0.1 broadcast_select_fusion
  64.1 0.6 fusion.2
  64.8 12.3 %collective-permute-done.3 = bf16[512,512]{1,0:T(8,128)(2,1)S(1)} collective-permute-done((bf16[512,512]{1,0:T(8,128)(2,1)}, bf16[512,512]{1,0:T(8,128)(2,1)S(1)}, u32[]{:S(2)}, u32[]{:S(2)}) %collective-permute-start.3) | collective-permute-done | bytes 524320 | tf_op jit(solution)/shard_map/ppermute | solution.py:20
  77.1 5.3 %collective-permute-done.2 = bf16[512,512]{1,0:T(8,128)(2,1)S(1)} collective-permute-done((bf16[512,512]{1,0:T(8,128)(2,1)S(1)}, bf16[512,512]{1,0:T(8,128)(2,1)S(1)}, u32[]{:S(2)}, u32[]{:S(2)}) %collective-permute-start.2) | collective-permute-done | bytes 524320 | tf_op jit(solution)/shard_map/ppermute | solution.py:20
  82.4 0.2 fusion
  82.6 0.8 fusion.7
  (17 shorter events, 0.2 us)
Async XLA Ops:
  0.6 39.6 %copy-start = (bf16[16,512]{1,0:T(8,128)(2,1)S(1)}, bf16[16,512]{1,0:T(8,128)(2,1)}, u32[]{:S(2)}) copy-start(bf16[16,512]{1,0:T(8,128)(2,1)} %param.10) | copy-start | bytes 49156
  2.6 12.6 %collective-permute-start.1 = (bf16[512,512]{1,0:T(8,128)(2,1)S(1)}, bf16[512,512]{1,0:T(8,128)(2,1)S(1)}, u32[]{:S(2)}, u32[]{:S(2)}) collective-permute-start(bf16[512,512]{1,0:T(8,128)(2,1)S(1)} %constant_dynamic-update-slice_fusion), channel_id=1, source_target_pairs={{0,1},{1,2},{2,3},{3,4},{4,5},{5,6},{6,7},{7,8},{8,9},{9,10},{10,1... | collective-permute-start | bytes 1572872 | tf_op jit(solution)/shard_map/ppermute | solution.py:20
  6.0 18.3 %collective-permute-start = (bf16[512,512]{1,0:T(8,128)(2,1)S(1)}, bf16[512,512]{1,0:T(8,128)(2,1)S(1)}, u32[]{:S(2)}, u32[]{:S(2)}) collective-permute-start(bf16[512,512]{1,0:T(8,128)(2,1)S(1)} %constant_dynamic-update-slice_fusion), channel_id=1, source_target_pairs={{0,2},{1,3},{2,4},{3,5},{4,6},{5,7},{6,8},{7,9},{8,10},{9,11},{10,... | collective-permute-start | bytes 1572872 | tf_op jit(solution)/shard_map/ppermute | solution.py:20
  10.5 13.9 %copy-start.1 = (bf16[512,512]{1,0:T(8,128)(2,1)S(1)}, bf16[512,512]{1,0:T(8,128)(2,1)}, u32[]{:S(2)}) copy-start(bf16[512,512]{1,0:T(8,128)(2,1)} %q_ref.1) | copy-start | bytes 1572868
  10.6 13.9 %copy-start.2 = (bf16[512,512]{1,0:T(8,128)(2,1)S(1)}, bf16[512,512]{1,0:T(8,128)(2,1)}, u32[]{:S(2)}) copy-start(bf16[512,512]{1,0:T(8,128)(2,1)} %do_ref.1) | copy-start | bytes 1572868
  40.1 1.0 %copy-start.3 = (bf16[512,512]{1,0:T(8,128)(2,1)S(1)}, bf16[512,512]{1,0:T(8,128)(2,1)}, u32[]{:S(2)}) copy-start(bf16[512,512]{1,0:T(8,128)(2,1)} %get-tuple-element.5) | copy-start | bytes 1572868
  41.4 14.5 %collective-permute-start.4 = (bf16[512,16]{0,1:T(8,128)(2,1)S(1)}, bf16[512,16]{0,1:T(8,128)(2,1)S(1)}, u32[]{:S(2)}, u32[]{:S(2)}) collective-permute-start(bf16[512,16]{0,1:T(8,128)(2,1)S(1)} %get-tuple-element.18), channel_id=1, source_target_pairs={{0,32},{32,64},{64,96},{96,128},{128,160},{160,192},{192,224},{224... | collective-permute-start | bytes 49160 | tf_op jit(solution)/shard_map/ppermute | solution.py:28
  44.1 14.1 %collective-permute-start.5 = (bf16[512,16]{0,1:T(8,128)(2,1)S(1)}, bf16[512,16]{0,1:T(8,128)(2,1)S(1)}, u32[]{:S(2)}, u32[]{:S(2)}) collective-permute-start(bf16[512,16]{0,1:T(8,128)(2,1)S(1)} %get-tuple-element.18), channel_id=1, source_target_pairs={{0,64},{32,96},{64,128},{96,160},{128,192},{160,224},{192,0},{224,... | collective-permute-start | bytes 49160 | tf_op jit(solution)/shard_map/ppermute | solution.py:28
  47.2 11.8 %collective-permute-start.6 = (bf16[512,16]{0,1:T(8,128)(2,1)S(1)}, bf16[512,16]{0,1:T(8,128)(2,1)S(1)}, u32[]{:S(2)}, u32[]{:S(2)}) collective-permute-start(bf16[512,16]{0,1:T(8,128)(2,1)S(1)} %get-tuple-element.18), channel_id=1, source_target_pairs={{0,96},{32,128},{64,160},{96,192},{128,224},{160,0},{192,32},{224,... | collective-permute-start | bytes 49160 | tf_op jit(solution)/shard_map/ppermute | solution.py:28
  50.9 10.5 %collective-permute-start.7 = (bf16[512,16]{0,1:T(8,128)(2,1)S(1)}, bf16[512,16]{0,1:T(8,128)(2,1)S(1)}, u32[]{:S(2)}, u32[]{:S(2)}) collective-permute-start(bf16[512,16]{0,1:T(8,128)(2,1)S(1)} %get-tuple-element.18), channel_id=1, source_target_pairs={{0,128},{32,160},{64,192},{96,224},{128,0},{160,32},{192,64},{224,... | collective-permute-start | bytes 49160 | tf_op jit(solution)/shard_map/ppermute | solution.py:28
  51.4 12.0 %collective-permute-start.8 = (bf16[512,16]{0,1:T(8,128)(2,1)S(1)}, bf16[512,16]{0,1:T(8,128)(2,1)S(1)}, u32[]{:S(2)}, u32[]{:S(2)}) collective-permute-start(bf16[512,16]{0,1:T(8,128)(2,1)S(1)} %get-tuple-element.18), channel_id=1, source_target_pairs={{0,160},{32,192},{64,224},{96,0},{128,32},{160,64},{192,96},{224,1... | collective-permute-start | bytes 49160 | tf_op jit(solution)/shard_map/ppermute | solution.py:28
  55.8 7.5 %collective-permute-start.9 = (bf16[512,16]{0,1:T(8,128)(2,1)S(1)}, bf16[512,16]{0,1:T(8,128)(2,1)S(1)}, u32[]{:S(2)}, u32[]{:S(2)}) collective-permute-start(bf16[512,16]{0,1:T(8,128)(2,1)S(1)} %get-tuple-element.18), channel_id=1, source_target_pairs={{0,192},{32,224},{64,0},{96,32},{128,64},{160,96},{192,128},{224,1... | collective-permute-start | bytes 49160 | tf_op jit(solution)/shard_map/ppermute | solution.py:28
  58.2 5.2 %collective-permute-start.10 = (bf16[512,16]{0,1:T(8,128)(2,1)S(1)}, bf16[512,16]{0,1:T(8,128)(2,1)S(1)}, u32[]{:S(2)}, u32[]{:S(2)}) collective-permute-start(bf16[512,16]{0,1:T(8,128)(2,1)S(1)} %get-tuple-element.18), channel_id=1, source_target_pairs={{0,224},{32,0},{64,32},{96,64},{128,96},{160,128},{192,160},{224,1... | collective-permute-start | bytes 49160 | tf_op jit(solution)/shard_map/ppermute | solution.py:28
  59.0 18.1 %collective-permute-start.3 = (bf16[512,512]{1,0:T(8,128)(2,1)}, bf16[512,512]{1,0:T(8,128)(2,1)S(1)}, u32[]{:S(2)}, u32[]{:S(2)}) collective-permute-start(bf16[512,512]{1,0:T(8,128)(2,1)} %get-tuple-element.14), channel_id=1, source_target_pairs={{2,0},{3,1},{4,2},{5,3},{6,4},{7,5},{8,6},{9,7},{10,8},{11,9},{12,... | collective-permute-start | bytes 1572872 | tf_op jit(solution)/shard_map/ppermute | solution.py:20
  61.4 21.0 %collective-permute-start.2 = (bf16[512,512]{1,0:T(8,128)(2,1)S(1)}, bf16[512,512]{1,0:T(8,128)(2,1)S(1)}, u32[]{:S(2)}, u32[]{:S(2)}) collective-permute-start(bf16[512,512]{1,0:T(8,128)(2,1)S(1)} %get-tuple-element.13), channel_id=1, source_target_pairs={{1,0},{2,1},{3,2},{4,3},{5,4},{6,5},{7,6},{8,7},{9,8},{10,9},{11,1... | collective-permute-start | bytes 1572872 | tf_op jit(solution)/shard_map/ppermute | solution.py:20

commit v3 on v2

--- a/solution.py
+++ b/solution.py
@@ -22,16 +22,12 @@
 
 def gathered_sum(part, axis):
     count = lax.axis_size(axis)
-    received = [part]
-    for shift in range(1, count):
-        route = [(i, (i + shift) % count) for i in range(count)]
-        received.append(lax.ppermute(part, axis, route))
-    stacked = jnp.stack(received).astype(jnp.float32)
-    order = (lax.axis_index(axis) - jnp.arange(count, dtype=jnp.int32)) % count
-    in_order = jnp.take(stacked, order, axis=0)
-    total = in_order[0]
-    for j in range(1, count):
-        total = total + in_order[j]
+    total = part.astype(jnp.float32)
+    stride = 1
+    while stride < count:
+        route = [(i, i ^ stride) for i in range(count)]
+        total = total + lax.ppermute(total, axis, route)
+        stride *= 2
     return total
 
 
@@ -178,7 +174,7 @@
         (((1,), (1,)), ((), ())),
         preferred_element_type=jnp.float32,
     )
-    adapter_gradient = gathered_sum(adapter_portion.astype(jnp.bfloat16), "head")
+    adapter_gradient = gathered_sum(adapter_portion, "head")
     return (
         attended,
         flattened_query,

time: 83.7 us -> 67.7 us (0.81)
  the two profiles are of different devices: /device:TPU:23 before, /device:TPU:24 now
where the time goes in v3:
time: 67.7 us; the launch traced here: 67.3 us
  starting transfers between devices  25.5 us (38%)
  waiting for transfers between devices  19.7 us (29%)
  Pallas kernels  15.7 us (23%)
  local copies, waits for them, and re-layouts  3.94 us (6%)
  other arithmetic  1.42 us (2%)
  between operations  0.84 us (1%)
    pallas_call x1, Pallas kernels, fused_attention(): pl.pallas_call(attention_kernel, grid=(groups, blocks), in_specs=[pl.Bloc...  15.7 us
    ppermute x4, waiting for transfers between devices, passed_along(): return lax.ppermute(block, axis, route)  14 us
    ppermute x4, starting transfers between devices, passed_along(): return lax.ppermute(block, axis, route)  13.5 us
    ppermute x3, starting transfers between devices, gathered_sum(): total = total + lax.ppermute(total, axis, route)  12 us
    ppermute x3, waiting for transfers between devices, gathered_sum(): total = total + lax.ppermute(total, axis, route)  5.73 us
  transfers between devices with their start and end apart: 7, of which 5 were waited for; matrix products, arithmetic and copies ran while one was open for 3% of the time, Pallas kernels for 0%

profile of v3, /device:TPU:24, one launch (start us, length us, event | category | flops | bytes accessed | tf_op | source)
XLA Modules:
  0.0 67.3 jit_solution(4892647506241942525)
XLA Ops:
  0.6 0.0 copy-start
  0.6 1.0 %constant_dynamic-update-slice_fusion.1 = bf16[512,512]{1,0:T(8,128)(2,1)S(1)} fusion(bf16[512,256]{1,0:T(8,128)(2,1)} %param.7), kind=kLoop, calls=%fused_computation.12 | loop fusion | bytes 524288
  1.6 1.0 %constant_dynamic-update-slice_fusion = bf16[512,512]{1,0:T(8,128)(2,1)S(1)} fusion(bf16[512,512]{1,0:T(8,128)(2,1)S(1)} %constant_dynamic-update-slice_fusion.1, bf16[512,256]{1,0:T(8,128)(2,1)} %param.8), kind=kLoop, calls=%fused_computation.11 | loop fusion | bytes 524288 | tf_op jit(solution)/shard_map/concatenate | solution.py:147
  2.6 1.9 %collective-permute-start.1 = (bf16[512,512]{1,0:T(8,128)(2,1)S(1)}, bf16[512,512]{1,0:T(8,128)(2,1)S(1)}, u32[]{:S(2)}, u32[]{:S(2)}) collective-permute-start(bf16[512,512]{1,0:T(8,128)(2,1)S(1)} %constant_dynamic-update-slice_fusion), channel_id=1, source_target_pairs={{0,1},{1,2},{2,3},{3,4},{4,5},{5,6},{6,7},{7,8},{8,9},{9,10},{10,1... | collective-permute-start | bytes 1572872 | tf_op jit(solution)/shard_map/ppermute | solution.py:20
  4.5 3.4 %collective-permute-start = (bf16[512,512]{1,0:T(8,128)(2,1)S(1)}, bf16[512,512]{1,0:T(8,128)(2,1)S(1)}, u32[]{:S(2)}, u32[]{:S(2)}) collective-permute-start(bf16[512,512]{1,0:T(8,128)(2,1)S(1)} %constant_dynamic-update-slice_fusion), channel_id=1, source_target_pairs={{0,2},{1,3},{2,4},{3,5},{4,6},{5,7},{6,8},{7,9},{8,10},{9,11},{10,... | collective-permute-start | bytes 1572872 | tf_op jit(solution)/shard_map/ppermute | solution.py:20
  8.0 0.7 %copy.14 = s32[32,1]{1,0:T(8,128)S(1)} copy(s32[32,1]{0,1:T(1,128)} %bitcast.5) | data formatting | bytes 256 | tf_op jit(solution)/shard_map/reshape.64
  8.7 0.1 reduce-window.8
  8.8 0.1 multiply_reduce_fusion
  8.9 0.1 convert_reduce_fusion.1
  9.0 0.2 copy.15
  9.1 0.1 convert_reduce_fusion
  9.3 0.0 copy-start.1
  9.3 0.0 copy-start.2
  9.3 9.0 %collective-permute-done.1 = bf16[512,512]{1,0:T(8,128)(2,1)S(1)} collective-permute-done((bf16[512,512]{1,0:T(8,128)(2,1)S(1)}, bf16[512,512]{1,0:T(8,128)(2,1)S(1)}, u32[]{:S(2)}, u32[]{:S(2)}) %collective-permute-start.1) | collective-permute-done | bytes 524320 | tf_op jit(solution)/shard_map/ppermute | solution.py:20
  18.3 5.0 %collective-permute-done = bf16[512,512]{1,0:T(8,128)(2,1)S(1)} collective-permute-done((bf16[512,512]{1,0:T(8,128)(2,1)S(1)}, bf16[512,512]{1,0:T(8,128)(2,1)S(1)}, u32[]{:S(2)}, u32[]{:S(2)}) %collective-permute-start) | collective-permute-done | bytes 524320 | tf_op jit(solution)/shard_map/ppermute | solution.py:20
  23.3 0.1 pad_maximum_fusion.k_ref.v_ref
  23.4 0.0 copy-done.1
  23.4 0.0 copy-done.2
  23.5 15.7 %shard_map.101 = (bf16[512,512]{1,0:T(8,128)(2,1)}, bf16[512,512]{1,0:T(8,128)(2,1)}, f32[1536,256]{1,0:T(8,128)S(1)}, f32[1536,256]{1,0:T(8,128)S(1)}) custom-call(bf16[512,512]{1,0:T(8,128)(2,1)S(1)} %copy-done.1, bf16[1536,512]{1,0:T(8,128)(2,1)S(1)} %pad_maximum_fusion.k_ref.v_ref, bf16[1536,512]{1,0:T(8,128)(2,1)S(1)} %pad_maximum_fusion.k_ref.v_ref, ...), custom_call_target="tpu_custom_call" | custom-call | flops 3623878656 | bytes 6815744 | tf_op jit(solution)/shard_map/pallas_call | solution.py:98
  39.1 0.1 slice.30
  39.2 0.1 slice.31
  39.2 0.1 maximum_convert_fusion
  39.3 0.0 copy-start.3
  39.3 0.1 fusion.2
  39.4 5.4 %collective-permute-start.2 = (bf16[512,512]{1,0:T(8,128)(2,1)S(1)}, bf16[512,512]{1,0:T(8,128)(2,1)S(1)}, u32[]{:S(2)}, u32[]{:S(2)}) collective-permute-start(bf16[512,512]{1,0:T(8,128)(2,1)S(1)} %get-tuple-element.13), channel_id=1, source_target_pairs={{1,0},{2,1},{3,2},{4,3},{5,4},{6,5},{7,6},{8,7},{9,8},{10,9},{11,1... | collective-permute-start | bytes 1572872 | tf_op jit(solution)/shard_map/ppermute | solution.py:20
  44.8 2.7 %collective-permute-start.3 = (bf16[512,512]{1,0:T(8,128)(2,1)S(1)}, bf16[512,512]{1,0:T(8,128)(2,1)S(1)}, u32[]{:S(2)}, u32[]{:S(2)}) collective-permute-start(bf16[512,512]{1,0:T(8,128)(2,1)S(1)} %get-tuple-element.14), channel_id=1, source_target_pairs={{2,0},{3,1},{4,2},{5,3},{6,4},{7,5},{8,6},{9,7},{10,8},{11,9},{12,... | collective-permute-start | bytes 1572872 | tf_op jit(solution)/shard_map/ppermute | solution.py:20
  47.6 0.0 copy-done
  47.6 0.0 copy-done.3
  47.6 0.2 fusion.4
  47.8 1.9 %collective-permute-start.4 = (f32[512,16]{0,1:T(8,128)S(1)}, f32[512,16]{0,1:T(8,128)S(1)}, u32[]{:S(2)}, u32[]{:S(2)}) collective-permute-start(f32[512,16]{0,1:T(8,128)S(1)} %fusion.4), channel_id=1, source_target_pairs={{0,32},{32,0},{64,96},{96,64},{128,160},{160,128},{192,224},{224,1... | collective-permute-start | bytes 98312 | tf_op jit(solution)/shard_map/ppermute | solution.py:29
  49.8 2.0 %collective-permute-done.4 = f32[512,16]{0,1:T(8,128)S(1)} collective-permute-done((f32[512,16]{0,1:T(8,128)S(1)}, f32[512,16]{0,1:T(8,128)S(1)}, u32[]{:S(2)}, u32[]{:S(2)}) %collective-permute-start.4) | collective-permute-done | bytes 32800 | tf_op jit(solution)/shard_map/ppermute | solution.py:29
  51.8 3.3 %collective-permute-start.5 = (f32[512,16]{0,1:T(8,128)S(1)}, f32[512,16]{0,1:T(8,128)S(1)}, u32[]{:S(2)}, u32[]{:S(2)}) collective-permute-start(f32[512,16]{0,1:T(8,128)S(1)} %add.67), channel_id=1, source_target_pairs={{0,64},{32,96},{64,0},{96,32},{128,192},{160,224},{192,128},{224,1... | collective-permute-start | bytes 98312 | tf_op jit(solution)/shard_map/ppermute | solution.py:29
  55.1 1.9 %collective-permute-done.5 = f32[512,16]{0,1:T(8,128)S(1)} collective-permute-done((f32[512,16]{0,1:T(8,128)S(1)}, f32[512,16]{0,1:T(8,128)S(1)}, u32[]{:S(2)}, u32[]{:S(2)}) %collective-permute-start.5) | collective-permute-done | bytes 32800 | tf_op jit(solution)/shard_map/ppermute | solution.py:29
  57.0 6.8 %collective-permute-start.6 = (f32[512,16]{0,1:T(8,128)S(1)}, f32[512,16]{0,1:T(8,128)S(1)}, u32[]{:S(2)}, u32[]{:S(2)}) collective-permute-start(f32[512,16]{0,1:T(8,128)S(1)} %add.68), channel_id=1, source_target_pairs={{0,128},{32,160},{64,192},{96,224},{128,0},{160,32},{192,64},{224,... | collective-permute-start | bytes 98312 | tf_op jit(solution)/shard_map/ppermute | solution.py:29
  63.9 1.8 %collective-permute-done.6 = f32[512,16]{0,1:T(8,128)S(1)} collective-permute-done((f32[512,16]{0,1:T(8,128)S(1)}, f32[512,16]{0,1:T(8,128)S(1)}, u32[]{:S(2)}, u32[]{:S(2)}) %collective-permute-start.6) | collective-permute-done | bytes 32800 | tf_op jit(solution)/shard_map/ppermute | solution.py:29
  65.7 0.6 add.69
  66.3 0.0 collective-permute-done.2
  66.3 0.0 collective-permute-done.3
  66.3 0.2 fusion
  66.5 0.8 %fusion.3 = (bf16[512,256]{1,0:T(8,128)(2,1)}, bf16[512,256]{1,0:T(8,128)(2,1)}) fusion(bf16[512,512]{1,0:T(8,128)(2,1)S(1)} %fusion), kind=kLoop, calls=%fused_computation.15 | loop fusion | bytes 1048576 | tf_op jit(solution)/shard_map/slice | solution.py:170
  (8 shorter events, 0.1 us)
Async XLA Ops:
  0.6 46.9 %copy-start = (bf16[16,512]{1,0:T(8,128)(2,1)S(1)}, bf16[16,512]{1,0:T(8,128)(2,1)}, u32[]{:S(2)}) copy-start(bf16[16,512]{1,0:T(8,128)(2,1)} %param.10) | copy-start | bytes 49156
  2.6 15.7 %collective-permute-start.1 = (bf16[512,512]{1,0:T(8,128)(2,1)S(1)}, bf16[512,512]{1,0:T(8,128)(2,1)S(1)}, u32[]{:S(2)}, u32[]{:S(2)}) collective-permute-start(bf16[512,512]{1,0:T(8,128)(2,1)S(1)} %constant_dynamic-update-slice_fusion), channel_id=1, source_target_pairs={{0,1},{1,2},{2,3},{3,4},{4,5},{5,6},{6,7},{7,8},{8,9},{9,10},{10,1... | collective-permute-start | bytes 1572872 | tf_op jit(solution)/shard_map/ppermute | solution.py:20
  4.5 18.8 %collective-permute-start = (bf16[512,512]{1,0:T(8,128)(2,1)S(1)}, bf16[512,512]{1,0:T(8,128)(2,1)S(1)}, u32[]{:S(2)}, u32[]{:S(2)}) collective-permute-start(bf16[512,512]{1,0:T(8,128)(2,1)S(1)} %constant_dynamic-update-slice_fusion), channel_id=1, source_target_pairs={{0,2},{1,3},{2,4},{3,5},{4,6},{5,7},{6,8},{7,9},{8,10},{9,11},{10,... | collective-permute-start | bytes 1572872 | tf_op jit(solution)/shard_map/ppermute | solution.py:20
  9.3 14.1 %copy-start.1 = (bf16[512,512]{1,0:T(8,128)(2,1)S(1)}, bf16[512,512]{1,0:T(8,128)(2,1)}, u32[]{:S(2)}) copy-start(bf16[512,512]{1,0:T(8,128)(2,1)} %q_ref.1) | copy-start | bytes 1572868
  9.3 14.1 %copy-start.2 = (bf16[512,512]{1,0:T(8,128)(2,1)S(1)}, bf16[512,512]{1,0:T(8,128)(2,1)}, u32[]{:S(2)}) copy-start(bf16[512,512]{1,0:T(8,128)(2,1)} %do_ref.1) | copy-start | bytes 1572868
  39.3 8.3 %copy-start.3 = (bf16[512,512]{1,0:T(8,128)(2,1)S(1)}, bf16[512,512]{1,0:T(8,128)(2,1)}, u32[]{:S(2)}) copy-start(bf16[512,512]{1,0:T(8,128)(2,1)} %get-tuple-element.5) | copy-start | bytes 1572868
  39.4 26.9 %collective-permute-start.2 = (bf16[512,512]{1,0:T(8,128)(2,1)S(1)}, bf16[512,512]{1,0:T(8,128)(2,1)S(1)}, u32[]{:S(2)}, u32[]{:S(2)}) collective-permute-start(bf16[512,512]{1,0:T(8,128)(2,1)S(1)} %get-tuple-element.13), channel_id=1, source_target_pairs={{1,0},{2,1},{3,2},{4,3},{5,4},{6,5},{7,6},{8,7},{9,8},{10,9},{11,1... | collective-permute-start | bytes 1572872 | tf_op jit(solution)/shard_map/ppermute | solution.py:20
  44.8 21.5 %collective-permute-start.3 = (bf16[512,512]{1,0:T(8,128)(2,1)S(1)}, bf16[512,512]{1,0:T(8,128)(2,1)S(1)}, u32[]{:S(2)}, u32[]{:S(2)}) collective-permute-start(bf16[512,512]{1,0:T(8,128)(2,1)S(1)} %get-tuple-element.14), channel_id=1, source_target_pairs={{2,0},{3,1},{4,2},{5,3},{6,4},{7,5},{8,6},{9,7},{10,8},{11,9},{12,... | collective-permute-start | bytes 1572872 | tf_op jit(solution)/shard_map/ppermute | solution.py:20
  47.8 3.9 %collective-permute-start.4 = (f32[512,16]{0,1:T(8,128)S(1)}, f32[512,16]{0,1:T(8,128)S(1)}, u32[]{:S(2)}, u32[]{:S(2)}) collective-permute-start(f32[512,16]{0,1:T(8,128)S(1)} %fusion.4), channel_id=1, source_target_pairs={{0,32},{32,0},{64,96},{96,64},{128,160},{160,128},{192,224},{224,1... | collective-permute-start | bytes 98312 | tf_op jit(solution)/shard_map/ppermute | solution.py:29
  51.8 5.2 %collective-permute-start.5 = (f32[512,16]{0,1:T(8,128)S(1)}, f32[512,16]{0,1:T(8,128)S(1)}, u32[]{:S(2)}, u32[]{:S(2)}) collective-permute-start(f32[512,16]{0,1:T(8,128)S(1)} %add.67), channel_id=1, source_target_pairs={{0,64},{32,96},{64,0},{96,32},{128,192},{160,224},{192,128},{224,1... | collective-permute-start | bytes 98312 | tf_op jit(solution)/shard_map/ppermute | solution.py:29
  57.0 8.7 %collective-permute-start.6 = (f32[512,16]{0,1:T(8,128)S(1)}, f32[512,16]{0,1:T(8,128)S(1)}, u32[]{:S(2)}, u32[]{:S(2)}) collective-permute-start(f32[512,16]{0,1:T(8,128)S(1)} %add.68), channel_id=1, source_target_pairs={{0,128},{32,160},{64,192},{96,224},{128,0},{160,32},{192,64},{224,... | collective-permute-start | bytes 98312 | tf_op jit(solution)/shard_map/ppermute | solution.py:29

commit v4 on v3

--- a/solution.py
+++ b/solution.py
@@ -18,17 +18,6 @@
     devices = range(lax.axis_size(axis))
     route = [(i - distance, i) for i in devices if i - distance in devices]
     return lax.ppermute(block, axis, route)
-
-
-def gathered_sum(part, axis):
-    count = lax.axis_size(axis)
-    total = part.astype(jnp.float32)
-    stride = 1
-    while stride < count:
-        route = [(i, i ^ stride) for i in range(count)]
-        total = total + lax.ppermute(total, axis, route)
-        stride *= 2
-    return total
 
 
 def doc_index(positions, doc_ends):
@@ -168,13 +157,16 @@
     total = jnp.concatenate([own[:cut_row], own[cut_row:] + returned], axis=0)
     key_total = total[:, :key_cols]
     value_total = total[:, key_cols:]
+    rank = adapter_up_matrix.shape[0]
+    lane_rows = -(-rank // HEAD_SIZE) * HEAD_SIZE
+    padded_up = jnp.pad(adapter_up_matrix, ((0, lane_rows - rank), (0, 0)))
     adapter_portion = lax.dot_general(
         flattened_query,
-        adapter_up_matrix,
+        padded_up,
         (((1,), (1,)), ((), ())),
         preferred_element_type=jnp.float32,
     )
-    adapter_gradient = gathered_sum(adapter_portion, "head")
+    adapter_gradient = lax.psum(adapter_portion, "head")[:, :rank]
     return (
         attended,
         flattened_query,

time: 67.7 us -> 142 us (2.10)
  waiting for transfers between devices: 19.7 us -> 88.3 us
  between operations: 0.84 us -> 14.2 us
  starting transfers between devices: 25.5 us -> 13.4 us
  local copies, waits for them, and re-layouts: 3.94 us -> 7.09 us
    psum x0 -> x1, waiting for transfers between devices: none -> 74.3 us  [body(): adapter_gradient = lax.psum(adapter_portion, 'head')[:, :rank]]
    ppermute x3 -> x0, starting transfers between devices: 12 us -> none  [gathered_sum(): total = total + lax.ppermute(total, axis, route)]
    ppermute x3 -> x0, waiting for transfers between devices: 5.73 us -> none  [gathered_sum(): total = total + lax.ppermute(total, axis, route)]
  transfers between devices with their start and end apart: 7 -> 5, of which waited for: 5 -> 3; matrix products, arithmetic and copies ran while one was open for 3% -> 3% of each run, Pallas kernels for 0% -> 0%
where the time goes in v4:
time: 142 us
  waiting for transfers between devices  88.3 us (62%)
  Pallas kernels  15.6 us (11%)
  between operations  14.2 us (10%)
  starting transfers between devices  13.4 us (9%)
  local copies, waits for them, and re-layouts  7.09 us (5%)
  other arithmetic  2.15 us (2%)
    psum x1, waiting for transfers between devices, body(): adapter_gradient = lax.psum(adapter_portion, 'head')[:, :rank]  74.3 us
    pallas_call x1, Pallas kernels, fused_attention(): pl.pallas_call(attention_kernel, grid=(groups, blocks), in_specs=[pl.Bloc...  15.6 us
    ppermute x4, waiting for transfers between devices, passed_along(): return lax.ppermute(block, axis, route)  14 us
    ppermute x4, starting transfers between devices, passed_along(): return lax.ppermute(block, axis, route)  13.3 us
  transfers between devices with their start and end apart: 5, of which 3 were waited for; matrix products, arithmetic and copies ran while one was open for 3% of the time, Pallas kernels for 0%

profile of v4, /device:TPU:24, one launch (start us, length us, event | category | flops | bytes accessed | tf_op | source)
XLA Modules:
  0.0 141.8 jit_solution(17654409103045351668)
XLA Ops:
  7.2 0.0 all-reduce.3.cloned.1.call-start
  7.2 1.0 constant_dynamic-update-slice_fusion.1
  8.2 1.0 constant_dynamic-update-slice_fusion
  9.2 1.9 %collective-permute-start.1 = (bf16[512,512]{1,0:T(8,128)(2,1)S(1)}, bf16[512,512]{1,0:T(8,128)(2,1)S(1)}, u32[]{:S(2)}, u32[]{:S(2)}) collective-permute-start(bf16[512,512]{1,0:T(8,128)(2,1)S(1)} %constant_dynamic-update-slice_fusion), channel_id=1, source_target_pairs={{0,1},{1,2},{2,3},{3,4},{4,5},{5,6},{6,7},{7,8},{8,9},{9,10},{10,1... | collective-permute-start | bytes 1572872 | tf_op jit(solution)/shard_map/ppermute | solution.py:20
  11.1 3.4 %collective-permute-start = (bf16[512,512]{1,0:T(8,128)(2,1)S(1)}, bf16[512,512]{1,0:T(8,128)(2,1)S(1)}, u32[]{:S(2)}, u32[]{:S(2)}) collective-permute-start(bf16[512,512]{1,0:T(8,128)(2,1)S(1)} %constant_dynamic-update-slice_fusion), channel_id=1, source_target_pairs={{0,2},{1,3},{2,4},{3,5},{4,6},{5,7},{6,8},{7,9},{8,10},{9,11},{10,... | collective-permute-start | bytes 1572872 | tf_op jit(solution)/shard_map/ppermute | solution.py:20
  14.5 0.7 copy.14
  15.3 0.1 reduce-window.8
  15.3 0.1 multiply_reduce_fusion
  15.4 0.1 convert_reduce_fusion.1
  15.5 0.2 copy.15
  15.7 0.1 convert_reduce_fusion
  15.9 0.0 copy-start
  15.9 0.0 copy-start.1
  15.9 9.0 %collective-permute-done.1 = bf16[512,512]{1,0:T(8,128)(2,1)S(1)} collective-permute-done((bf16[512,512]{1,0:T(8,128)(2,1)S(1)}, bf16[512,512]{1,0:T(8,128)(2,1)S(1)}, u32[]{:S(2)}, u32[]{:S(2)}) %collective-permute-start.1) | collective-permute-done | bytes 524320 | tf_op jit(solution)/shard_map/ppermute | solution.py:20
  24.9 5.0 %collective-permute-done = bf16[512,512]{1,0:T(8,128)(2,1)S(1)} collective-permute-done((bf16[512,512]{1,0:T(8,128)(2,1)S(1)}, bf16[512,512]{1,0:T(8,128)(2,1)S(1)}, u32[]{:S(2)}, u32[]{:S(2)}) %collective-permute-start) | collective-permute-done | bytes 524320 | tf_op jit(solution)/shard_map/ppermute | solution.py:20
  29.9 0.1 pad_maximum_fusion.k_ref.v_ref
  30.0 0.0 copy-done
  30.0 0.0 copy-done.1
  30.0 15.6 %shard_map.101 = (bf16[512,512]{1,0:T(8,128)(2,1)}, bf16[512,512]{1,0:T(8,128)(2,1)}, f32[1536,256]{1,0:T(8,128)S(1)}, f32[1536,256]{1,0:T(8,128)S(1)}) custom-call(bf16[512,512]{1,0:T(8,128)(2,1)S(1)} %copy-done, bf16[1536,512]{1,0:T(8,128)(2,1)S(1)} %pad_maximum_fusion.k_ref.v_ref, bf16[1536,512]{1,0:T(8,128)(2,1)S(1)} %pad_maximum_fusion.k_ref.v_ref, ...), custom_call_target="tpu_custom_call" | custom-call | flops 3623878656 | bytes 6815744 | tf_op jit(solution)/shard_map/pallas_call | solution.py:87
  45.7 0.1 slice.33
  45.7 0.1 slice.34
  45.8 0.1 maximum_convert_fusion
  45.9 0.0 copy-start.2
  45.9 0.0 copy-start.3
  45.9 1.1 fusion.5
  46.9 5.3 %collective-permute-start.2 = (bf16[512,512]{1,0:T(8,128)(2,1)}, bf16[512,512]{1,0:T(8,128)(2,1)}, u32[]{:S(2)}, u32[]{:S(2)}) collective-permute-start(bf16[512,512]{1,0:T(8,128)(2,1)} %get-tuple-element.13), channel_id=1, source_target_pairs={{1,0},{2,1},{3,2},{4,3},{5,4},{6,5},{7,6},{8,7},{9,8},{10,9},{11,1... | collective-permute-start | bytes 1572872 | tf_op jit(solution)/shard_map/ppermute | solution.py:20
  52.2 2.7 %collective-permute-start.3 = (bf16[512,512]{1,0:T(8,128)(2,1)}, bf16[512,512]{1,0:T(8,128)(2,1)}, u32[]{:S(2)}, u32[]{:S(2)}) collective-permute-start(bf16[512,512]{1,0:T(8,128)(2,1)} %get-tuple-element.14), channel_id=1, source_target_pairs={{2,0},{3,1},{4,2},{5,3},{6,4},{7,5},{8,6},{9,7},{10,8},{11,9},{12,... | collective-permute-start | bytes 1572872 | tf_op jit(solution)/shard_map/ppermute | solution.py:20
  55.0 0.0 copy-done.2
  55.0 0.0 copy-done.3
  55.0 1.0 fusion.2
  56.0 0.0 all-reduce.3.cloned.1.call-update
  56.0 0.8 slice.31
  56.9 74.3 %all-reduce.3.cloned.1.call-done = f32[512,128]{0,1:T(8,128)} async-done(((f32[512,128]{0,1:T(8,128)}), f32[512,128]{0,1:T(8,128)}) %all-reduce.3.cloned.1.call-update) | async-done | bytes 262160 | tf_op jit(solution)/shard_map/psum | solution.py:169
  131.2 1.4 slice.44
  132.6 0.0 collective-permute-done.2
  132.6 0.0 collective-permute-done.3
  132.6 1.5 %fusion = bf16[512,512]{1,0:T(8,128)(2,1)S(1)} fusion(f32[512,256]{1,0:T(8,128)S(1)} %slice.32, f32[512,256]{1,0:T(8,128)} %slice.31, bf16[512,512]{1,0:T(8,128)(2,1)} %collective-permute-done.3, bf16[512,512]{1,0:T(8,128)(2,1)} %collective-permute-done.2), kind=kLoop, calls=%fused_computation.3 | loop fusion | flops 1572864 | bytes 2621440 | tf_op jit(solution)/shard_map/convert.1
  134.1 0.8 fusion.6
  (5 shorter events, 0.1 us)
Async XLA Ops:
  7.2 124.1 %all-reduce.3.cloned.1.call-start = ((), (), s32[]{:S(2)}) async-start(), calls=%async_computation | async-start | bytes 524288 | tf_op jit(solution)/shard_map/psum | solution.py:169
  9.2 15.7 %collective-permute-start.1 = (bf16[512,512]{1,0:T(8,128)(2,1)S(1)}, bf16[512,512]{1,0:T(8,128)(2,1)S(1)}, u32[]{:S(2)}, u32[]{:S(2)}) collective-permute-start(bf16[512,512]{1,0:T(8,128)(2,1)S(1)} %constant_dynamic-update-slice_fusion), channel_id=1, source_target_pairs={{0,1},{1,2},{2,3},{3,4},{4,5},{5,6},{6,7},{7,8},{8,9},{9,10},{10,1... | collective-permute-start | bytes 1572872 | tf_op jit(solution)/shard_map/ppermute | solution.py:20
  11.1 18.8 %collective-permute-start = (bf16[512,512]{1,0:T(8,128)(2,1)S(1)}, bf16[512,512]{1,0:T(8,128)(2,1)S(1)}, u32[]{:S(2)}, u32[]{:S(2)}) collective-permute-start(bf16[512,512]{1,0:T(8,128)(2,1)S(1)} %constant_dynamic-update-slice_fusion), channel_id=1, source_target_pairs={{0,2},{1,3},{2,4},{3,5},{4,6},{5,7},{6,8},{7,9},{8,10},{9,11},{10,... | collective-permute-start | bytes 1572872 | tf_op jit(solution)/shard_map/ppermute | solution.py:20
  15.9 14.1 %copy-start = (bf16[512,512]{1,0:T(8,128)(2,1)S(1)}, bf16[512,512]{1,0:T(8,128)(2,1)}, u32[]{:S(2)}) copy-start(bf16[512,512]{1,0:T(8,128)(2,1)} %q_ref.1) | copy-start | bytes 1572868
  15.9 14.1 %copy-start.1 = (bf16[512,512]{1,0:T(8,128)(2,1)S(1)}, bf16[512,512]{1,0:T(8,128)(2,1)}, u32[]{:S(2)}) copy-start(bf16[512,512]{1,0:T(8,128)(2,1)} %do_ref.1) | copy-start | bytes 1572868
  45.9 9.1 %copy-start.2 = (bf16[512,512]{1,0:T(8,128)(2,1)S(1)}, bf16[512,512]{1,0:T(8,128)(2,1)}, u32[]{:S(2)}) copy-start(bf16[512,512]{1,0:T(8,128)(2,1)} %get-tuple-element.5) | copy-start | bytes 1572868
  45.9 9.1 %copy-start.3 = (bf16[16,512]{1,0:T(8,128)(2,1)S(1)}, bf16[16,512]{1,0:T(8,128)(2,1)}, u32[]{:S(2)}) copy-start(bf16[16,512]{1,0:T(8,128)(2,1)} %param.10) | copy-start | bytes 49156
  46.9 85.7 %collective-permute-start.2 = (bf16[512,512]{1,0:T(8,128)(2,1)}, bf16[512,512]{1,0:T(8,128)(2,1)}, u32[]{:S(2)}, u32[]{:S(2)}) collective-permute-start(bf16[512,512]{1,0:T(8,128)(2,1)} %get-tuple-element.13), channel_id=1, source_target_pairs={{1,0},{2,1},{3,2},{4,3},{5,4},{6,5},{7,6},{8,7},{9,8},{10,9},{11,1... | collective-permute-start | bytes 1572872 | tf_op jit(solution)/shard_map/ppermute | solution.py:20
  52.2 80.4 %collective-permute-start.3 = (bf16[512,512]{1,0:T(8,128)(2,1)}, bf16[512,512]{1,0:T(8,128)(2,1)}, u32[]{:S(2)}, u32[]{:S(2)}) collective-permute-start(bf16[512,512]{1,0:T(8,128)(2,1)} %get-tuple-element.14), channel_id=1, source_target_pairs={{2,0},{3,1},{4,2},{5,3},{6,4},{7,5},{8,6},{9,7},{10,8},{11,9},{12,... | collective-permute-start | bytes 1572872 | tf_op jit(solution)/shard_map/ppermute | solution.py:20
Sparse Core Ops, SparseCore 0:
  56.2 75.0 all-reduce.2

commit v5 on v3

--- a/solution.py
+++ b/solution.py
@@ -20,14 +20,22 @@
     return lax.ppermute(block, axis, route)
 
 
-def gathered_sum(part, axis):
-    count = lax.axis_size(axis)
-    total = part.astype(jnp.float32)
+def pairings(count):
+    if count == 8:
+        return [[i ^ 2 for i in range(8)], [(6 - i) % 8 if i % 2 == 0 else (8 - i) % 8 for i in range(8)], [i ^ 1 for i in range(8)]]
+    rounds = []
     stride = 1
     while stride < count:
-        route = [(i, i ^ stride) for i in range(count)]
+        rounds.append([i ^ stride for i in range(count)])
+        stride *= 2
+    return rounds
+
+
+def gathered_sum(part, axis):
+    total = part.astype(jnp.float32)
+    for partner in pairings(lax.axis_size(axis)):
+        route = [(i, partner[i]) for i in range(len(partner))]
         total = total + lax.ppermute(total, axis, route)
-        stride *= 2
     return total
 
 

time: 67.7 us -> 66.7 us (0.985)
  starting transfers between devices: 25.5 us -> 23.4 us
  waiting for transfers between devices: 19.7 us -> 20.9 us
    ppermute x3, starting transfers between devices: 12 us -> 9.94 us  [gathered_sum(): total = total + lax.ppermute(total, axis, route)]
    ppermute x3, waiting for transfers between devices: 5.73 us -> 6.94 us  [gathered_sum(): total = total + lax.ppermute(total, axis, route)]
where the time goes in v5:
time: 66.7 us; the launch traced here: 66.4 us
  starting transfers between devices  23.4 us (35%)
  waiting for transfers between devices  20.9 us (31%)
  Pallas kernels  15.7 us (24%)
  local copies, waits for them, and re-layouts  3.94 us (6%)
  other arithmetic  1.42 us (2%)
  between operations  0.84 us (1%)
    pallas_call x1, Pallas kernels, fused_attention(): pl.pallas_call(attention_kernel, grid=(groups, blocks), in_specs=[pl.Bloc...  15.7 us
    ppermute x4, waiting for transfers between devices, passed_along(): return lax.ppermute(block, axis, route)  14 us
    ppermute x4, starting transfers between devices, passed_along(): return lax.ppermute(block, axis, route)  13.5 us
    ppermute x3, starting transfers between devices, gathered_sum(): total = total + lax.ppermute(total, axis, route)  9.94 us
    ppermute x3, waiting for transfers between devices, gathered_sum(): total = total + lax.ppermute(total, axis, route)  6.94 us
  transfers between devices with their start and end apart: 7, of which 5 were waited for; matrix products, arithmetic and copies ran while one was open for 3% of the time, Pallas kernels for 0%

profile of v5, /device:TPU:24, one launch (start us, length us, event | category | flops | bytes accessed | tf_op | source)
XLA Modules:
  0.0 66.4 jit_solution(72283509848313896)
XLA Ops:
  0.6 0.0 copy-start
  0.6 1.0 %constant_dynamic-update-slice_fusion.1 = bf16[512,512]{1,0:T(8,128)(2,1)S(1)} fusion(bf16[512,256]{1,0:T(8,128)(2,1)} %param.7), kind=kLoop, calls=%fused_computation.12 | loop fusion | bytes 524288
  1.6 1.0 %constant_dynamic-update-slice_fusion = bf16[512,512]{1,0:T(8,128)(2,1)S(1)} fusion(bf16[512,512]{1,0:T(8,128)(2,1)S(1)} %constant_dynamic-update-slice_fusion.1, bf16[512,256]{1,0:T(8,128)(2,1)} %param.8), kind=kLoop, calls=%fused_computation.11 | loop fusion | bytes 524288 | tf_op jit(solution)/shard_map/concatenate | solution.py:155
  2.6 1.9 %collective-permute-start.1 = (bf16[512,512]{1,0:T(8,128)(2,1)S(1)}, bf16[512,512]{1,0:T(8,128)(2,1)S(1)}, u32[]{:S(2)}, u32[]{:S(2)}) collective-permute-start(bf16[512,512]{1,0:T(8,128)(2,1)S(1)} %constant_dynamic-update-slice_fusion), channel_id=1, source_target_pairs={{0,1},{1,2},{2,3},{3,4},{4,5},{5,6},{6,7},{7,8},{8,9},{9,10},{10,1... | collective-permute-start | bytes 1572872 | tf_op jit(solution)/shard_map/ppermute | solution.py:20
  4.5 3.4 %collective-permute-start = (bf16[512,512]{1,0:T(8,128)(2,1)S(1)}, bf16[512,512]{1,0:T(8,128)(2,1)S(1)}, u32[]{:S(2)}, u32[]{:S(2)}) collective-permute-start(bf16[512,512]{1,0:T(8,128)(2,1)S(1)} %constant_dynamic-update-slice_fusion), channel_id=1, source_target_pairs={{0,2},{1,3},{2,4},{3,5},{4,6},{5,7},{6,8},{7,9},{8,10},{9,11},{10,... | collective-permute-start | bytes 1572872 | tf_op jit(solution)/shard_map/ppermute | solution.py:20
  8.0 0.7 %copy.14 = s32[32,1]{1,0:T(8,128)S(1)} copy(s32[32,1]{0,1:T(1,128)} %bitcast.5) | data formatting | bytes 256 | tf_op jit(solution)/shard_map/reshape.64
  8.7 0.1 reduce-window.8
  8.8 0.1 multiply_reduce_fusion
  8.9 0.1 convert_reduce_fusion.1
  9.0 0.2 copy.15
  9.1 0.1 convert_reduce_fusion
  9.3 0.0 copy-start.1
  9.3 0.0 copy-start.2
  9.3 9.0 %collective-permute-done.1 = bf16[512,512]{1,0:T(8,128)(2,1)S(1)} collective-permute-done((bf16[512,512]{1,0:T(8,128)(2,1)S(1)}, bf16[512,512]{1,0:T(8,128)(2,1)S(1)}, u32[]{:S(2)}, u32[]{:S(2)}) %collective-permute-start.1) | collective-permute-done | bytes 524320 | tf_op jit(solution)/shard_map/ppermute | solution.py:20
  18.3 5.0 %collective-permute-done = bf16[512,512]{1,0:T(8,128)(2,1)S(1)} collective-permute-done((bf16[512,512]{1,0:T(8,128)(2,1)S(1)}, bf16[512,512]{1,0:T(8,128)(2,1)S(1)}, u32[]{:S(2)}, u32[]{:S(2)}) %collective-permute-start) | collective-permute-done | bytes 524320 | tf_op jit(solution)/shard_map/ppermute | solution.py:20
  23.3 0.1 pad_maximum_fusion.k_ref.v_ref
  23.4 0.0 copy-done.1
  23.4 0.0 copy-done.2
  23.5 15.7 %shard_map.101 = (bf16[512,512]{1,0:T(8,128)(2,1)}, bf16[512,512]{1,0:T(8,128)(2,1)}, f32[1536,256]{1,0:T(8,128)S(1)}, f32[1536,256]{1,0:T(8,128)S(1)}) custom-call(bf16[512,512]{1,0:T(8,128)(2,1)S(1)} %copy-done.1, bf16[1536,512]{1,0:T(8,128)(2,1)S(1)} %pad_maximum_fusion.k_ref.v_ref, bf16[1536,512]{1,0:T(8,128)(2,1)S(1)} %pad_maximum_fusion.k_ref.v_ref, ...), custom_call_target="tpu_custom_call" | custom-call | flops 3623878656 | bytes 6815744 | tf_op jit(solution)/shard_map/pallas_call | solution.py:106
  39.1 0.1 slice.30
  39.2 0.1 slice.31
  39.2 0.1 maximum_convert_fusion
  39.3 0.0 copy-start.3
  39.3 0.1 fusion.2
  39.4 5.4 %collective-permute-start.2 = (bf16[512,512]{1,0:T(8,128)(2,1)S(1)}, bf16[512,512]{1,0:T(8,128)(2,1)S(1)}, u32[]{:S(2)}, u32[]{:S(2)}) collective-permute-start(bf16[512,512]{1,0:T(8,128)(2,1)S(1)} %get-tuple-element.13), channel_id=1, source_target_pairs={{1,0},{2,1},{3,2},{4,3},{5,4},{6,5},{7,6},{8,7},{9,8},{10,9},{11,1... | collective-permute-start | bytes 1572872 | tf_op jit(solution)/shard_map/ppermute | solution.py:20
  44.8 2.7 %collective-permute-start.3 = (bf16[512,512]{1,0:T(8,128)(2,1)S(1)}, bf16[512,512]{1,0:T(8,128)(2,1)S(1)}, u32[]{:S(2)}, u32[]{:S(2)}) collective-permute-start(bf16[512,512]{1,0:T(8,128)(2,1)S(1)} %get-tuple-element.14), channel_id=1, source_target_pairs={{2,0},{3,1},{4,2},{5,3},{6,4},{7,5},{8,6},{9,7},{10,8},{11,9},{12,... | collective-permute-start | bytes 1572872 | tf_op jit(solution)/shard_map/ppermute | solution.py:20
  47.6 0.0 copy-done
  47.6 0.0 copy-done.3
  47.6 0.2 fusion.4
  47.8 3.3 %collective-permute-start.4 = (f32[512,16]{0,1:T(8,128)S(1)}, f32[512,16]{0,1:T(8,128)S(1)}, u32[]{:S(2)}, u32[]{:S(2)}) collective-permute-start(f32[512,16]{0,1:T(8,128)S(1)} %fusion.4), channel_id=1, source_target_pairs={{0,64},{32,96},{64,0},{96,32},{128,192},{160,224},{192,128},{224,1... | collective-permute-start | bytes 98312 | tf_op jit(solution)/shard_map/ppermute | solution.py:38
  51.1 2.2 %collective-permute-done.4 = f32[512,16]{0,1:T(8,128)S(1)} collective-permute-done((f32[512,16]{0,1:T(8,128)S(1)}, f32[512,16]{0,1:T(8,128)S(1)}, u32[]{:S(2)}, u32[]{:S(2)}) %collective-permute-start.4) | collective-permute-done | bytes 32800 | tf_op jit(solution)/shard_map/ppermute | solution.py:38
  53.3 5.6 %collective-permute-start.5 = (f32[512,16]{0,1:T(8,128)S(1)}, f32[512,16]{0,1:T(8,128)S(1)}, u32[]{:S(2)}, u32[]{:S(2)}) collective-permute-start(f32[512,16]{0,1:T(8,128)S(1)} %add.67), channel_id=1, source_target_pairs={{0,192},{32,224},{64,128},{96,160},{128,64},{160,96},{192,0},{224,... | collective-permute-start | bytes 98312 | tf_op jit(solution)/shard_map/ppermute | solution.py:38
  59.0 1.9 %collective-permute-done.5 = f32[512,16]{0,1:T(8,128)S(1)} collective-permute-done((f32[512,16]{0,1:T(8,128)S(1)}, f32[512,16]{0,1:T(8,128)S(1)}, u32[]{:S(2)}, u32[]{:S(2)}) %collective-permute-start.5) | collective-permute-done | bytes 32800 | tf_op jit(solution)/shard_map/ppermute | solution.py:38
  60.9 1.0 %collective-permute-start.6 = (f32[512,16]{0,1:T(8,128)S(1)}, f32[512,16]{0,1:T(8,128)S(1)}, u32[]{:S(2)}, u32[]{:S(2)}) collective-permute-start(f32[512,16]{0,1:T(8,128)S(1)} %add.68), channel_id=1, source_target_pairs={{0,32},{32,0},{64,96},{96,64},{128,160},{160,128},{192,224},{224,1... | collective-permute-start | bytes 98312 | tf_op jit(solution)/shard_map/ppermute | solution.py:38
  62.0 2.8 %collective-permute-done.6 = f32[512,16]{0,1:T(8,128)S(1)} collective-permute-done((f32[512,16]{0,1:T(8,128)S(1)}, f32[512,16]{0,1:T(8,128)S(1)}, u32[]{:S(2)}, u32[]{:S(2)}) %collective-permute-start.6) | collective-permute-done | bytes 32800 | tf_op jit(solution)/shard_map/ppermute | solution.py:38
  64.8 0.6 add.69
  65.4 0.0 collective-permute-done.2
  65.4 0.0 collective-permute-done.3
  65.4 0.2 fusion
  65.6 0.8 %fusion.3 = (bf16[512,256]{1,0:T(8,128)(2,1)}, bf16[512,256]{1,0:T(8,128)(2,1)}) fusion(bf16[512,512]{1,0:T(8,128)(2,1)S(1)} %fusion), kind=kLoop, calls=%fused_computation.15 | loop fusion | bytes 1048576 | tf_op jit(solution)/shard_map/slice | solution.py:178
  (8 shorter events, 0.1 us)
Async XLA Ops:
  0.6 46.9 %copy-start = (bf16[16,512]{1,0:T(8,128)(2,1)S(1)}, bf16[16,512]{1,0:T(8,128)(2,1)}, u32[]{:S(2)}) copy-start(bf16[16,512]{1,0:T(8,128)(2,1)} %param.10) | copy-start | bytes 49156
  2.6 15.7 %collective-permute-start.1 = (bf16[512,512]{1,0:T(8,128)(2,1)S(1)}, bf16[512,512]{1,0:T(8,128)(2,1)S(1)}, u32[]{:S(2)}, u32[]{:S(2)}) collective-permute-start(bf16[512,512]{1,0:T(8,128)(2,1)S(1)} %constant_dynamic-update-slice_fusion), channel_id=1, source_target_pairs={{0,1},{1,2},{2,3},{3,4},{4,5},{5,6},{6,7},{7,8},{8,9},{9,10},{10,1... | collective-permute-start | bytes 1572872 | tf_op jit(solution)/shard_map/ppermute | solution.py:20
  4.5 18.8 %collective-permute-start = (bf16[512,512]{1,0:T(8,128)(2,1)S(1)}, bf16[512,512]{1,0:T(8,128)(2,1)S(1)}, u32[]{:S(2)}, u32[]{:S(2)}) collective-permute-start(bf16[512,512]{1,0:T(8,128)(2,1)S(1)} %constant_dynamic-update-slice_fusion), channel_id=1, source_target_pairs={{0,2},{1,3},{2,4},{3,5},{4,6},{5,7},{6,8},{7,9},{8,10},{9,11},{10,... | collective-permute-start | bytes 1572872 | tf_op jit(solution)/shard_map/ppermute | solution.py:20
  9.3 14.1 %copy-start.1 = (bf16[512,512]{1,0:T(8,128)(2,1)S(1)}, bf16[512,512]{1,0:T(8,128)(2,1)}, u32[]{:S(2)}) copy-start(bf16[512,512]{1,0:T(8,128)(2,1)} %q_ref.1) | copy-start | bytes 1572868
  9.3 14.1 %copy-start.2 = (bf16[512,512]{1,0:T(8,128)(2,1)S(1)}, bf16[512,512]{1,0:T(8,128)(2,1)}, u32[]{:S(2)}) copy-start(bf16[512,512]{1,0:T(8,128)(2,1)} %do_ref.1) | copy-start | bytes 1572868
  39.3 8.3 %copy-start.3 = (bf16[512,512]{1,0:T(8,128)(2,1)S(1)}, bf16[512,512]{1,0:T(8,128)(2,1)}, u32[]{:S(2)}) copy-start(bf16[512,512]{1,0:T(8,128)(2,1)} %get-tuple-element.5) | copy-start | bytes 1572868
  39.4 26.0 %collective-permute-start.2 = (bf16[512,512]{1,0:T(8,128)(2,1)S(1)}, bf16[512,512]{1,0:T(8,128)(2,1)S(1)}, u32[]{:S(2)}, u32[]{:S(2)}) collective-permute-start(bf16[512,512]{1,0:T(8,128)(2,1)S(1)} %get-tuple-element.13), channel_id=1, source_target_pairs={{1,0},{2,1},{3,2},{4,3},{5,4},{6,5},{7,6},{8,7},{9,8},{10,9},{11,1... | collective-permute-start | bytes 1572872 | tf_op jit(solution)/shard_map/ppermute | solution.py:20
  44.8 20.6 %collective-permute-start.3 = (bf16[512,512]{1,0:T(8,128)(2,1)S(1)}, bf16[512,512]{1,0:T(8,128)(2,1)S(1)}, u32[]{:S(2)}, u32[]{:S(2)}) collective-permute-start(bf16[512,512]{1,0:T(8,128)(2,1)S(1)} %get-tuple-element.14), channel_id=1, source_target_pairs={{2,0},{3,1},{4,2},{5,3},{6,4},{7,5},{8,6},{9,7},{10,8},{11,9},{12,... | collective-permute-start | bytes 1572872 | tf_op jit(solution)/shard_map/ppermute | solution.py:20
  47.8 5.5 %collective-permute-start.4 = (f32[512,16]{0,1:T(8,128)S(1)}, f32[512,16]{0,1:T(8,128)S(1)}, u32[]{:S(2)}, u32[]{:S(2)}) collective-permute-start(f32[512,16]{0,1:T(8,128)S(1)} %fusion.4), channel_id=1, source_target_pairs={{0,64},{32,96},{64,0},{96,32},{128,192},{160,224},{192,128},{224,1... | collective-permute-start | bytes 98312 | tf_op jit(solution)/shard_map/ppermute | solution.py:38
  53.3 7.5 %collective-permute-start.5 = (f32[512,16]{0,1:T(8,128)S(1)}, f32[512,16]{0,1:T(8,128)S(1)}, u32[]{:S(2)}, u32[]{:S(2)}) collective-permute-start(f32[512,16]{0,1:T(8,128)S(1)} %add.67), channel_id=1, source_target_pairs={{0,192},{32,224},{64,128},{96,160},{128,64},{160,96},{192,0},{224,... | collective-permute-start | bytes 98312 | tf_op jit(solution)/shard_map/ppermute | solution.py:38
  60.9 3.9 %collective-permute-start.6 = (f32[512,16]{0,1:T(8,128)S(1)}, f32[512,16]{0,1:T(8,128)S(1)}, u32[]{:S(2)}, u32[]{:S(2)}) collective-permute-start(f32[512,16]{0,1:T(8,128)S(1)} %add.68), channel_id=1, source_target_pairs={{0,32},{32,0},{64,96},{96,64},{128,160},{160,128},{192,224},{224,1... | collective-permute-start | bytes 98312 | tf_op jit(solution)/shard_map/ppermute | solution.py:38

commit v6 on v5

--- a/solution.py
+++ b/solution.py
@@ -44,7 +44,7 @@
     return jnp.where(positions < 0, -1, counted)
 
 
-def attention_kernel(q_ref, k_ref, v_ref, do_ref, qdoc_ref, kdoc_ref,
+def attention_kernel(q_ref, k_ref, v_ref, do_ref, qdoc_ref, kdoc_ref, bias_ref,
                      o_ref, dq_ref, dk_ref, dv_ref):
     qb = pl.program_id(1)
     rows = q_ref.shape[0]
@@ -63,14 +63,10 @@
     qdoc = qdoc_ref[...]
     qdoc = jnp.concatenate([qdoc, qdoc], axis=0)
     kdoc = kdoc_ref[:, pl.ds(key_first, span)]
-    row = lax.broadcasted_iota(jnp.int32, (2 * rows, span), 0) % rows
-    col = lax.broadcasted_iota(jnp.int32, (2 * rows, span), 1)
-    offset = row + WIN - col
-    live = (offset >= 0) & (offset < WIN) & (qdoc == kdoc)
 
     s = lax.dot_general(q, k, (((1,), (1,)), ((), ())),
                         preferred_element_type=jnp.float32) * softmax_scale
-    masked = jnp.where(live, s, masked_value)
+    masked = jnp.where(qdoc == kdoc, s + bias_ref[...], masked_value)
     row_max = jnp.max(masked, axis=1, keepdims=True)
     e = jnp.exp(masked - row_max)
     row_sum = jnp.sum(e, axis=1, keepdims=True)
@@ -113,6 +109,7 @@
             pl.BlockSpec((rows, pair), lambda g, b: (b, g)),
             pl.BlockSpec((rows, 1), lambda g, b: (b, 0)),
             pl.BlockSpec((1, ext_rows), lambda g, b: (0, 0)),
+            pl.BlockSpec((2 * rows, span), lambda g, b: (0, 0)),
         ],
         out_specs=[
             pl.BlockSpec((rows, pair), lambda g, b: (b, g)),
@@ -133,7 +130,16 @@
         cost_estimate=pl.CostEstimate(
             flops=flops, transcendentals=groups * blocks * 2 * rows * span,
             bytes_accessed=nbytes),
-    )(queries, extended, extended, output_gradient, qdoc, kdoc)
+    )(queries, extended, extended, output_gradient, qdoc, kdoc, window_bias(rows))
+
+
+def window_bias(rows):
+    span = rows + WIN
+    row = lax.broadcasted_iota(jnp.int32, (2 * rows, span), 0) % rows
+    col = lax.broadcasted_iota(jnp.int32, (2 * rows, span), 1)
+    offset = row + WIN - col
+    inside = (offset >= 0) & (offset < WIN)
+    return jnp.where(inside, 0.0, masked_value).astype(jnp.float32)
 
 
 def body(

time: 66.7 us -> 67.7 us (1.015)
  other arithmetic: 1.42 us -> 2.92 us
    concatenate x1, other arithmetic: 0.1 us -> 1.27 us  [body(): extended = jnp.concatenate(arrived[::-1] + [joined], axis=0)]
  transfers between devices with their start and end apart: 7 -> 7, of which waited for: 5 -> 5; matrix products, arithmetic and copies ran while one was open for 3% -> 4% of each run, Pallas kernels for 0% -> 0%
where the time goes in v6:
time: 67.7 us; the launch traced here: 67.4 us
  starting transfers between devices  23.4 us (35%)
  waiting for transfers between devices  20.5 us (30%)
  Pallas kernels  15.5 us (23%)
  local copies, waits for them, and re-layouts  3.93 us (6%)
  other arithmetic  2.92 us (4%)
  between operations  0.85 us (1%)
    pallas_call x1, Pallas kernels, fused_attention(): pl.pallas_call(attention_kernel, grid=(groups, blocks), in_specs=[pl.Bloc...  15.5 us
    ppermute x4, waiting for transfers between devices, passed_along(): return lax.ppermute(block, axis, route)  13.7 us
    ppermute x4, starting transfers between devices, passed_along(): return lax.ppermute(block, axis, route)  13.5 us
    ppermute x3, starting transfers between devices, gathered_sum(): total = total + lax.ppermute(total, axis, route)  9.97 us
    ppermute x3, waiting for transfers between devices, gathered_sum(): total = total + lax.ppermute(total, axis, route)  6.88 us
  transfers between devices with their start and end apart: 7, of which 5 were waited for; matrix products, arithmetic and copies ran while one was open for 4% of the time, Pallas kernels for 0%

profile of v6, /device:TPU:24, one launch (start us, length us, event | category | flops | bytes accessed | tf_op | source)
XLA Modules:
  0.0 67.4 jit_solution(18036938442641181428)
XLA Ops:
  0.6 0.0 copy-start
  0.6 1.0 %constant_dynamic-update-slice_fusion.1 = bf16[512,512]{1,0:T(8,128)(2,1)S(1)} fusion(bf16[512,256]{1,0:T(8,128)(2,1)} %param.7), kind=kLoop, calls=%fused_computation.17 | loop fusion | bytes 524288
  1.6 1.0 %constant_dynamic-update-slice_fusion = bf16[512,512]{1,0:T(8,128)(2,1)S(1)} fusion(bf16[512,512]{1,0:T(8,128)(2,1)S(1)} %constant_dynamic-update-slice_fusion.1, bf16[512,256]{1,0:T(8,128)(2,1)} %param.8), kind=kLoop, calls=%fused_computation.16 | loop fusion | bytes 524288 | tf_op jit(solution)/shard_map/concatenate | solution.py:161
  2.6 1.9 %collective-permute-start.1 = (bf16[512,512]{1,0:T(8,128)(2,1)S(1)}, bf16[512,512]{1,0:T(8,128)(2,1)S(1)}, u32[]{:S(2)}, u32[]{:S(2)}) collective-permute-start(bf16[512,512]{1,0:T(8,128)(2,1)S(1)} %constant_dynamic-update-slice_fusion), channel_id=1, source_target_pairs={{0,1},{1,2},{2,3},{3,4},{4,5},{5,6},{6,7},{7,8},{8,9},{9,10},{10,1... | collective-permute-start | bytes 1572872 | tf_op jit(solution)/shard_map/ppermute | solution.py:20
  4.5 3.4 %collective-permute-start = (bf16[512,512]{1,0:T(8,128)(2,1)S(1)}, bf16[512,512]{1,0:T(8,128)(2,1)S(1)}, u32[]{:S(2)}, u32[]{:S(2)}) collective-permute-start(bf16[512,512]{1,0:T(8,128)(2,1)S(1)} %constant_dynamic-update-slice_fusion), channel_id=1, source_target_pairs={{0,2},{1,3},{2,4},{3,5},{4,6},{5,7},{6,8},{7,9},{8,10},{9,11},{10,... | collective-permute-start | bytes 1572872 | tf_op jit(solution)/shard_map/ppermute | solution.py:20
  8.0 0.7 %copy.14 = s32[32,1]{1,0:T(8,128)S(1)} copy(s32[32,1]{0,1:T(1,128)} %bitcast.5) | data formatting | bytes 256 | tf_op jit(solution)/shard_map/reshape.64
  8.7 0.1 reduce-window.8
  8.8 0.1 multiply_reduce_fusion
  8.9 0.1 convert_reduce_fusion
  9.0 0.1 convert_reduce_fusion.1
  9.1 0.1 copy.15
  9.3 0.3 fusion.3.bias_ref
  9.7 0.0 copy-start.1
  9.7 0.0 copy-start.2
  9.7 8.6 %collective-permute-done.1 = bf16[512,512]{1,0:T(8,128)(2,1)S(1)} collective-permute-done((bf16[512,512]{1,0:T(8,128)(2,1)S(1)}, bf16[512,512]{1,0:T(8,128)(2,1)S(1)}, u32[]{:S(2)}, u32[]{:S(2)}) %collective-permute-start.1) | collective-permute-done | bytes 524320 | tf_op jit(solution)/shard_map/ppermute | solution.py:20
  18.3 5.0 %collective-permute-done = bf16[512,512]{1,0:T(8,128)(2,1)S(1)} collective-permute-done((bf16[512,512]{1,0:T(8,128)(2,1)S(1)}, bf16[512,512]{1,0:T(8,128)(2,1)S(1)}, u32[]{:S(2)}, u32[]{:S(2)}) %collective-permute-start) | collective-permute-done | bytes 524320 | tf_op jit(solution)/shard_map/ppermute | solution.py:20
  23.3 1.3 %pad_maximum_fusion.k_ref.v_ref = bf16[1536,512]{1,0:T(8,128)(2,1)} fusion(bf16[512,512]{1,0:T(8,128)(2,1)S(1)} %constant_dynamic-update-slice_fusion, bf16[512,512]{1,0:T(8,128)(2,1)S(1)} %collective-permute-done.1, bf16[512,512]{1,0:T(8,128)(2,1)S(1)} %collective-permute-done), kind=kLoop, calls=%fused_computation.1 | loop fusion | flops 4718592 | bytes 3145728 | tf_op jit(solution)/shard_map/concatenate | solution.py:165
  24.6 0.0 copy-done.1
  24.6 0.0 copy-done.2
  24.6 15.5 %shard_map.101 = (bf16[512,512]{1,0:T(8,128)(2,1)}, bf16[512,512]{1,0:T(8,128)(2,1)}, f32[1536,256]{1,0:T(8,128)S(1)}, f32[1536,256]{1,0:T(8,128)S(1)}) custom-call(bf16[512,512]{1,0:T(8,128)(2,1)S(1)} %copy-done.1, bf16[1536,512]{1,0:T(8,128)(2,1)} %pad_maximum_fusion.k_ref.v_ref, bf16[1536,512]{1,0:T(8,128)(2,1)} %pad_maximum_fusion.k_ref.v_ref, ...), custom_call_target="tpu_custom_call" | custom-call | flops 3623878656 | bytes 6815744 | tf_op jit(solution)/shard_map/pallas_call | solution.py:102
  40.1 0.1 slice.30
  40.1 0.1 slice.31
  40.2 0.1 maximum_convert_fusion
  40.3 0.0 copy-start.3
  40.3 0.1 fusion.7
  40.4 5.4 %collective-permute-start.2 = (bf16[512,512]{1,0:T(8,128)(2,1)S(1)}, bf16[512,512]{1,0:T(8,128)(2,1)S(1)}, u32[]{:S(2)}, u32[]{:S(2)}) collective-permute-start(bf16[512,512]{1,0:T(8,128)(2,1)S(1)} %get-tuple-element.13), channel_id=1, source_target_pairs={{1,0},{2,1},{3,2},{4,3},{5,4},{6,5},{7,6},{8,7},{9,8},{10,9},{11,1... | collective-permute-start | bytes 1572872 | tf_op jit(solution)/shard_map/ppermute | solution.py:20
  45.8 2.7 %collective-permute-start.3 = (bf16[512,512]{1,0:T(8,128)(2,1)S(1)}, bf16[512,512]{1,0:T(8,128)(2,1)S(1)}, u32[]{:S(2)}, u32[]{:S(2)}) collective-permute-start(bf16[512,512]{1,0:T(8,128)(2,1)S(1)} %get-tuple-element.14), channel_id=1, source_target_pairs={{2,0},{3,1},{4,2},{5,3},{6,4},{7,5},{8,6},{9,7},{10,8},{11,9},{12,... | collective-permute-start | bytes 1572872 | tf_op jit(solution)/shard_map/ppermute | solution.py:20
  48.5 0.0 copy-done
  48.6 0.0 copy-done.3
  48.6 0.2 fusion.9
  48.8 3.3 %collective-permute-start.4 = (f32[512,16]{0,1:T(8,128)S(1)}, f32[512,16]{0,1:T(8,128)S(1)}, u32[]{:S(2)}, u32[]{:S(2)}) collective-permute-start(f32[512,16]{0,1:T(8,128)S(1)} %fusion.9), channel_id=1, source_target_pairs={{0,64},{32,96},{64,0},{96,32},{128,192},{160,224},{192,128},{224,1... | collective-permute-start | bytes 98312 | tf_op jit(solution)/shard_map/ppermute | solution.py:38
  52.1 2.2 %collective-permute-done.4 = f32[512,16]{0,1:T(8,128)S(1)} collective-permute-done((f32[512,16]{0,1:T(8,128)S(1)}, f32[512,16]{0,1:T(8,128)S(1)}, u32[]{:S(2)}, u32[]{:S(2)}) %collective-permute-start.4) | collective-permute-done | bytes 32800 | tf_op jit(solution)/shard_map/ppermute | solution.py:38
  54.3 5.6 %collective-permute-start.5 = (f32[512,16]{0,1:T(8,128)S(1)}, f32[512,16]{0,1:T(8,128)S(1)}, u32[]{:S(2)}, u32[]{:S(2)}) collective-permute-start(f32[512,16]{0,1:T(8,128)S(1)} %add.79), channel_id=1, source_target_pairs={{0,192},{32,224},{64,128},{96,160},{128,64},{160,96},{192,0},{224,... | collective-permute-start | bytes 98312 | tf_op jit(solution)/shard_map/ppermute | solution.py:38
  59.9 1.9 %collective-permute-done.5 = f32[512,16]{0,1:T(8,128)S(1)} collective-permute-done((f32[512,16]{0,1:T(8,128)S(1)}, f32[512,16]{0,1:T(8,128)S(1)}, u32[]{:S(2)}, u32[]{:S(2)}) %collective-permute-start.5) | collective-permute-done | bytes 32800 | tf_op jit(solution)/shard_map/ppermute | solution.py:38
  61.8 1.0 %collective-permute-start.6 = (f32[512,16]{0,1:T(8,128)S(1)}, f32[512,16]{0,1:T(8,128)S(1)}, u32[]{:S(2)}, u32[]{:S(2)}) collective-permute-start(f32[512,16]{0,1:T(8,128)S(1)} %add.80), channel_id=1, source_target_pairs={{0,32},{32,0},{64,96},{96,64},{128,160},{160,128},{192,224},{224,1... | collective-permute-start | bytes 98312 | tf_op jit(solution)/shard_map/ppermute | solution.py:38
  63.0 2.8 %collective-permute-done.6 = f32[512,16]{0,1:T(8,128)S(1)} collective-permute-done((f32[512,16]{0,1:T(8,128)S(1)}, f32[512,16]{0,1:T(8,128)S(1)}, u32[]{:S(2)}, u32[]{:S(2)}) %collective-permute-start.6) | collective-permute-done | bytes 32800 | tf_op jit(solution)/shard_map/ppermute | solution.py:38
  65.8 0.6 add.81
  66.4 0.0 collective-permute-done.2
  66.4 0.0 collective-permute-done.3
  66.4 0.2 fusion.4
  66.6 0.8 %fusion.8 = (bf16[512,256]{1,0:T(8,128)(2,1)}, bf16[512,256]{1,0:T(8,128)(2,1)}) fusion(bf16[512,512]{1,0:T(8,128)(2,1)S(1)} %fusion.4), kind=kLoop, calls=%fused_computation.23 | loop fusion | bytes 1048576 | tf_op jit(solution)/shard_map/slice | solution.py:184
  (10 shorter events, 0.2 us)
Async XLA Ops:
  0.6 47.9 %copy-start = (bf16[16,512]{1,0:T(8,128)(2,1)S(1)}, bf16[16,512]{1,0:T(8,128)(2,1)}, u32[]{:S(2)}) copy-start(bf16[16,512]{1,0:T(8,128)(2,1)} %param.10) | copy-start | bytes 49156
  2.6 15.7 %collective-permute-start.1 = (bf16[512,512]{1,0:T(8,128)(2,1)S(1)}, bf16[512,512]{1,0:T(8,128)(2,1)S(1)}, u32[]{:S(2)}, u32[]{:S(2)}) collective-permute-start(bf16[512,512]{1,0:T(8,128)(2,1)S(1)} %constant_dynamic-update-slice_fusion), channel_id=1, source_target_pairs={{0,1},{1,2},{2,3},{3,4},{4,5},{5,6},{6,7},{7,8},{8,9},{9,10},{10,1... | collective-permute-start | bytes 1572872 | tf_op jit(solution)/shard_map/ppermute | solution.py:20
  4.5 18.8 %collective-permute-start = (bf16[512,512]{1,0:T(8,128)(2,1)S(1)}, bf16[512,512]{1,0:T(8,128)(2,1)S(1)}, u32[]{:S(2)}, u32[]{:S(2)}) collective-permute-start(bf16[512,512]{1,0:T(8,128)(2,1)S(1)} %constant_dynamic-update-slice_fusion), channel_id=1, source_target_pairs={{0,2},{1,3},{2,4},{3,5},{4,6},{5,7},{6,8},{7,9},{8,10},{9,11},{10,... | collective-permute-start | bytes 1572872 | tf_op jit(solution)/shard_map/ppermute | solution.py:20
  9.7 14.9 %copy-start.1 = (bf16[512,512]{1,0:T(8,128)(2,1)S(1)}, bf16[512,512]{1,0:T(8,128)(2,1)}, u32[]{:S(2)}) copy-start(bf16[512,512]{1,0:T(8,128)(2,1)} %q_ref.1) | copy-start | bytes 1572868
  9.7 14.9 %copy-start.2 = (bf16[512,512]{1,0:T(8,128)(2,1)S(1)}, bf16[512,512]{1,0:T(8,128)(2,1)}, u32[]{:S(2)}) copy-start(bf16[512,512]{1,0:T(8,128)(2,1)} %do_ref.1) | copy-start | bytes 1572868
  40.3 8.3 %copy-start.3 = (bf16[512,512]{1,0:T(8,128)(2,1)S(1)}, bf16[512,512]{1,0:T(8,128)(2,1)}, u32[]{:S(2)}) copy-start(bf16[512,512]{1,0:T(8,128)(2,1)} %get-tuple-element.5) | copy-start | bytes 1572868
  40.4 26.0 %collective-permute-start.2 = (bf16[512,512]{1,0:T(8,128)(2,1)S(1)}, bf16[512,512]{1,0:T(8,128)(2,1)S(1)}, u32[]{:S(2)}, u32[]{:S(2)}) collective-permute-start(bf16[512,512]{1,0:T(8,128)(2,1)S(1)} %get-tuple-element.13), channel_id=1, source_target_pairs={{1,0},{2,1},{3,2},{4,3},{5,4},{6,5},{7,6},{8,7},{9,8},{10,9},{11,1... | collective-permute-start | bytes 1572872 | tf_op jit(solution)/shard_map/ppermute | solution.py:20
  45.8 20.6 %collective-permute-start.3 = (bf16[512,512]{1,0:T(8,128)(2,1)S(1)}, bf16[512,512]{1,0:T(8,128)(2,1)S(1)}, u32[]{:S(2)}, u32[]{:S(2)}) collective-permute-start(bf16[512,512]{1,0:T(8,128)(2,1)S(1)} %get-tuple-element.14), channel_id=1, source_target_pairs={{2,0},{3,1},{4,2},{5,3},{6,4},{7,5},{8,6},{9,7},{10,8},{11,9},{12,... | collective-permute-start | bytes 1572872 | tf_op jit(solution)/shard_map/ppermute | solution.py:20
  48.8 5.5 %collective-permute-start.4 = (f32[512,16]{0,1:T(8,128)S(1)}, f32[512,16]{0,1:T(8,128)S(1)}, u32[]{:S(2)}, u32[]{:S(2)}) collective-permute-start(f32[512,16]{0,1:T(8,128)S(1)} %fusion.9), channel_id=1, source_target_pairs={{0,64},{32,96},{64,0},{96,32},{128,192},{160,224},{192,128},{224,1... | collective-permute-start | bytes 98312 | tf_op jit(solution)/shard_map/ppermute | solution.py:38
  54.3 7.5 %collective-permute-start.5 = (f32[512,16]{0,1:T(8,128)S(1)}, f32[512,16]{0,1:T(8,128)S(1)}, u32[]{:S(2)}, u32[]{:S(2)}) collective-permute-start(f32[512,16]{0,1:T(8,128)S(1)} %add.79), channel_id=1, source_target_pairs={{0,192},{32,224},{64,128},{96,160},{128,64},{160,96},{192,0},{224,... | collective-permute-start | bytes 98312 | tf_op jit(solution)/shard_map/ppermute | solution.py:38
  61.8 3.9 %collective-permute-start.6 = (f32[512,16]{0,1:T(8,128)S(1)}, f32[512,16]{0,1:T(8,128)S(1)}, u32[]{:S(2)}, u32[]{:S(2)}) collective-permute-start(f32[512,16]{0,1:T(8,128)S(1)} %add.80), channel_id=1, source_target_pairs={{0,32},{32,0},{64,96},{96,64},{128,160},{160,128},{192,224},{224,1... | collective-permute-start | bytes 98312 | tf_op jit(solution)/shard_map/ppermute | solution.py:38

commit v7 on v6

--- a/solution.py
+++ b/solution.py
@@ -45,7 +45,7 @@
 
 
 def attention_kernel(q_ref, k_ref, v_ref, do_ref, qdoc_ref, kdoc_ref, bias_ref,
-                     o_ref, dq_ref, dk_ref, dv_ref):
+                     o_ref, dq_ref, dk_ref, dv_ref, dk_acc, dv_acc):
     qb = pl.program_id(1)
     rows = q_ref.shape[0]
     span = rows + WIN
@@ -53,8 +53,8 @@
 
     @pl.when(qb == 0)
     def _():
-        dk_ref[...] = jnp.zeros_like(dk_ref)
-        dv_ref[...] = jnp.zeros_like(dv_ref)
+        dk_acc[...] = jnp.zeros_like(dk_acc)
+        dv_acc[...] = jnp.zeros_like(dv_acc)
 
     q = jnp.concatenate([q_ref[:, :HEAD_SIZE], q_ref[:, HEAD_SIZE:]], axis=0)
     do = jnp.concatenate([do_ref[:, :HEAD_SIZE], do_ref[:, HEAD_SIZE:]], axis=0)
@@ -78,16 +78,19 @@
                          preferred_element_type=jnp.float32)
     ds = (p * (dp - row_dot)).astype(jnp.bfloat16)
     dq = jnp.dot(ds, k, preferred_element_type=jnp.float32) * softmax_scale
-    dk = lax.dot_general(ds, q, (((0,), (0,)), ((), ())),
-                         preferred_element_type=jnp.float32) * softmax_scale
-    dv = lax.dot_general(p_low, do, (((0,), (0,)), ((), ())),
-                         preferred_element_type=jnp.float32)
+    dk = jnp.dot(q.T, ds, preferred_element_type=jnp.float32) * softmax_scale
+    dv = jnp.dot(do.T, p_low, preferred_element_type=jnp.float32)
     o_ref[:, :HEAD_SIZE] = o[:rows].astype(o_ref.dtype)
     o_ref[:, HEAD_SIZE:] = o[rows:].astype(o_ref.dtype)
     dq_ref[:, :HEAD_SIZE] = dq[:rows].astype(dq_ref.dtype)
     dq_ref[:, HEAD_SIZE:] = dq[rows:].astype(dq_ref.dtype)
-    dk_ref[pl.ds(key_first, span), :] += dk
-    dv_ref[pl.ds(key_first, span), :] += dv
+    dk_acc[:, pl.ds(key_first, span)] += dk
+    dv_acc[:, pl.ds(key_first, span)] += dv
+
+    @pl.when(qb == pl.num_programs(1) - 1)
+    def _():
+        dk_ref[...] = dk_acc[...].T
+        dv_ref[...] = dv_acc[...].T
 
 
 def fused_attention(queries, extended, output_gradient, qdoc, kdoc, rows=BLK):
@@ -122,6 +125,10 @@
             jax.ShapeDtypeStruct((tokens, query_cols), jnp.bfloat16),
             jax.ShapeDtypeStruct((ext_rows, joined_cols // 2), jnp.float32),
             jax.ShapeDtypeStruct((ext_rows, joined_cols // 2), jnp.float32),
+        ],
+        scratch_shapes=[
+            pltpu.VMEM((HEAD_SIZE, ext_rows), jnp.float32),
+            pltpu.VMEM((HEAD_SIZE, ext_rows), jnp.float32),
         ],
         compiler_params=pltpu.CompilerParams(
             dimension_semantics=("arbitrary", "arbitrary"),

time: 67.7 us -> 67.9 us (level)
  no operation moved by 1% of the time
where the time goes in v7:
time: 67.9 us; the launch traced here: 67.6 us
  starting transfers between devices  23.5 us (35%)
  waiting for transfers between devices  20.5 us (30%)
  Pallas kernels  15.7 us (23%)
  local copies, waits for them, and re-layouts  3.93 us (6%)
  other arithmetic  2.92 us (4%)
  between operations  0.85 us (1%)
    pallas_call x1, Pallas kernels, fused_attention(): pl.pallas_call(attention_kernel, grid=(groups, blocks), in_specs=[pl.Bloc...  15.7 us
    ppermute x4, waiting for transfers between devices, passed_along(): return lax.ppermute(block, axis, route)  13.7 us
    ppermute x4, starting transfers between devices, passed_along(): return lax.ppermute(block, axis, route)  13.5 us
    ppermute x3, starting transfers between devices, gathered_sum(): total = total + lax.ppermute(total, axis, route)  10 us
    ppermute x3, waiting for transfers between devices, gathered_sum(): total = total + lax.ppermute(total, axis, route)  6.83 us
  transfers between devices with their start and end apart: 7, of which 5 were waited for; matrix products, arithmetic and copies ran while one was open for 4% of the time, Pallas kernels for 0%

profile of v7, /device:TPU:24, one launch (start us, length us, event | category | flops | bytes accessed | tf_op | source)
XLA Modules:
  0.0 67.6 jit_solution(9026610394603362007)
XLA Ops:
  0.6 0.0 copy-start
  0.6 1.0 %constant_dynamic-update-slice_fusion.1 = bf16[512,512]{1,0:T(8,128)(2,1)S(1)} fusion(bf16[512,256]{1,0:T(8,128)(2,1)} %param.7), kind=kLoop, calls=%fused_computation.17 | loop fusion | bytes 524288
  1.6 1.0 %constant_dynamic-update-slice_fusion = bf16[512,512]{1,0:T(8,128)(2,1)S(1)} fusion(bf16[512,512]{1,0:T(8,128)(2,1)S(1)} %constant_dynamic-update-slice_fusion.1, bf16[512,256]{1,0:T(8,128)(2,1)} %param.8), kind=kLoop, calls=%fused_computation.16 | loop fusion | bytes 524288 | tf_op jit(solution)/shard_map/concatenate | solution.py:168
  2.6 1.9 %collective-permute-start.1 = (bf16[512,512]{1,0:T(8,128)(2,1)S(1)}, bf16[512,512]{1,0:T(8,128)(2,1)S(1)}, u32[]{:S(2)}, u32[]{:S(2)}) collective-permute-start(bf16[512,512]{1,0:T(8,128)(2,1)S(1)} %constant_dynamic-update-slice_fusion), channel_id=1, source_target_pairs={{0,1},{1,2},{2,3},{3,4},{4,5},{5,6},{6,7},{7,8},{8,9},{9,10},{10,1... | collective-permute-start | bytes 1572872 | tf_op jit(solution)/shard_map/ppermute | solution.py:20
  4.5 3.4 %collective-permute-start = (bf16[512,512]{1,0:T(8,128)(2,1)S(1)}, bf16[512,512]{1,0:T(8,128)(2,1)S(1)}, u32[]{:S(2)}, u32[]{:S(2)}) collective-permute-start(bf16[512,512]{1,0:T(8,128)(2,1)S(1)} %constant_dynamic-update-slice_fusion), channel_id=1, source_target_pairs={{0,2},{1,3},{2,4},{3,5},{4,6},{5,7},{6,8},{7,9},{8,10},{9,11},{10,... | collective-permute-start | bytes 1572872 | tf_op jit(solution)/shard_map/ppermute | solution.py:20
  8.0 0.7 %copy.14 = s32[32,1]{1,0:T(8,128)S(1)} copy(s32[32,1]{0,1:T(1,128)} %bitcast.5) | data formatting | bytes 256 | tf_op jit(solution)/shard_map/reshape.64
  8.7 0.1 reduce-window.8
  8.8 0.1 multiply_reduce_fusion
  8.9 0.1 convert_reduce_fusion
  9.0 0.1 convert_reduce_fusion.1
  9.1 0.1 copy.15
  9.3 0.3 fusion.3.bias_ref
  9.7 0.0 copy-start.1
  9.7 0.0 copy-start.2
  9.7 8.6 %collective-permute-done.1 = bf16[512,512]{1,0:T(8,128)(2,1)S(1)} collective-permute-done((bf16[512,512]{1,0:T(8,128)(2,1)S(1)}, bf16[512,512]{1,0:T(8,128)(2,1)S(1)}, u32[]{:S(2)}, u32[]{:S(2)}) %collective-permute-start.1) | collective-permute-done | bytes 524320 | tf_op jit(solution)/shard_map/ppermute | solution.py:20
  18.3 5.0 %collective-permute-done = bf16[512,512]{1,0:T(8,128)(2,1)S(1)} collective-permute-done((bf16[512,512]{1,0:T(8,128)(2,1)S(1)}, bf16[512,512]{1,0:T(8,128)(2,1)S(1)}, u32[]{:S(2)}, u32[]{:S(2)}) %collective-permute-start) | collective-permute-done | bytes 524320 | tf_op jit(solution)/shard_map/ppermute | solution.py:20
  23.3 1.3 %pad_maximum_fusion.k_ref.v_ref = bf16[1536,512]{1,0:T(8,128)(2,1)} fusion(bf16[512,512]{1,0:T(8,128)(2,1)S(1)} %constant_dynamic-update-slice_fusion, bf16[512,512]{1,0:T(8,128)(2,1)S(1)} %collective-permute-done.1, bf16[512,512]{1,0:T(8,128)(2,1)S(1)} %collective-permute-done), kind=kLoop, calls=%fused_computation.1 | loop fusion | flops 4718592 | bytes 3145728 | tf_op jit(solution)/shard_map/concatenate | solution.py:172
  24.6 0.0 copy-done.1
  24.6 0.0 copy-done.2
  24.6 15.7 %shard_map.101 = (bf16[512,512]{1,0:T(8,128)(2,1)}, bf16[512,512]{1,0:T(8,128)(2,1)}, f32[1536,256]{1,0:T(8,128)S(1)}, f32[1536,256]{1,0:T(8,128)S(1)}) custom-call(bf16[512,512]{1,0:T(8,128)(2,1)S(1)} %copy-done.1, bf16[1536,512]{1,0:T(8,128)(2,1)} %pad_maximum_fusion.k_ref.v_ref, bf16[1536,512]{1,0:T(8,128)(2,1)} %pad_maximum_fusion.k_ref.v_ref, ...), custom_call_target="tpu_custom_call" | custom-call | flops 3623878656 | bytes 6815744 | tf_op jit(solution)/shard_map/pallas_call | solution.py:105
  40.3 0.1 slice.30
  40.4 0.1 slice.31
  40.4 0.1 maximum_convert_fusion
  40.5 0.0 copy-start.3
  40.5 0.1 fusion.7
  40.6 5.4 %collective-permute-start.2 = (bf16[512,512]{1,0:T(8,128)(2,1)S(1)}, bf16[512,512]{1,0:T(8,128)(2,1)S(1)}, u32[]{:S(2)}, u32[]{:S(2)}) collective-permute-start(bf16[512,512]{1,0:T(8,128)(2,1)S(1)} %get-tuple-element.13), channel_id=1, source_target_pairs={{1,0},{2,1},{3,2},{4,3},{5,4},{6,5},{7,6},{8,7},{9,8},{10,9},{11,1... | collective-permute-start | bytes 1572872 | tf_op jit(solution)/shard_map/ppermute | solution.py:20
  46.1 2.7 %collective-permute-start.3 = (bf16[512,512]{1,0:T(8,128)(2,1)S(1)}, bf16[512,512]{1,0:T(8,128)(2,1)S(1)}, u32[]{:S(2)}, u32[]{:S(2)}) collective-permute-start(bf16[512,512]{1,0:T(8,128)(2,1)S(1)} %get-tuple-element.14), channel_id=1, source_target_pairs={{2,0},{3,1},{4,2},{5,3},{6,4},{7,5},{8,6},{9,7},{10,8},{11,9},{12,... | collective-permute-start | bytes 1572872 | tf_op jit(solution)/shard_map/ppermute | solution.py:20
  48.8 0.0 copy-done
  48.8 0.0 copy-done.3
  48.8 0.2 fusion.9
  49.1 3.3 %collective-permute-start.4 = (f32[512,16]{0,1:T(8,128)S(1)}, f32[512,16]{0,1:T(8,128)S(1)}, u32[]{:S(2)}, u32[]{:S(2)}) collective-permute-start(f32[512,16]{0,1:T(8,128)S(1)} %fusion.9), channel_id=1, source_target_pairs={{0,64},{32,96},{64,0},{96,32},{128,192},{160,224},{192,128},{224,1... | collective-permute-start | bytes 98312 | tf_op jit(solution)/shard_map/ppermute | solution.py:38
  52.4 2.2 %collective-permute-done.4 = f32[512,16]{0,1:T(8,128)S(1)} collective-permute-done((f32[512,16]{0,1:T(8,128)S(1)}, f32[512,16]{0,1:T(8,128)S(1)}, u32[]{:S(2)}, u32[]{:S(2)}) %collective-permute-start.4) | collective-permute-done | bytes 32800 | tf_op jit(solution)/shard_map/ppermute | solution.py:38
  54.5 5.6 %collective-permute-start.5 = (f32[512,16]{0,1:T(8,128)S(1)}, f32[512,16]{0,1:T(8,128)S(1)}, u32[]{:S(2)}, u32[]{:S(2)}) collective-permute-start(f32[512,16]{0,1:T(8,128)S(1)} %add.79), channel_id=1, source_target_pairs={{0,192},{32,224},{64,128},{96,160},{128,64},{160,96},{192,0},{224,... | collective-permute-start | bytes 98312 | tf_op jit(solution)/shard_map/ppermute | solution.py:38
  60.2 1.9 %collective-permute-done.5 = f32[512,16]{0,1:T(8,128)S(1)} collective-permute-done((f32[512,16]{0,1:T(8,128)S(1)}, f32[512,16]{0,1:T(8,128)S(1)}, u32[]{:S(2)}, u32[]{:S(2)}) %collective-permute-start.5) | collective-permute-done | bytes 32800 | tf_op jit(solution)/shard_map/ppermute | solution.py:38
  62.1 1.1 %collective-permute-start.6 = (f32[512,16]{0,1:T(8,128)S(1)}, f32[512,16]{0,1:T(8,128)S(1)}, u32[]{:S(2)}, u32[]{:S(2)}) collective-permute-start(f32[512,16]{0,1:T(8,128)S(1)} %add.80), channel_id=1, source_target_pairs={{0,32},{32,0},{64,96},{96,64},{128,160},{160,128},{192,224},{224,1... | collective-permute-start | bytes 98312 | tf_op jit(solution)/shard_map/ppermute | solution.py:38
  63.2 2.8 %collective-permute-done.6 = f32[512,16]{0,1:T(8,128)S(1)} collective-permute-done((f32[512,16]{0,1:T(8,128)S(1)}, f32[512,16]{0,1:T(8,128)S(1)}, u32[]{:S(2)}, u32[]{:S(2)}) %collective-permute-start.6) | collective-permute-done | bytes 32800 | tf_op jit(solution)/shard_map/ppermute | solution.py:38
  66.0 0.6 add.81
  66.6 0.0 collective-permute-done.2
  66.6 0.0 collective-permute-done.3
  66.6 0.2 fusion.4
  66.8 0.8 %fusion.8 = (bf16[512,256]{1,0:T(8,128)(2,1)}, bf16[512,256]{1,0:T(8,128)(2,1)}) fusion(bf16[512,512]{1,0:T(8,128)(2,1)S(1)} %fusion.4), kind=kLoop, calls=%fused_computation.23 | loop fusion | bytes 1048576 | tf_op jit(solution)/shard_map/slice | solution.py:191
  (10 shorter events, 0.2 us)
Async XLA Ops:
  0.6 48.2 %copy-start = (bf16[16,512]{1,0:T(8,128)(2,1)S(1)}, bf16[16,512]{1,0:T(8,128)(2,1)}, u32[]{:S(2)}) copy-start(bf16[16,512]{1,0:T(8,128)(2,1)} %param.10) | copy-start | bytes 49156
  2.6 15.7 %collective-permute-start.1 = (bf16[512,512]{1,0:T(8,128)(2,1)S(1)}, bf16[512,512]{1,0:T(8,128)(2,1)S(1)}, u32[]{:S(2)}, u32[]{:S(2)}) collective-permute-start(bf16[512,512]{1,0:T(8,128)(2,1)S(1)} %constant_dynamic-update-slice_fusion), channel_id=1, source_target_pairs={{0,1},{1,2},{2,3},{3,4},{4,5},{5,6},{6,7},{7,8},{8,9},{9,10},{10,1... | collective-permute-start | bytes 1572872 | tf_op jit(solution)/shard_map/ppermute | solution.py:20
  4.5 18.8 %collective-permute-start = (bf16[512,512]{1,0:T(8,128)(2,1)S(1)}, bf16[512,512]{1,0:T(8,128)(2,1)S(1)}, u32[]{:S(2)}, u32[]{:S(2)}) collective-permute-start(bf16[512,512]{1,0:T(8,128)(2,1)S(1)} %constant_dynamic-update-slice_fusion), channel_id=1, source_target_pairs={{0,2},{1,3},{2,4},{3,5},{4,6},{5,7},{6,8},{7,9},{8,10},{9,11},{10,... | collective-permute-start | bytes 1572872 | tf_op jit(solution)/shard_map/ppermute | solution.py:20
  9.7 14.9 %copy-start.1 = (bf16[512,512]{1,0:T(8,128)(2,1)S(1)}, bf16[512,512]{1,0:T(8,128)(2,1)}, u32[]{:S(2)}) copy-start(bf16[512,512]{1,0:T(8,128)(2,1)} %q_ref.1) | copy-start | bytes 1572868
  9.7 14.9 %copy-start.2 = (bf16[512,512]{1,0:T(8,128)(2,1)S(1)}, bf16[512,512]{1,0:T(8,128)(2,1)}, u32[]{:S(2)}) copy-start(bf16[512,512]{1,0:T(8,128)(2,1)} %do_ref.1) | copy-start | bytes 1572868
  40.5 8.3 %copy-start.3 = (bf16[512,512]{1,0:T(8,128)(2,1)S(1)}, bf16[512,512]{1,0:T(8,128)(2,1)}, u32[]{:S(2)}) copy-start(bf16[512,512]{1,0:T(8,128)(2,1)} %get-tuple-element.5) | copy-start | bytes 1572868
  40.6 26.0 %collective-permute-start.2 = (bf16[512,512]{1,0:T(8,128)(2,1)S(1)}, bf16[512,512]{1,0:T(8,128)(2,1)S(1)}, u32[]{:S(2)}, u32[]{:S(2)}) collective-permute-start(bf16[512,512]{1,0:T(8,128)(2,1)S(1)} %get-tuple-element.13), channel_id=1, source_target_pairs={{1,0},{2,1},{3,2},{4,3},{5,4},{6,5},{7,6},{8,7},{9,8},{10,9},{11,1... | collective-permute-start | bytes 1572872 | tf_op jit(solution)/shard_map/ppermute | solution.py:20
  46.1 20.6 %collective-permute-start.3 = (bf16[512,512]{1,0:T(8,128)(2,1)S(1)}, bf16[512,512]{1,0:T(8,128)(2,1)S(1)}, u32[]{:S(2)}, u32[]{:S(2)}) collective-permute-start(bf16[512,512]{1,0:T(8,128)(2,1)S(1)} %get-tuple-element.14), channel_id=1, source_target_pairs={{2,0},{3,1},{4,2},{5,3},{6,4},{7,5},{8,6},{9,7},{10,8},{11,9},{12,... | collective-permute-start | bytes 1572872 | tf_op jit(solution)/shard_map/ppermute | solution.py:20
  49.1 5.5 %collective-permute-start.4 = (f32[512,16]{0,1:T(8,128)S(1)}, f32[512,16]{0,1:T(8,128)S(1)}, u32[]{:S(2)}, u32[]{:S(2)}) collective-permute-start(f32[512,16]{0,1:T(8,128)S(1)} %fusion.9), channel_id=1, source_target_pairs={{0,64},{32,96},{64,0},{96,32},{128,192},{160,224},{192,128},{224,1... | collective-permute-start | bytes 98312 | tf_op jit(solution)/shard_map/ppermute | solution.py:38
  54.5 7.5 %collective-permute-start.5 = (f32[512,16]{0,1:T(8,128)S(1)}, f32[512,16]{0,1:T(8,128)S(1)}, u32[]{:S(2)}, u32[]{:S(2)}) collective-permute-start(f32[512,16]{0,1:T(8,128)S(1)} %add.79), channel_id=1, source_target_pairs={{0,192},{32,224},{64,128},{96,160},{128,64},{160,96},{192,0},{224,... | collective-permute-start | bytes 98312 | tf_op jit(solution)/shard_map/ppermute | solution.py:38
  62.1 3.9 %collective-permute-start.6 = (f32[512,16]{0,1:T(8,128)S(1)}, f32[512,16]{0,1:T(8,128)S(1)}, u32[]{:S(2)}, u32[]{:S(2)}) collective-permute-start(f32[512,16]{0,1:T(8,128)S(1)} %add.80), channel_id=1, source_target_pairs={{0,32},{32,0},{64,96},{96,64},{128,160},{160,128},{192,224},{224,1... | collective-permute-start | bytes 98312 | tf_op jit(solution)/shard_map/ppermute | solution.py:38

commit v8 on v7

--- a/solution.py
+++ b/solution.py
@@ -93,7 +93,7 @@
         dv_ref[...] = dv_acc[...].T
 
 
-def fused_attention(queries, extended, output_gradient, qdoc, kdoc, rows=BLK):
+def fused_attention(queries, extended, output_gradient, qdoc, kdoc, rows=2 * BLK):
     tokens, query_cols = queries.shape
     ext_rows, joined_cols = extended.shape
     groups = joined_cols // (2 * HEAD_SIZE)

time: 67.9 us -> 66.2 us (0.975)
  waiting for transfers between devices: 20.5 us -> 18.7 us
    select_n x1, other arithmetic: 0.32 us -> 2.13 us  [window_bias(): return jnp.where(inside, 0.0, masked_value).astype(jnp.float32)]
    ppermute x4, waiting for transfers between devices: 13.7 us -> 11.8 us  [passed_along(): return lax.ppermute(block, axis, route)]
    concatenate x1, other arithmetic: 1.27 us -> 0.1 us  [body(): extended = jnp.concatenate(arrived[::-1] + [joined], axis=0)]
  transfers between devices with their start and end apart: 7 -> 7, of which waited for: 5 -> 5; matrix products, arithmetic and copies ran while one was open for 4% -> 7% of each run, Pallas kernels for 0% -> 0%
where the time goes in v8:
time: 66.2 us; the launch traced here: 65.9 us
  starting transfers between devices  23.3 us (35%)
  waiting for transfers between devices  18.7 us (28%)
  Pallas kernels  15.3 us (23%)
  local copies, waits for them, and re-layouts  3.93 us (6%)
  other arithmetic  3.57 us (5%)
  between operations  0.86 us (1%)
    pallas_call x1, Pallas kernels, fused_attention(): pl.pallas_call(attention_kernel, grid=(groups, blocks), in_specs=[pl.Bloc...  15.3 us
    ppermute x4, starting transfers between devices, passed_along(): return lax.ppermute(block, axis, route)  13.3 us
    ppermute x4, waiting for transfers between devices, passed_along(): return lax.ppermute(block, axis, route)  11.8 us
    ppermute x3, starting transfers between devices, gathered_sum(): total = total + lax.ppermute(total, axis, route)  9.96 us
    ppermute x3, waiting for transfers between devices, gathered_sum(): total = total + lax.ppermute(total, axis, route)  6.9 us
    select_n x1, other arithmetic, window_bias(): return jnp.where(inside, 0.0, masked_value).astype(jnp.float32)  2.13 us
  transfers between devices with their start and end apart: 7, of which 5 were waited for; matrix products, arithmetic and copies ran while one was open for 7% of the time, Pallas kernels for 0%

profile of v8, /device:TPU:24, one launch (start us, length us, event | category | flops | bytes accessed | tf_op | source)
XLA Modules:
  0.0 65.9 jit_solution(3793954306614697418)
XLA Ops:
  0.6 0.0 copy-start
  0.6 1.0 %constant_dynamic-update-slice_fusion.1 = bf16[512,512]{1,0:T(8,128)(2,1)S(1)} fusion(bf16[512,256]{1,0:T(8,128)(2,1)} %param.7), kind=kLoop, calls=%fused_computation.17 | loop fusion | bytes 524288
  1.6 1.0 %constant_dynamic-update-slice_fusion = bf16[512,512]{1,0:T(8,128)(2,1)S(1)} fusion(bf16[512,512]{1,0:T(8,128)(2,1)S(1)} %constant_dynamic-update-slice_fusion.1, bf16[512,256]{1,0:T(8,128)(2,1)} %param.8), kind=kLoop, calls=%fused_computation.16 | loop fusion | bytes 524288 | tf_op jit(solution)/shard_map/concatenate | solution.py:168
  2.6 1.9 %collective-permute-start.1 = (bf16[512,512]{1,0:T(8,128)(2,1)S(1)}, bf16[512,512]{1,0:T(8,128)(2,1)S(1)}, u32[]{:S(2)}, u32[]{:S(2)}) collective-permute-start(bf16[512,512]{1,0:T(8,128)(2,1)S(1)} %constant_dynamic-update-slice_fusion), channel_id=1, source_target_pairs={{0,1},{1,2},{2,3},{3,4},{4,5},{5,6},{6,7},{7,8},{8,9},{9,10},{10,1... | collective-permute-start | bytes 1572872 | tf_op jit(solution)/shard_map/ppermute | solution.py:20
  4.5 3.4 %collective-permute-start = (bf16[512,512]{1,0:T(8,128)(2,1)S(1)}, bf16[512,512]{1,0:T(8,128)(2,1)S(1)}, u32[]{:S(2)}, u32[]{:S(2)}) collective-permute-start(bf16[512,512]{1,0:T(8,128)(2,1)S(1)} %constant_dynamic-update-slice_fusion), channel_id=1, source_target_pairs={{0,2},{1,3},{2,4},{3,5},{4,6},{5,7},{6,8},{7,9},{8,10},{9,11},{10,... | collective-permute-start | bytes 1572872 | tf_op jit(solution)/shard_map/ppermute | solution.py:20
  8.0 0.7 %copy.14 = s32[32,1]{1,0:T(8,128)S(1)} copy(s32[32,1]{0,1:T(1,128)} %bitcast.5) | data formatting | bytes 256 | tf_op jit(solution)/shard_map/reshape.64
  8.7 0.1 reduce-window.8
  8.8 0.1 multiply_reduce_fusion
  8.9 0.1 convert_reduce_fusion
  9.0 0.1 convert_reduce_fusion.1
  9.1 0.1 copy.15
  9.3 0.0 copy-start.1
  9.3 0.0 copy-start.2
  9.3 2.1 %fusion.3.bias_ref = f32[512,1280]{1,0:T(8,128)} fusion(s32[512]{0:T(512)S(1)} %get-tuple-element.17, s32[512]{0:T(512)S(1)} %get-tuple-element.18, pred[512]{0:T(512)(128)(4,1)S(1)} %fusion.9), kind=kLoop, calls=%fused_computation.4 | loop fusion | flops 4587520 | bytes 2626048 | tf_op jit(solution)/shard_map/jit(_where)/select_n | solution.py:149
  11.5 6.8 %collective-permute-done.1 = bf16[512,512]{1,0:T(8,128)(2,1)S(1)} collective-permute-done((bf16[512,512]{1,0:T(8,128)(2,1)S(1)}, bf16[512,512]{1,0:T(8,128)(2,1)S(1)}, u32[]{:S(2)}, u32[]{:S(2)}) %collective-permute-start.1) | collective-permute-done | bytes 524320 | tf_op jit(solution)/shard_map/ppermute | solution.py:20
  18.3 5.0 %collective-permute-done = bf16[512,512]{1,0:T(8,128)(2,1)S(1)} collective-permute-done((bf16[512,512]{1,0:T(8,128)(2,1)S(1)}, bf16[512,512]{1,0:T(8,128)(2,1)S(1)}, u32[]{:S(2)}, u32[]{:S(2)}) %collective-permute-start) | collective-permute-done | bytes 524320 | tf_op jit(solution)/shard_map/ppermute | solution.py:20
  23.3 0.1 pad_maximum_fusion.k_ref.v_ref
  23.4 0.0 copy-done.1
  23.4 0.0 copy-done.2
  23.5 15.3 %shard_map.101 = (bf16[512,512]{1,0:T(8,128)(2,1)}, bf16[512,512]{1,0:T(8,128)(2,1)}, f32[1536,256]{1,0:T(8,128)S(1)}, f32[1536,256]{1,0:T(8,128)S(1)}) custom-call(bf16[512,512]{1,0:T(8,128)(2,1)S(1)} %copy-done.1, bf16[1536,512]{1,0:T(8,128)(2,1)S(1)} %pad_maximum_fusion.k_ref.v_ref, bf16[1536,512]{1,0:T(8,128)(2,1)S(1)} %pad_maximum_fusion.k_ref.v_ref, ...), custom_call_target="tpu_custom_call" | custom-call | flops 4026531840 | bytes 6815744 | tf_op jit(solution)/shard_map/pallas_call | solution.py:105
  38.7 0.1 slice.30
  38.8 0.0 copy-start.3
  38.8 0.1 slice.31
  38.8 0.1 maximum_convert_fusion
  38.9 0.1 fusion.10
  39.0 5.3 %collective-permute-start.2 = (bf16[512,512]{1,0:T(8,128)(2,1)S(1)}, bf16[512,512]{1,0:T(8,128)(2,1)S(1)}, u32[]{:S(2)}, u32[]{:S(2)}) collective-permute-start(bf16[512,512]{1,0:T(8,128)(2,1)S(1)} %get-tuple-element.13), channel_id=1, source_target_pairs={{1,0},{2,1},{3,2},{4,3},{5,4},{6,5},{7,6},{8,7},{9,8},{10,9},{11,1... | collective-permute-start | bytes 1572872 | tf_op jit(solution)/shard_map/ppermute | solution.py:20
  44.3 2.7 %collective-permute-start.3 = (bf16[512,512]{1,0:T(8,128)(2,1)S(1)}, bf16[512,512]{1,0:T(8,128)(2,1)S(1)}, u32[]{:S(2)}, u32[]{:S(2)}) collective-permute-start(bf16[512,512]{1,0:T(8,128)(2,1)S(1)} %get-tuple-element.14), channel_id=1, source_target_pairs={{2,0},{3,1},{4,2},{5,3},{6,4},{7,5},{8,6},{9,7},{10,8},{11,9},{12,... | collective-permute-start | bytes 1572872 | tf_op jit(solution)/shard_map/ppermute | solution.py:20
  47.0 0.0 copy-done
  47.0 0.0 copy-done.3
  47.0 0.2 fusion.12
  47.3 3.3 %collective-permute-start.4 = (f32[512,16]{0,1:T(8,128)S(1)}, f32[512,16]{0,1:T(8,128)S(1)}, u32[]{:S(2)}, u32[]{:S(2)}) collective-permute-start(f32[512,16]{0,1:T(8,128)S(1)} %fusion.12), channel_id=1, source_target_pairs={{0,64},{32,96},{64,0},{96,32},{128,192},{160,224},{192,128},{224,1... | collective-permute-start | bytes 98312 | tf_op jit(solution)/shard_map/ppermute | solution.py:38
  50.6 2.2 %collective-permute-done.4 = f32[512,16]{0,1:T(8,128)S(1)} collective-permute-done((f32[512,16]{0,1:T(8,128)S(1)}, f32[512,16]{0,1:T(8,128)S(1)}, u32[]{:S(2)}, u32[]{:S(2)}) %collective-permute-start.4) | collective-permute-done | bytes 32800 | tf_op jit(solution)/shard_map/ppermute | solution.py:38
  52.8 5.6 %collective-permute-start.5 = (f32[512,16]{0,1:T(8,128)S(1)}, f32[512,16]{0,1:T(8,128)S(1)}, u32[]{:S(2)}, u32[]{:S(2)}) collective-permute-start(f32[512,16]{0,1:T(8,128)S(1)} %add.79), channel_id=1, source_target_pairs={{0,192},{32,224},{64,128},{96,160},{128,64},{160,96},{192,0},{224,... | collective-permute-start | bytes 98312 | tf_op jit(solution)/shard_map/ppermute | solution.py:38
  58.4 1.9 %collective-permute-done.5 = f32[512,16]{0,1:T(8,128)S(1)} collective-permute-done((f32[512,16]{0,1:T(8,128)S(1)}, f32[512,16]{0,1:T(8,128)S(1)}, u32[]{:S(2)}, u32[]{:S(2)}) %collective-permute-start.5) | collective-permute-done | bytes 32800 | tf_op jit(solution)/shard_map/ppermute | solution.py:38
  60.3 1.0 %collective-permute-start.6 = (f32[512,16]{0,1:T(8,128)S(1)}, f32[512,16]{0,1:T(8,128)S(1)}, u32[]{:S(2)}, u32[]{:S(2)}) collective-permute-start(f32[512,16]{0,1:T(8,128)S(1)} %add.80), channel_id=1, source_target_pairs={{0,32},{32,0},{64,96},{96,64},{128,160},{160,128},{192,224},{224,1... | collective-permute-start | bytes 98312 | tf_op jit(solution)/shard_map/ppermute | solution.py:38
  61.4 2.8 %collective-permute-done.6 = f32[512,16]{0,1:T(8,128)S(1)} collective-permute-done((f32[512,16]{0,1:T(8,128)S(1)}, f32[512,16]{0,1:T(8,128)S(1)}, u32[]{:S(2)}, u32[]{:S(2)}) %collective-permute-start.6) | collective-permute-done | bytes 32800 | tf_op jit(solution)/shard_map/ppermute | solution.py:38
  64.2 0.6 add.81
  64.9 0.0 collective-permute-done.2
  64.9 0.0 collective-permute-done.3
  64.9 0.2 fusion.4
  65.1 0.8 %fusion.11 = (bf16[512,256]{1,0:T(8,128)(2,1)}, bf16[512,256]{1,0:T(8,128)(2,1)}) fusion(bf16[512,512]{1,0:T(8,128)(2,1)S(1)} %fusion.4), kind=kLoop, calls=%fused_computation.25 | loop fusion | bytes 1048576 | tf_op jit(solution)/shard_map/slice | solution.py:191
  (10 shorter events, 0.2 us)
Async XLA Ops:
  0.6 46.4 %copy-start = (bf16[16,512]{1,0:T(8,128)(2,1)S(1)}, bf16[16,512]{1,0:T(8,128)(2,1)}, u32[]{:S(2)}) copy-start(bf16[16,512]{1,0:T(8,128)(2,1)} %param.10) | copy-start | bytes 49156
  2.6 15.7 %collective-permute-start.1 = (bf16[512,512]{1,0:T(8,128)(2,1)S(1)}, bf16[512,512]{1,0:T(8,128)(2,1)S(1)}, u32[]{:S(2)}, u32[]{:S(2)}) collective-permute-start(bf16[512,512]{1,0:T(8,128)(2,1)S(1)} %constant_dynamic-update-slice_fusion), channel_id=1, source_target_pairs={{0,1},{1,2},{2,3},{3,4},{4,5},{5,6},{6,7},{7,8},{8,9},{9,10},{10,1... | collective-permute-start | bytes 1572872 | tf_op jit(solution)/shard_map/ppermute | solution.py:20
  4.5 18.8 %collective-permute-start = (bf16[512,512]{1,0:T(8,128)(2,1)S(1)}, bf16[512,512]{1,0:T(8,128)(2,1)S(1)}, u32[]{:S(2)}, u32[]{:S(2)}) collective-permute-start(bf16[512,512]{1,0:T(8,128)(2,1)S(1)} %constant_dynamic-update-slice_fusion), channel_id=1, source_target_pairs={{0,2},{1,3},{2,4},{3,5},{4,6},{5,7},{6,8},{7,9},{8,10},{9,11},{10,... | collective-permute-start | bytes 1572872 | tf_op jit(solution)/shard_map/ppermute | solution.py:20
  9.3 14.1 %copy-start.1 = (bf16[512,512]{1,0:T(8,128)(2,1)S(1)}, bf16[512,512]{1,0:T(8,128)(2,1)}, u32[]{:S(2)}) copy-start(bf16[512,512]{1,0:T(8,128)(2,1)} %q_ref.1) | copy-start | bytes 1572868
  9.3 14.1 %copy-start.2 = (bf16[512,512]{1,0:T(8,128)(2,1)S(1)}, bf16[512,512]{1,0:T(8,128)(2,1)}, u32[]{:S(2)}) copy-start(bf16[512,512]{1,0:T(8,128)(2,1)} %do_ref.1) | copy-start | bytes 1572868
  38.8 8.3 %copy-start.3 = (bf16[512,512]{1,0:T(8,128)(2,1)S(1)}, bf16[512,512]{1,0:T(8,128)(2,1)}, u32[]{:S(2)}) copy-start(bf16[512,512]{1,0:T(8,128)(2,1)} %get-tuple-element.5) | copy-start | bytes 1572868
  39.0 25.9 %collective-permute-start.2 = (bf16[512,512]{1,0:T(8,128)(2,1)S(1)}, bf16[512,512]{1,0:T(8,128)(2,1)S(1)}, u32[]{:S(2)}, u32[]{:S(2)}) collective-permute-start(bf16[512,512]{1,0:T(8,128)(2,1)S(1)} %get-tuple-element.13), channel_id=1, source_target_pairs={{1,0},{2,1},{3,2},{4,3},{5,4},{6,5},{7,6},{8,7},{9,8},{10,9},{11,1... | collective-permute-start | bytes 1572872 | tf_op jit(solution)/shard_map/ppermute | solution.py:20
  44.3 20.6 %collective-permute-start.3 = (bf16[512,512]{1,0:T(8,128)(2,1)S(1)}, bf16[512,512]{1,0:T(8,128)(2,1)S(1)}, u32[]{:S(2)}, u32[]{:S(2)}) collective-permute-start(bf16[512,512]{1,0:T(8,128)(2,1)S(1)} %get-tuple-element.14), channel_id=1, source_target_pairs={{2,0},{3,1},{4,2},{5,3},{6,4},{7,5},{8,6},{9,7},{10,8},{11,9},{12,... | collective-permute-start | bytes 1572872 | tf_op jit(solution)/shard_map/ppermute | solution.py:20
  47.3 5.5 %collective-permute-start.4 = (f32[512,16]{0,1:T(8,128)S(1)}, f32[512,16]{0,1:T(8,128)S(1)}, u32[]{:S(2)}, u32[]{:S(2)}) collective-permute-start(f32[512,16]{0,1:T(8,128)S(1)} %fusion.12), channel_id=1, source_target_pairs={{0,64},{32,96},{64,0},{96,32},{128,192},{160,224},{192,128},{224,1... | collective-permute-start | bytes 98312 | tf_op jit(solution)/shard_map/ppermute | solution.py:38
  52.8 7.5 %collective-permute-start.5 = (f32[512,16]{0,1:T(8,128)S(1)}, f32[512,16]{0,1:T(8,128)S(1)}, u32[]{:S(2)}, u32[]{:S(2)}) collective-permute-start(f32[512,16]{0,1:T(8,128)S(1)} %add.79), channel_id=1, source_target_pairs={{0,192},{32,224},{64,128},{96,160},{128,64},{160,96},{192,0},{224,... | collective-permute-start | bytes 98312 | tf_op jit(solution)/shard_map/ppermute | solution.py:38
  60.3 3.9 %collective-permute-start.6 = (f32[512,16]{0,1:T(8,128)S(1)}, f32[512,16]{0,1:T(8,128)S(1)}, u32[]{:S(2)}, u32[]{:S(2)}) collective-permute-start(f32[512,16]{0,1:T(8,128)S(1)} %add.80), channel_id=1, source_target_pairs={{0,32},{32,0},{64,96},{96,64},{128,160},{160,128},{192,224},{224,1... | collective-permute-start | bytes 98312 | tf_op jit(solution)/shard_map/ppermute | solution.py:38

commit v9 on v8

--- a/solution.py
+++ b/solution.py
@@ -149,6 +149,22 @@
     return jnp.where(inside, 0.0, masked_value).astype(jnp.float32)
 
 
+def join_kernel(k_ref, v_ref, o_ref):
+    cols = k_ref.shape[1]
+    o_ref[:, :cols] = k_ref[...]
+    o_ref[:, cols:] = v_ref[...]
+
+
+def joined_columns(keys, values):
+    rows, cols = keys.shape
+    return pl.pallas_call(
+        join_kernel,
+        out_shape=jax.ShapeDtypeStruct((rows, 2 * cols), keys.dtype),
+        cost_estimate=pl.CostEstimate(
+            flops=0, transcendentals=0, bytes_accessed=4 * rows * cols * keys.dtype.itemsize),
+    )(keys, values)
+
+
 def body(
     queries,
     key_head_tensor,
@@ -165,7 +181,7 @@
     first_pos = lax.axis_index("ctx") * tokens_here
     lowest = first_pos - WIN
     doc_ends = jnp.cumsum(document_block_counts) * BLK
-    joined = jnp.concatenate([key_head_tensor, value_head_tensor], axis=1)
+    joined = joined_columns(key_head_tensor, value_head_tensor)
     arrived = []
     for hop_num in range(hop_count):
         arrived.append(passed_along(joined, "ctx", hop_num + 1))

time: 66.2 us -> 66.4 us (level)
  local copies, waits for them, and re-layouts: 3.93 us -> 1.99 us
  Pallas kernels: 15.3 us -> 17.1 us
    pallas_call x0 -> x1, Pallas kernels: none -> 1.87 us  [joined_columns(): pl.pallas_call(join_kernel, out_shape=jax.ShapeDtypeStruct((rows, 2 * col...]
    unnamed x9 -> x10, local copies, waits for them, and re-layouts: 1 us -> 0.03 us
    concatenate x1 -> x0, local copies, waits for them, and re-layouts: 0.97 us -> none  [body(): joined = jnp.concatenate([key_head_tensor, value_head_tensor], axis=1)]
where the time goes in v9:
time: 66.4 us; the launch traced here: 66.1 us
  starting transfers between devices  23.4 us (35%)
  waiting for transfers between devices  19 us (29%)
  Pallas kernels  17.1 us (26%)
  other arithmetic  3.57 us (5%)
  local copies, waits for them, and re-layouts  1.99 us (3%)
  between operations  0.85 us (1%)
    pallas_call x1, Pallas kernels, fused_attention(): pl.pallas_call(attention_kernel, grid=(groups, blocks), in_specs=[pl.Bloc...  15.3 us
    ppermute x4, starting transfers between devices, passed_along(): return lax.ppermute(block, axis, route)  13.5 us
    ppermute x4, waiting for transfers between devices, passed_along(): return lax.ppermute(block, axis, route)  12.1 us
    ppermute x3, starting transfers between devices, gathered_sum(): total = total + lax.ppermute(total, axis, route)  9.96 us
    ppermute x3, waiting for transfers between devices, gathered_sum(): total = total + lax.ppermute(total, axis, route)  6.89 us
    select_n x1, other arithmetic, window_bias(): return jnp.where(inside, 0.0, masked_value).astype(jnp.float32)  2.13 us
    pallas_call x1, Pallas kernels, joined_columns(): pl.pallas_call(join_kernel, out_shape=jax.ShapeDtypeStruct((rows, 2 * col...  1.87 us
  transfers between devices with their start and end apart: 7, of which 5 were waited for; matrix products, arithmetic and copies ran while one was open for 7% of the time, Pallas kernels for 0%

profile of v9, /device:TPU:24, one launch (start us, length us, event | category | flops | bytes accessed | tf_op | source)
XLA Modules:
  0.0 66.1 jit_solution(668056229260044729)
XLA Ops:
  0.6 0.0 copy-start
  0.6 1.9 %shard_map.101 = bf16[512,512]{1,0:T(8,128)(2,1)} custom-call(bf16[512,256]{1,0:T(8,128)(2,1)} %k_ref.1, bf16[512,256]{1,0:T(8,128)(2,1)} %v_ref.1), custom_call_target="tpu_custom_call" | custom-call | bytes 1048576 | tf_op jit(solution)/shard_map/pallas_call | solution.py:160
  2.5 0.0 copy-start.3
  2.5 2.0 %collective-permute-start.1 = (bf16[512,512]{1,0:T(8,128)(2,1)}, bf16[512,512]{1,0:T(8,128)(2,1)S(1)}, u32[]{:S(2)}, u32[]{:S(2)}) collective-permute-start(bf16[512,512]{1,0:T(8,128)(2,1)} %shard_map.101), channel_id=1, source_target_pairs={{0,1},{1,2},{2,3},{3,4},{4,5},{5,6},{6,7},{7,8},{8,9},{9,10},{10,1... | collective-permute-start | bytes 1572872 | tf_op jit(solution)/shard_map/ppermute | solution.py:20
  4.6 3.4 %collective-permute-start = (bf16[512,512]{1,0:T(8,128)(2,1)}, bf16[512,512]{1,0:T(8,128)(2,1)S(1)}, u32[]{:S(2)}, u32[]{:S(2)}) collective-permute-start(bf16[512,512]{1,0:T(8,128)(2,1)} %shard_map.101), channel_id=1, source_target_pairs={{0,2},{1,3},{2,4},{3,5},{4,6},{5,7},{6,8},{7,9},{8,10},{9,11},{10,... | collective-permute-start | bytes 1572872 | tf_op jit(solution)/shard_map/ppermute | solution.py:20
  8.0 0.7 %copy.14 = s32[32,1]{1,0:T(8,128)S(1)} copy(s32[32,1]{0,1:T(1,128)} %bitcast.5) | data formatting | bytes 256 | tf_op jit(solution)/shard_map/reshape.64
  8.8 0.1 reduce-window.8
  8.8 0.1 multiply_reduce_fusion
  8.9 0.1 convert_reduce_fusion
  9.1 0.1 convert_reduce_fusion.1
  9.2 0.1 copy.15
  9.4 0.0 copy-start.1
  9.4 0.0 copy-start.2
  9.4 2.1 %fusion.3.bias_ref = f32[512,1280]{1,0:T(8,128)} fusion(s32[512]{0:T(512)S(1)} %get-tuple-element.17, s32[512]{0:T(512)S(1)} %get-tuple-element.18, pred[512]{0:T(512)(128)(4,1)S(1)} %fusion.9), kind=kLoop, calls=%fused_computation.4 | loop fusion | flops 4587520 | bytes 2626048 | tf_op jit(solution)/shard_map/jit(_where)/select_n | solution.py:149
  11.5 7.0 %collective-permute-done.1 = bf16[512,512]{1,0:T(8,128)(2,1)S(1)} collective-permute-done((bf16[512,512]{1,0:T(8,128)(2,1)}, bf16[512,512]{1,0:T(8,128)(2,1)S(1)}, u32[]{:S(2)}, u32[]{:S(2)}) %collective-permute-start.1) | collective-permute-done | bytes 524320 | tf_op jit(solution)/shard_map/ppermute | solution.py:20
  18.6 5.0 %collective-permute-done = bf16[512,512]{1,0:T(8,128)(2,1)S(1)} collective-permute-done((bf16[512,512]{1,0:T(8,128)(2,1)}, bf16[512,512]{1,0:T(8,128)(2,1)S(1)}, u32[]{:S(2)}, u32[]{:S(2)}) %collective-permute-start) | collective-permute-done | bytes 524320 | tf_op jit(solution)/shard_map/ppermute | solution.py:20
  23.6 0.0 copy-done.3
  23.6 0.1 pad_maximum_fusion.k_ref.v_ref
  23.7 0.0 copy-done.1
  23.7 0.0 copy-done.2
  23.7 15.3 %shard_map.102 = (bf16[512,512]{1,0:T(8,128)(2,1)}, bf16[512,512]{1,0:T(8,128)(2,1)}, f32[1536,256]{1,0:T(8,128)S(1)}, f32[1536,256]{1,0:T(8,128)S(1)}) custom-call(bf16[512,512]{1,0:T(8,128)(2,1)S(1)} %copy-done.1, bf16[1536,512]{1,0:T(8,128)(2,1)S(1)} %pad_maximum_fusion.k_ref.v_ref, bf16[1536,512]{1,0:T(8,128)(2,1)S(1)} %pad_maximum_fusion.k_ref.v_ref, ...), custom_call_target="tpu_custom_call" | custom-call | flops 4026531840 | bytes 6815744 | tf_op jit(solution)/shard_map/pallas_call | solution.py:105
  39.0 0.1 slice.30
  39.0 0.0 copy-start.4
  39.0 0.1 slice.31
  39.1 0.1 maximum_convert_fusion
  39.2 0.1 fusion.10
  39.2 5.3 %collective-permute-start.2 = (bf16[512,512]{1,0:T(8,128)(2,1)S(1)}, bf16[512,512]{1,0:T(8,128)(2,1)S(1)}, u32[]{:S(2)}, u32[]{:S(2)}) collective-permute-start(bf16[512,512]{1,0:T(8,128)(2,1)S(1)} %get-tuple-element.13), channel_id=1, source_target_pairs={{1,0},{2,1},{3,2},{4,3},{5,4},{6,5},{7,6},{8,7},{9,8},{10,9},{11,1... | collective-permute-start | bytes 1572872 | tf_op jit(solution)/shard_map/ppermute | solution.py:20
  44.5 2.7 %collective-permute-start.3 = (bf16[512,512]{1,0:T(8,128)(2,1)S(1)}, bf16[512,512]{1,0:T(8,128)(2,1)S(1)}, u32[]{:S(2)}, u32[]{:S(2)}) collective-permute-start(bf16[512,512]{1,0:T(8,128)(2,1)S(1)} %get-tuple-element.14), channel_id=1, source_target_pairs={{2,0},{3,1},{4,2},{5,3},{6,4},{7,5},{8,6},{9,7},{10,8},{11,9},{12,... | collective-permute-start | bytes 1572872 | tf_op jit(solution)/shard_map/ppermute | solution.py:20
  47.3 0.0 copy-done
  47.3 0.0 copy-done.4
  47.3 0.2 fusion.12
  47.5 3.3 %collective-permute-start.4 = (f32[512,16]{0,1:T(8,128)S(1)}, f32[512,16]{0,1:T(8,128)S(1)}, u32[]{:S(2)}, u32[]{:S(2)}) collective-permute-start(f32[512,16]{0,1:T(8,128)S(1)} %fusion.12), channel_id=1, source_target_pairs={{0,64},{32,96},{64,0},{96,32},{128,192},{160,224},{192,128},{224,1... | collective-permute-start | bytes 98312 | tf_op jit(solution)/shard_map/ppermute | solution.py:38
  50.8 2.2 %collective-permute-done.4 = f32[512,16]{0,1:T(8,128)S(1)} collective-permute-done((f32[512,16]{0,1:T(8,128)S(1)}, f32[512,16]{0,1:T(8,128)S(1)}, u32[]{:S(2)}, u32[]{:S(2)}) %collective-permute-start.4) | collective-permute-done | bytes 32800 | tf_op jit(solution)/shard_map/ppermute | solution.py:38
  53.0 5.6 %collective-permute-start.5 = (f32[512,16]{0,1:T(8,128)S(1)}, f32[512,16]{0,1:T(8,128)S(1)}, u32[]{:S(2)}, u32[]{:S(2)}) collective-permute-start(f32[512,16]{0,1:T(8,128)S(1)} %add.79), channel_id=1, source_target_pairs={{0,192},{32,224},{64,128},{96,160},{128,64},{160,96},{192,0},{224,... | collective-permute-start | bytes 98312 | tf_op jit(solution)/shard_map/ppermute | solution.py:38
  58.7 1.9 %collective-permute-done.5 = f32[512,16]{0,1:T(8,128)S(1)} collective-permute-done((f32[512,16]{0,1:T(8,128)S(1)}, f32[512,16]{0,1:T(8,128)S(1)}, u32[]{:S(2)}, u32[]{:S(2)}) %collective-permute-start.5) | collective-permute-done | bytes 32800 | tf_op jit(solution)/shard_map/ppermute | solution.py:38
  60.6 1.0 %collective-permute-start.6 = (f32[512,16]{0,1:T(8,128)S(1)}, f32[512,16]{0,1:T(8,128)S(1)}, u32[]{:S(2)}, u32[]{:S(2)}) collective-permute-start(f32[512,16]{0,1:T(8,128)S(1)} %add.80), channel_id=1, source_target_pairs={{0,32},{32,0},{64,96},{96,64},{128,160},{160,128},{192,224},{224,1... | collective-permute-start | bytes 98312 | tf_op jit(solution)/shard_map/ppermute | solution.py:38
  61.7 2.8 %collective-permute-done.6 = f32[512,16]{0,1:T(8,128)S(1)} collective-permute-done((f32[512,16]{0,1:T(8,128)S(1)}, f32[512,16]{0,1:T(8,128)S(1)}, u32[]{:S(2)}, u32[]{:S(2)}) %collective-permute-start.6) | collective-permute-done | bytes 32800 | tf_op jit(solution)/shard_map/ppermute | solution.py:38
  64.5 0.6 add.81
  65.1 0.0 collective-permute-done.2
  65.1 0.0 collective-permute-done.3
  65.1 0.2 fusion.4
  65.3 0.8 %fusion.11 = (bf16[512,256]{1,0:T(8,128)(2,1)}, bf16[512,256]{1,0:T(8,128)(2,1)}) fusion(bf16[512,512]{1,0:T(8,128)(2,1)S(1)} %fusion.4), kind=kLoop, calls=%fused_computation.23 | loop fusion | bytes 1048576 | tf_op jit(solution)/shard_map/slice | solution.py:207
  (10 shorter events, 0.2 us)
Async XLA Ops:
  0.6 46.6 %copy-start = (bf16[16,512]{1,0:T(8,128)(2,1)S(1)}, bf16[16,512]{1,0:T(8,128)(2,1)}, u32[]{:S(2)}) copy-start(bf16[16,512]{1,0:T(8,128)(2,1)} %param.10) | copy-start | bytes 49156
  2.5 21.1 %copy-start.3 = (bf16[512,512]{1,0:T(8,128)(2,1)S(1)}, bf16[512,512]{1,0:T(8,128)(2,1)}, u32[]{:S(2)}) copy-start(bf16[512,512]{1,0:T(8,128)(2,1)} %shard_map.101) | copy-start | bytes 1572868
  2.5 16.0 %collective-permute-start.1 = (bf16[512,512]{1,0:T(8,128)(2,1)}, bf16[512,512]{1,0:T(8,128)(2,1)S(1)}, u32[]{:S(2)}, u32[]{:S(2)}) collective-permute-start(bf16[512,512]{1,0:T(8,128)(2,1)} %shard_map.101), channel_id=1, source_target_pairs={{0,1},{1,2},{2,3},{3,4},{4,5},{5,6},{6,7},{7,8},{8,9},{9,10},{10,1... | collective-permute-start | bytes 1572872 | tf_op jit(solution)/shard_map/ppermute | solution.py:20
  4.6 19.0 %collective-permute-start = (bf16[512,512]{1,0:T(8,128)(2,1)}, bf16[512,512]{1,0:T(8,128)(2,1)S(1)}, u32[]{:S(2)}, u32[]{:S(2)}) collective-permute-start(bf16[512,512]{1,0:T(8,128)(2,1)} %shard_map.101), channel_id=1, source_target_pairs={{0,2},{1,3},{2,4},{3,5},{4,6},{5,7},{6,8},{7,9},{8,10},{9,11},{10,... | collective-permute-start | bytes 1572872 | tf_op jit(solution)/shard_map/ppermute | solution.py:20
  9.4 14.3 %copy-start.1 = (bf16[512,512]{1,0:T(8,128)(2,1)S(1)}, bf16[512,512]{1,0:T(8,128)(2,1)}, u32[]{:S(2)}) copy-start(bf16[512,512]{1,0:T(8,128)(2,1)} %q_ref.1) | copy-start | bytes 1572868
  9.4 14.3 %copy-start.2 = (bf16[512,512]{1,0:T(8,128)(2,1)S(1)}, bf16[512,512]{1,0:T(8,128)(2,1)}, u32[]{:S(2)}) copy-start(bf16[512,512]{1,0:T(8,128)(2,1)} %do_ref.1) | copy-start | bytes 1572868
  39.0 8.3 %copy-start.4 = (bf16[512,512]{1,0:T(8,128)(2,1)S(1)}, bf16[512,512]{1,0:T(8,128)(2,1)}, u32[]{:S(2)}) copy-start(bf16[512,512]{1,0:T(8,128)(2,1)} %get-tuple-element.5) | copy-start | bytes 1572868
  39.2 25.9 %collective-permute-start.2 = (bf16[512,512]{1,0:T(8,128)(2,1)S(1)}, bf16[512,512]{1,0:T(8,128)(2,1)S(1)}, u32[]{:S(2)}, u32[]{:S(2)}) collective-permute-start(bf16[512,512]{1,0:T(8,128)(2,1)S(1)} %get-tuple-element.13), channel_id=1, source_target_pairs={{1,0},{2,1},{3,2},{4,3},{5,4},{6,5},{7,6},{8,7},{9,8},{10,9},{11,1... | collective-permute-start | bytes 1572872 | tf_op jit(solution)/shard_map/ppermute | solution.py:20
  44.5 20.6 %collective-permute-start.3 = (bf16[512,512]{1,0:T(8,128)(2,1)S(1)}, bf16[512,512]{1,0:T(8,128)(2,1)S(1)}, u32[]{:S(2)}, u32[]{:S(2)}) collective-permute-start(bf16[512,512]{1,0:T(8,128)(2,1)S(1)} %get-tuple-element.14), channel_id=1, source_target_pairs={{2,0},{3,1},{4,2},{5,3},{6,4},{7,5},{8,6},{9,7},{10,8},{11,9},{12,... | collective-permute-start | bytes 1572872 | tf_op jit(solution)/shard_map/ppermute | solution.py:20
  47.5 5.5 %collective-permute-start.4 = (f32[512,16]{0,1:T(8,128)S(1)}, f32[512,16]{0,1:T(8,128)S(1)}, u32[]{:S(2)}, u32[]{:S(2)}) collective-permute-start(f32[512,16]{0,1:T(8,128)S(1)} %fusion.12), channel_id=1, source_target_pairs={{0,64},{32,96},{64,0},{96,32},{128,192},{160,224},{192,128},{224,1... | collective-permute-start | bytes 98312 | tf_op jit(solution)/shard_map/ppermute | solution.py:38
  53.0 7.5 %collective-permute-start.5 = (f32[512,16]{0,1:T(8,128)S(1)}, f32[512,16]{0,1:T(8,128)S(1)}, u32[]{:S(2)}, u32[]{:S(2)}) collective-permute-start(f32[512,16]{0,1:T(8,128)S(1)} %add.79), channel_id=1, source_target_pairs={{0,192},{32,224},{64,128},{96,160},{128,64},{160,96},{192,0},{224,... | collective-permute-start | bytes 98312 | tf_op jit(solution)/shard_map/ppermute | solution.py:38
  60.6 3.9 %collective-permute-start.6 = (f32[512,16]{0,1:T(8,128)S(1)}, f32[512,16]{0,1:T(8,128)S(1)}, u32[]{:S(2)}, u32[]{:S(2)}) collective-permute-start(f32[512,16]{0,1:T(8,128)S(1)} %add.80), channel_id=1, source_target_pairs={{0,32},{32,0},{64,96},{96,64},{128,160},{160,128},{192,224},{224,1... | collective-permute-start | bytes 98312 | tf_op jit(solution)/shard_map/ppermute | solution.py:38

commit v10 on v8

--- a/solution.py
+++ b/solution.py
@@ -44,7 +44,7 @@
     return jnp.where(positions < 0, -1, counted)
 
 
-def attention_kernel(q_ref, k_ref, v_ref, do_ref, qdoc_ref, kdoc_ref, bias_ref,
+def attention_kernel(q_ref, k_ref, v_ref, do_ref, qdoc_ref, kdoc_ref,
                      o_ref, dq_ref, dk_ref, dv_ref, dk_acc, dv_acc):
     qb = pl.program_id(1)
     rows = q_ref.shape[0]
@@ -63,10 +63,14 @@
     qdoc = qdoc_ref[...]
     qdoc = jnp.concatenate([qdoc, qdoc], axis=0)
     kdoc = kdoc_ref[:, pl.ds(key_first, span)]
+    row = lax.broadcasted_iota(jnp.int32, (2 * rows, span), 0) % rows
+    col = lax.broadcasted_iota(jnp.int32, (2 * rows, span), 1)
+    offset = row + WIN - col
+    live = (offset >= 0) & (offset < WIN) & (qdoc == kdoc)
 
     s = lax.dot_general(q, k, (((1,), (1,)), ((), ())),
                         preferred_element_type=jnp.float32) * softmax_scale
-    masked = jnp.where(qdoc == kdoc, s + bias_ref[...], masked_value)
+    masked = jnp.where(live, s, masked_value)
     row_max = jnp.max(masked, axis=1, keepdims=True)
     e = jnp.exp(masked - row_max)
     row_sum = jnp.sum(e, axis=1, keepdims=True)
@@ -112,7 +116,6 @@
             pl.BlockSpec((rows, pair), lambda g, b: (b, g)),
             pl.BlockSpec((rows, 1), lambda g, b: (b, 0)),
             pl.BlockSpec((1, ext_rows), lambda g, b: (0, 0)),
-            pl.BlockSpec((2 * rows, span), lambda g, b: (0, 0)),
         ],
         out_specs=[
             pl.BlockSpec((rows, pair), lambda g, b: (b, g)),
@@ -137,16 +140,7 @@
         cost_estimate=pl.CostEstimate(
             flops=flops, transcendentals=groups * blocks * 2 * rows * span,
             bytes_accessed=nbytes),
-    )(queries, extended, extended, output_gradient, qdoc, kdoc, window_bias(rows))
-
-
-def window_bias(rows):
-    span = rows + WIN
-    row = lax.broadcasted_iota(jnp.int32, (2 * rows, span), 0) % rows
-    col = lax.broadcasted_iota(jnp.int32, (2 * rows, span), 1)
-    offset = row + WIN - col
-    inside = (offset >= 0) & (offset < WIN)
-    return jnp.where(inside, 0.0, masked_value).astype(jnp.float32)
+    )(queries, extended, extended, output_gradient, qdoc, kdoc)
 
 
 def body(

time: 66.2 us -> 66.4 us (level)
  waiting for transfers between devices: 18.7 us -> 20.9 us
  other arithmetic: 3.57 us -> 1.42 us
    ppermute x4, waiting for transfers between devices: 11.8 us -> 14 us  [passed_along(): return lax.ppermute(block, axis, route)]
    select_n x1 -> x0, other arithmetic: 2.13 us -> none  [window_bias(): return jnp.where(inside, 0.0, masked_value).astype(jnp.float32)]
  transfers between devices with their start and end apart: 7 -> 7, of which waited for: 5 -> 5; matrix products, arithmetic and copies ran while one was open for 7% -> 3% of each run, Pallas kernels for 0% -> 0%
where the time goes in v10:
time: 66.4 us; the launch traced here: 66.2 us
  starting transfers between devices  23.4 us (35%)
  waiting for transfers between devices  20.9 us (31%)
  Pallas kernels  15.4 us (23%)
  local copies, waits for them, and re-layouts  3.94 us (6%)
  other arithmetic  1.42 us (2%)
  between operations  0.84 us (1%)
    pallas_call x1, Pallas kernels, fused_attention(): pl.pallas_call(attention_kernel, grid=(groups, blocks), in_specs=[pl.Bloc...  15.4 us
    ppermute x4, waiting for transfers between devices, passed_along(): return lax.ppermute(block, axis, route)  14 us
    ppermute x4, starting transfers between devices, passed_along(): return lax.ppermute(block, axis, route)  13.5 us
    ppermute x3, starting transfers between devices, gathered_sum(): total = total + lax.ppermute(total, axis, route)  9.96 us
    ppermute x3, waiting for transfers between devices, gathered_sum(): total = total + lax.ppermute(total, axis, route)  6.9 us
  transfers between devices with their start and end apart: 7, of which 5 were waited for; matrix products, arithmetic and copies ran while one was open for 3% of the time, Pallas kernels for 0%

profile of v10, /device:TPU:24, one launch (start us, length us, event | category | flops | bytes accessed | tf_op | source)
XLA Modules:
  0.0 66.2 jit_solution(12980601564249378864)
XLA Ops:
  0.6 0.0 copy-start
  0.6 1.0 %constant_dynamic-update-slice_fusion.1 = bf16[512,512]{1,0:T(8,128)(2,1)S(1)} fusion(bf16[512,256]{1,0:T(8,128)(2,1)} %param.7), kind=kLoop, calls=%fused_computation.12 | loop fusion | bytes 524288
  1.6 1.0 %constant_dynamic-update-slice_fusion = bf16[512,512]{1,0:T(8,128)(2,1)S(1)} fusion(bf16[512,512]{1,0:T(8,128)(2,1)S(1)} %constant_dynamic-update-slice_fusion.1, bf16[512,256]{1,0:T(8,128)(2,1)} %param.8), kind=kLoop, calls=%fused_computation.11 | loop fusion | bytes 524288 | tf_op jit(solution)/shard_map/concatenate | solution.py:162
  2.6 1.9 %collective-permute-start.1 = (bf16[512,512]{1,0:T(8,128)(2,1)S(1)}, bf16[512,512]{1,0:T(8,128)(2,1)S(1)}, u32[]{:S(2)}, u32[]{:S(2)}) collective-permute-start(bf16[512,512]{1,0:T(8,128)(2,1)S(1)} %constant_dynamic-update-slice_fusion), channel_id=1, source_target_pairs={{0,1},{1,2},{2,3},{3,4},{4,5},{5,6},{6,7},{7,8},{8,9},{9,10},{10,1... | collective-permute-start | bytes 1572872 | tf_op jit(solution)/shard_map/ppermute | solution.py:20
  4.5 3.4 %collective-permute-start = (bf16[512,512]{1,0:T(8,128)(2,1)S(1)}, bf16[512,512]{1,0:T(8,128)(2,1)S(1)}, u32[]{:S(2)}, u32[]{:S(2)}) collective-permute-start(bf16[512,512]{1,0:T(8,128)(2,1)S(1)} %constant_dynamic-update-slice_fusion), channel_id=1, source_target_pairs={{0,2},{1,3},{2,4},{3,5},{4,6},{5,7},{6,8},{7,9},{8,10},{9,11},{10,... | collective-permute-start | bytes 1572872 | tf_op jit(solution)/shard_map/ppermute | solution.py:20
  8.0 0.7 %copy.14 = s32[32,1]{1,0:T(8,128)S(1)} copy(s32[32,1]{0,1:T(1,128)} %bitcast.5) | data formatting | bytes 256 | tf_op jit(solution)/shard_map/reshape.64
  8.7 0.1 reduce-window.8
  8.8 0.1 multiply_reduce_fusion
  8.9 0.1 convert_reduce_fusion.1
  9.0 0.2 copy.15
  9.1 0.1 convert_reduce_fusion
  9.3 0.0 copy-start.1
  9.3 0.0 copy-start.2
  9.3 9.0 %collective-permute-done.1 = bf16[512,512]{1,0:T(8,128)(2,1)S(1)} collective-permute-done((bf16[512,512]{1,0:T(8,128)(2,1)S(1)}, bf16[512,512]{1,0:T(8,128)(2,1)S(1)}, u32[]{:S(2)}, u32[]{:S(2)}) %collective-permute-start.1) | collective-permute-done | bytes 524320 | tf_op jit(solution)/shard_map/ppermute | solution.py:20
  18.3 5.0 %collective-permute-done = bf16[512,512]{1,0:T(8,128)(2,1)S(1)} collective-permute-done((bf16[512,512]{1,0:T(8,128)(2,1)S(1)}, bf16[512,512]{1,0:T(8,128)(2,1)S(1)}, u32[]{:S(2)}, u32[]{:S(2)}) %collective-permute-start) | collective-permute-done | bytes 524320 | tf_op jit(solution)/shard_map/ppermute | solution.py:20
  23.3 0.1 pad_maximum_fusion.k_ref.v_ref
  23.4 0.0 copy-done.1
  23.4 0.0 copy-done.2
  23.5 15.4 %shard_map.101 = (bf16[512,512]{1,0:T(8,128)(2,1)}, bf16[512,512]{1,0:T(8,128)(2,1)}, f32[1536,256]{1,0:T(8,128)S(1)}, f32[1536,256]{1,0:T(8,128)S(1)}) custom-call(bf16[512,512]{1,0:T(8,128)(2,1)S(1)} %copy-done.1, bf16[1536,512]{1,0:T(8,128)(2,1)S(1)} %pad_maximum_fusion.k_ref.v_ref, bf16[1536,512]{1,0:T(8,128)(2,1)S(1)} %pad_maximum_fusion.k_ref.v_ref, ...), custom_call_target="tpu_custom_call" | custom-call | flops 4026531840 | bytes 6815744 | tf_op jit(solution)/shard_map/pallas_call | solution.py:109
  38.9 0.1 slice.30
  38.9 0.1 slice.31
  39.0 0.1 maximum_convert_fusion
  39.1 0.0 copy-start.3
  39.1 0.1 fusion.2
  39.1 5.4 %collective-permute-start.2 = (bf16[512,512]{1,0:T(8,128)(2,1)S(1)}, bf16[512,512]{1,0:T(8,128)(2,1)S(1)}, u32[]{:S(2)}, u32[]{:S(2)}) collective-permute-start(bf16[512,512]{1,0:T(8,128)(2,1)S(1)} %get-tuple-element.13), channel_id=1, source_target_pairs={{1,0},{2,1},{3,2},{4,3},{5,4},{6,5},{7,6},{8,7},{9,8},{10,9},{11,1... | collective-permute-start | bytes 1572872 | tf_op jit(solution)/shard_map/ppermute | solution.py:20
  44.6 2.7 %collective-permute-start.3 = (bf16[512,512]{1,0:T(8,128)(2,1)S(1)}, bf16[512,512]{1,0:T(8,128)(2,1)S(1)}, u32[]{:S(2)}, u32[]{:S(2)}) collective-permute-start(bf16[512,512]{1,0:T(8,128)(2,1)S(1)} %get-tuple-element.14), channel_id=1, source_target_pairs={{2,0},{3,1},{4,2},{5,3},{6,4},{7,5},{8,6},{9,7},{10,8},{11,9},{12,... | collective-permute-start | bytes 1572872 | tf_op jit(solution)/shard_map/ppermute | solution.py:20
  47.3 0.0 copy-done
  47.3 0.0 copy-done.3
  47.3 0.2 fusion.4
  47.6 3.3 %collective-permute-start.4 = (f32[512,16]{0,1:T(8,128)S(1)}, f32[512,16]{0,1:T(8,128)S(1)}, u32[]{:S(2)}, u32[]{:S(2)}) collective-permute-start(f32[512,16]{0,1:T(8,128)S(1)} %fusion.4), channel_id=1, source_target_pairs={{0,64},{32,96},{64,0},{96,32},{128,192},{160,224},{192,128},{224,1... | collective-permute-start | bytes 98312 | tf_op jit(solution)/shard_map/ppermute | solution.py:38
  50.9 2.2 %collective-permute-done.4 = f32[512,16]{0,1:T(8,128)S(1)} collective-permute-done((f32[512,16]{0,1:T(8,128)S(1)}, f32[512,16]{0,1:T(8,128)S(1)}, u32[]{:S(2)}, u32[]{:S(2)}) %collective-permute-start.4) | collective-permute-done | bytes 32800 | tf_op jit(solution)/shard_map/ppermute | solution.py:38
  53.1 5.6 %collective-permute-start.5 = (f32[512,16]{0,1:T(8,128)S(1)}, f32[512,16]{0,1:T(8,128)S(1)}, u32[]{:S(2)}, u32[]{:S(2)}) collective-permute-start(f32[512,16]{0,1:T(8,128)S(1)} %add.67), channel_id=1, source_target_pairs={{0,192},{32,224},{64,128},{96,160},{128,64},{160,96},{192,0},{224,... | collective-permute-start | bytes 98312 | tf_op jit(solution)/shard_map/ppermute | solution.py:38
  58.7 1.9 %collective-permute-done.5 = f32[512,16]{0,1:T(8,128)S(1)} collective-permute-done((f32[512,16]{0,1:T(8,128)S(1)}, f32[512,16]{0,1:T(8,128)S(1)}, u32[]{:S(2)}, u32[]{:S(2)}) %collective-permute-start.5) | collective-permute-done | bytes 32800 | tf_op jit(solution)/shard_map/ppermute | solution.py:38
  60.6 1.0 %collective-permute-start.6 = (f32[512,16]{0,1:T(8,128)S(1)}, f32[512,16]{0,1:T(8,128)S(1)}, u32[]{:S(2)}, u32[]{:S(2)}) collective-permute-start(f32[512,16]{0,1:T(8,128)S(1)} %add.68), channel_id=1, source_target_pairs={{0,32},{32,0},{64,96},{96,64},{128,160},{160,128},{192,224},{224,1... | collective-permute-start | bytes 98312 | tf_op jit(solution)/shard_map/ppermute | solution.py:38
  61.7 2.8 %collective-permute-done.6 = f32[512,16]{0,1:T(8,128)S(1)} collective-permute-done((f32[512,16]{0,1:T(8,128)S(1)}, f32[512,16]{0,1:T(8,128)S(1)}, u32[]{:S(2)}, u32[]{:S(2)}) %collective-permute-start.6) | collective-permute-done | bytes 32800 | tf_op jit(solution)/shard_map/ppermute | solution.py:38
  64.5 0.6 add.69
  65.1 0.0 collective-permute-done.2
  65.1 0.0 collective-permute-done.3
  65.1 0.2 fusion
  65.3 0.8 %fusion.3 = (bf16[512,256]{1,0:T(8,128)(2,1)}, bf16[512,256]{1,0:T(8,128)(2,1)}) fusion(bf16[512,512]{1,0:T(8,128)(2,1)S(1)} %fusion), kind=kLoop, calls=%fused_computation.15 | loop fusion | bytes 1048576 | tf_op jit(solution)/shard_map/slice | solution.py:185
  (8 shorter events, 0.1 us)
Async XLA Ops:
  0.6 46.7 %copy-start = (bf16[16,512]{1,0:T(8,128)(2,1)S(1)}, bf16[16,512]{1,0:T(8,128)(2,1)}, u32[]{:S(2)}) copy-start(bf16[16,512]{1,0:T(8,128)(2,1)} %param.10) | copy-start | bytes 49156
  2.6 15.7 %collective-permute-start.1 = (bf16[512,512]{1,0:T(8,128)(2,1)S(1)}, bf16[512,512]{1,0:T(8,128)(2,1)S(1)}, u32[]{:S(2)}, u32[]{:S(2)}) collective-permute-start(bf16[512,512]{1,0:T(8,128)(2,1)S(1)} %constant_dynamic-update-slice_fusion), channel_id=1, source_target_pairs={{0,1},{1,2},{2,3},{3,4},{4,5},{5,6},{6,7},{7,8},{8,9},{9,10},{10,1... | collective-permute-start | bytes 1572872 | tf_op jit(solution)/shard_map/ppermute | solution.py:20
  4.5 18.8 %collective-permute-start = (bf16[512,512]{1,0:T(8,128)(2,1)S(1)}, bf16[512,512]{1,0:T(8,128)(2,1)S(1)}, u32[]{:S(2)}, u32[]{:S(2)}) collective-permute-start(bf16[512,512]{1,0:T(8,128)(2,1)S(1)} %constant_dynamic-update-slice_fusion), channel_id=1, source_target_pairs={{0,2},{1,3},{2,4},{3,5},{4,6},{5,7},{6,8},{7,9},{8,10},{9,11},{10,... | collective-permute-start | bytes 1572872 | tf_op jit(solution)/shard_map/ppermute | solution.py:20
  9.3 14.1 %copy-start.1 = (bf16[512,512]{1,0:T(8,128)(2,1)S(1)}, bf16[512,512]{1,0:T(8,128)(2,1)}, u32[]{:S(2)}) copy-start(bf16[512,512]{1,0:T(8,128)(2,1)} %q_ref.1) | copy-start | bytes 1572868
  9.3 14.1 %copy-start.2 = (bf16[512,512]{1,0:T(8,128)(2,1)S(1)}, bf16[512,512]{1,0:T(8,128)(2,1)}, u32[]{:S(2)}) copy-start(bf16[512,512]{1,0:T(8,128)(2,1)} %do_ref.1) | copy-start | bytes 1572868
  39.1 8.3 %copy-start.3 = (bf16[512,512]{1,0:T(8,128)(2,1)S(1)}, bf16[512,512]{1,0:T(8,128)(2,1)}, u32[]{:S(2)}) copy-start(bf16[512,512]{1,0:T(8,128)(2,1)} %get-tuple-element.5) | copy-start | bytes 1572868
  39.1 26.0 %collective-permute-start.2 = (bf16[512,512]{1,0:T(8,128)(2,1)S(1)}, bf16[512,512]{1,0:T(8,128)(2,1)S(1)}, u32[]{:S(2)}, u32[]{:S(2)}) collective-permute-start(bf16[512,512]{1,0:T(8,128)(2,1)S(1)} %get-tuple-element.13), channel_id=1, source_target_pairs={{1,0},{2,1},{3,2},{4,3},{5,4},{6,5},{7,6},{8,7},{9,8},{10,9},{11,1... | collective-permute-start | bytes 1572872 | tf_op jit(solution)/shard_map/ppermute | solution.py:20
  44.6 20.6 %collective-permute-start.3 = (bf16[512,512]{1,0:T(8,128)(2,1)S(1)}, bf16[512,512]{1,0:T(8,128)(2,1)S(1)}, u32[]{:S(2)}, u32[]{:S(2)}) collective-permute-start(bf16[512,512]{1,0:T(8,128)(2,1)S(1)} %get-tuple-element.14), channel_id=1, source_target_pairs={{2,0},{3,1},{4,2},{5,3},{6,4},{7,5},{8,6},{9,7},{10,8},{11,9},{12,... | collective-permute-start | bytes 1572872 | tf_op jit(solution)/shard_map/ppermute | solution.py:20
  47.6 5.5 %collective-permute-start.4 = (f32[512,16]{0,1:T(8,128)S(1)}, f32[512,16]{0,1:T(8,128)S(1)}, u32[]{:S(2)}, u32[]{:S(2)}) collective-permute-start(f32[512,16]{0,1:T(8,128)S(1)} %fusion.4), channel_id=1, source_target_pairs={{0,64},{32,96},{64,0},{96,32},{128,192},{160,224},{192,128},{224,1... | collective-permute-start | bytes 98312 | tf_op jit(solution)/shard_map/ppermute | solution.py:38
  53.1 7.5 %collective-permute-start.5 = (f32[512,16]{0,1:T(8,128)S(1)}, f32[512,16]{0,1:T(8,128)S(1)}, u32[]{:S(2)}, u32[]{:S(2)}) collective-permute-start(f32[512,16]{0,1:T(8,128)S(1)} %add.67), channel_id=1, source_target_pairs={{0,192},{32,224},{64,128},{96,160},{128,64},{160,96},{192,0},{224,... | collective-permute-start | bytes 98312 | tf_op jit(solution)/shard_map/ppermute | solution.py:38
  60.6 3.9 %collective-permute-start.6 = (f32[512,16]{0,1:T(8,128)S(1)}, f32[512,16]{0,1:T(8,128)S(1)}, u32[]{:S(2)}, u32[]{:S(2)}) collective-permute-start(f32[512,16]{0,1:T(8,128)S(1)} %add.68), channel_id=1, source_target_pairs={{0,32},{32,0},{64,96},{96,64},{128,160},{160,128},{192,224},{224,1... | collective-permute-start | bytes 98312 | tf_op jit(solution)/shard_map/ppermute | solution.py:38

commit v11 on v10

--- a/solution.py
+++ b/solution.py
@@ -1,3 +1,5 @@
+import functools
+
 import jax
 import jax.numpy as jnp
 from jax import lax
@@ -44,12 +46,14 @@
     return jnp.where(positions < 0, -1, counted)
 
 
-def attention_kernel(q_ref, k_ref, v_ref, do_ref, qdoc_ref, kdoc_ref,
+SPAN_BUCKETS = (2, 4)
+
+
+def attention_kernel(need_ref, q_ref, k_ref, v_ref, do_ref, qdoc_ref, kdoc_ref,
                      o_ref, dq_ref, dk_ref, dv_ref, dk_acc, dv_acc):
     qb = pl.program_id(1)
     rows = q_ref.shape[0]
-    span = rows + WIN
-    key_first = pl.multiple_of(qb * rows, rows)
+    full = (rows + WIN) // rows
 
     @pl.when(qb == 0)
     def _():
@@ -58,38 +62,48 @@
 
     q = jnp.concatenate([q_ref[:, :HEAD_SIZE], q_ref[:, HEAD_SIZE:]], axis=0)
     do = jnp.concatenate([do_ref[:, :HEAD_SIZE], do_ref[:, HEAD_SIZE:]], axis=0)
-    k = k_ref[pl.ds(key_first, span), :]
-    v = v_ref[pl.ds(key_first, span), :]
     qdoc = qdoc_ref[...]
     qdoc = jnp.concatenate([qdoc, qdoc], axis=0)
-    kdoc = kdoc_ref[:, pl.ds(key_first, span)]
-    row = lax.broadcasted_iota(jnp.int32, (2 * rows, span), 0) % rows
-    col = lax.broadcasted_iota(jnp.int32, (2 * rows, span), 1)
-    offset = row + WIN - col
-    live = (offset >= 0) & (offset < WIN) & (qdoc == kdoc)
-
-    s = lax.dot_general(q, k, (((1,), (1,)), ((), ())),
-                        preferred_element_type=jnp.float32) * softmax_scale
-    masked = jnp.where(live, s, masked_value)
-    row_max = jnp.max(masked, axis=1, keepdims=True)
-    e = jnp.exp(masked - row_max)
-    row_sum = jnp.sum(e, axis=1, keepdims=True)
-    p = e * (1.0 / row_sum)
-    p_low = p.astype(jnp.bfloat16)
-    o = jnp.dot(p_low, v, preferred_element_type=jnp.float32)
-    row_dot = jnp.sum(do.astype(jnp.float32) * o, axis=1, keepdims=True)
-    dp = lax.dot_general(do, v, (((1,), (1,)), ((), ())),
-                         preferred_element_type=jnp.float32)
-    ds = (p * (dp - row_dot)).astype(jnp.bfloat16)
-    dq = jnp.dot(ds, k, preferred_element_type=jnp.float32) * softmax_scale
-    dk = jnp.dot(q.T, ds, preferred_element_type=jnp.float32) * softmax_scale
-    dv = jnp.dot(do.T, p_low, preferred_element_type=jnp.float32)
-    o_ref[:, :HEAD_SIZE] = o[:rows].astype(o_ref.dtype)
-    o_ref[:, HEAD_SIZE:] = o[rows:].astype(o_ref.dtype)
-    dq_ref[:, :HEAD_SIZE] = dq[:rows].astype(dq_ref.dtype)
-    dq_ref[:, HEAD_SIZE:] = dq[rows:].astype(dq_ref.dtype)
-    dk_acc[:, pl.ds(key_first, span)] += dk
-    dv_acc[:, pl.ds(key_first, span)] += dv
+    need = need_ref[qb]
+
+    def run(width):
+        span = width * rows
+        key_first = pl.multiple_of((qb + full - width) * rows, rows)
+        k = k_ref[pl.ds(key_first, span), :]
+        v = v_ref[pl.ds(key_first, span), :]
+        kdoc = kdoc_ref[:, pl.ds(key_first, span)]
+        row = lax.broadcasted_iota(jnp.int32, (2 * rows, span), 0) % rows
+        col = lax.broadcasted_iota(jnp.int32, (2 * rows, span), 1)
+        offset = row + span - rows - col
+        live = (offset >= 0) & (offset < WIN) & (qdoc == kdoc)
+
+        s = lax.dot_general(q, k, (((1,), (1,)), ((), ())),
+                            preferred_element_type=jnp.float32) * softmax_scale
+        masked = jnp.where(live, s, masked_value)
+        row_max = jnp.max(masked, axis=1, keepdims=True)
+        e = jnp.exp(masked - row_max)
+        row_sum = jnp.sum(e, axis=1, keepdims=True)
+        p = e * (1.0 / row_sum)
+        p_low = p.astype(jnp.bfloat16)
+        o = jnp.dot(p_low, v, preferred_element_type=jnp.float32)
+        row_dot = jnp.sum(do.astype(jnp.float32) * o, axis=1, keepdims=True)
+        dp = lax.dot_general(do, v, (((1,), (1,)), ((), ())),
+                             preferred_element_type=jnp.float32)
+        ds = (p * (dp - row_dot)).astype(jnp.bfloat16)
+        dq = jnp.dot(ds, k, preferred_element_type=jnp.float32) * softmax_scale
+        dk = jnp.dot(q.T, ds, preferred_element_type=jnp.float32) * softmax_scale
+        dv = jnp.dot(do.T, p_low, preferred_element_type=jnp.float32)
+        o_ref[:, :HEAD_SIZE] = o[:rows].astype(o_ref.dtype)
+        o_ref[:, HEAD_SIZE:] = o[rows:].astype(o_ref.dtype)
+        dq_ref[:, :HEAD_SIZE] = dq[:rows].astype(dq_ref.dtype)
+        dq_ref[:, HEAD_SIZE:] = dq[rows:].astype(dq_ref.dtype)
+        dk_acc[:, pl.ds(key_first, span)] += dk
+        dv_acc[:, pl.ds(key_first, span)] += dv
+
+    low = 0
+    for width in SPAN_BUCKETS + (full,):
+        pl.when((need > low) & (need <= width))(functools.partial(run, width))
+        low = width
 
     @pl.when(qb == pl.num_programs(1) - 1)
     def _():
@@ -97,7 +111,7 @@
         dv_ref[...] = dv_acc[...].T
 
 
-def fused_attention(queries, extended, output_gradient, qdoc, kdoc, rows=2 * BLK):
+def fused_attention(need, queries, extended, output_gradient, qdoc, kdoc, rows=BLK):
     tokens, query_cols = queries.shape
     ext_rows, joined_cols = extended.shape
     groups = joined_cols // (2 * HEAD_SIZE)
@@ -110,6 +124,7 @@
         attention_kernel,
         grid=(groups, blocks),
         in_specs=[
+            pl.BlockSpec(memory_space=pltpu.SMEM),
             pl.BlockSpec((rows, pair), lambda g, b: (b, g)),
             pl.BlockSpec((ext_rows, HEAD_SIZE), lambda g, b: (0, g)),
             pl.BlockSpec((ext_rows, HEAD_SIZE), lambda g, b: (0, g + groups)),
@@ -140,7 +155,18 @@
         cost_estimate=pl.CostEstimate(
             flops=flops, transcendentals=groups * blocks * 2 * rows * span,
             bytes_accessed=nbytes),
-    )(queries, extended, extended, output_gradient, qdoc, kdoc)
+    )(need, queries, extended, extended, output_gradient, qdoc, kdoc)
+
+
+def live_key_blocks(block_first, blocks, doc_ends):
+    full = (BLK + WIN) // BLK
+    local = jnp.arange(blocks, dtype=jnp.int32)
+    first_row = (block_first + local) * BLK
+    doc = jnp.sum((first_row[:, None] >= doc_ends[None, :]).astype(jnp.int32), axis=1)
+    ends = jnp.concatenate([jnp.zeros((1,), jnp.int32), doc_ends.astype(jnp.int32)])
+    doc_first = ends[doc] // BLK
+    ext_first = doc_first - (block_first - WIN // BLK)
+    return jnp.clip(local + full - jnp.maximum(local, ext_first), 1, full).astype(jnp.int32)
 
 
 def body(
@@ -166,7 +192,9 @@
     extended = jnp.concatenate(arrived[::-1] + [joined], axis=0)
     qdoc = doc_index(first_pos + jnp.arange(tokens_here, dtype=jnp.int32), doc_ends)
     kdoc = doc_index(lowest + jnp.arange(WIN + tokens_here, dtype=jnp.int32), doc_ends)
+    need = live_key_blocks(first_pos // BLK, tokens_here // BLK, doc_ends)
     attended, flattened_query, key_grads, value_grads = fused_attention(
+        need,
         queries, extended, output_gradient, qdoc[:, None], kdoc[None, :]
     )
     halo_grads = jnp.concatenate([key_grads[:WIN], value_grads[:WIN]], axis=1)

time: 66.4 us -> 67.6 us (1.018)
  starting transfers between devices: 23.4 us -> 30.2 us
  Pallas kernels: 15.4 us -> 10.3 us
  waiting for transfers between devices: 20.9 us -> 19.7 us
    ppermute x4, starting transfers between devices: 13.5 us -> 19.9 us  [passed_along(): return lax.ppermute(block, axis, route)]
    pallas_call x1, Pallas kernels: 15.4 us -> 10.3 us  [fused_attention(): pl.pallas_call(attention_kernel, grid=(groups, blocks), in_specs=[pl.Bloc...]
    ppermute x4, waiting for transfers between devices: 14 us -> 13 us  [passed_along(): return lax.ppermute(block, axis, route)]
  transfers between devices with their start and end apart: 7 -> 7, of which waited for: 5 -> 5; matrix products, arithmetic and copies ran while one was open for 3% -> 5% of each run, Pallas kernels for 0% -> 0%
where the time goes in v11:
time: 67.6 us
  starting transfers between devices  30.2 us (45%)
  waiting for transfers between devices  19.7 us (29%)
  Pallas kernels  10.3 us (15%)
  local copies, waits for them, and re-layouts  4.57 us (7%)
  other arithmetic  1.72 us (3%)
  between operations  0.87 us (1%)
    ppermute x4, starting transfers between devices, passed_along(): return lax.ppermute(block, axis, route)  19.9 us
    ppermute x4, waiting for transfers between devices, passed_along(): return lax.ppermute(block, axis, route)  13 us
    ppermute x3, starting transfers between devices, gathered_sum(): total = total + lax.ppermute(total, axis, route)  10.3 us
    pallas_call x1, Pallas kernels, fused_attention(): pl.pallas_call(attention_kernel, grid=(groups, blocks), in_specs=[pl.Bloc...  10.3 us
    ppermute x3, waiting for transfers between devices, gathered_sum(): total = total + lax.ppermute(total, axis, route)  6.68 us
  transfers between devices with their start and end apart: 7, of which 5 were waited for; matrix products, arithmetic and copies ran while one was open for 5% of the time, Pallas kernels for 0%

profile of v11, /device:TPU:24, one launch (start us, length us, event | category | flops | bytes accessed | tf_op | source)
XLA Modules:
  0.0 67.6 jit_solution(9580368650535987405)
XLA Ops:
  0.6 0.0 copy-start
  0.6 1.0 %constant_dynamic-update-slice_fusion.1 = bf16[512,512]{1,0:T(8,128)(2,1)S(1)} fusion(bf16[512,256]{1,0:T(8,128)(2,1)} %param.7), kind=kLoop, calls=%fused_computation.14 | loop fusion | bytes 524288
  1.6 1.0 %constant_dynamic-update-slice_fusion = bf16[512,512]{1,0:T(8,128)(2,1)S(1)} fusion(bf16[512,512]{1,0:T(8,128)(2,1)S(1)} %constant_dynamic-update-slice_fusion.1, bf16[512,256]{1,0:T(8,128)(2,1)} %param.8), kind=kLoop, calls=%fused_computation.13 | loop fusion | bytes 524288 | tf_op jit(solution)/shard_map/concatenate | solution.py:188
  2.6 1.9 %collective-permute-start.1 = (bf16[512,512]{1,0:T(8,128)(2,1)S(1)}, bf16[512,512]{1,0:T(8,128)(2,1)S(1)}, u32[]{:S(2)}, u32[]{:S(2)}) collective-permute-start(bf16[512,512]{1,0:T(8,128)(2,1)S(1)} %constant_dynamic-update-slice_fusion), channel_id=1, source_target_pairs={{0,1},{1,2},{2,3},{3,4},{4,5},{5,6},{6,7},{7,8},{8,9},{9,10},{10,1... | collective-permute-start | bytes 1572872 | tf_op jit(solution)/shard_map/ppermute | solution.py:22
  4.5 3.4 %collective-permute-start = (bf16[512,512]{1,0:T(8,128)(2,1)S(1)}, bf16[512,512]{1,0:T(8,128)(2,1)S(1)}, u32[]{:S(2)}, u32[]{:S(2)}) collective-permute-start(bf16[512,512]{1,0:T(8,128)(2,1)S(1)} %constant_dynamic-update-slice_fusion), channel_id=1, source_target_pairs={{0,2},{1,3},{2,4},{3,5},{4,6},{5,7},{6,8},{7,9},{8,10},{9,11},{10,... | collective-permute-start | bytes 1572872 | tf_op jit(solution)/shard_map/ppermute | solution.py:22
  8.0 0.7 %copy.14 = s32[32,1]{1,0:T(8,128)S(1)} copy(s32[32,1]{0,1:T(1,128)} %bitcast.9) | data formatting | bytes 256 | tf_op jit(solution)/shard_map/reshape.76
  8.7 0.1 reduce-window.7
  8.8 0.1 multiply_reduce_fusion
  8.9 0.1 convert_reduce_fusion.1
  9.0 0.2 convert_reduce_fusion.2
  9.2 0.1 pad_add_fusion
  9.3 0.1 copy.15
  9.4 0.6 gather_fusion
  10.1 0.1 convert_reduce_fusion
  10.3 0.0 copy-start.1
  10.3 0.0 copy-start.2
  10.3 8.0 %collective-permute-done.1 = bf16[512,512]{1,0:T(8,128)(2,1)S(1)} collective-permute-done((bf16[512,512]{1,0:T(8,128)(2,1)S(1)}, bf16[512,512]{1,0:T(8,128)(2,1)S(1)}, u32[]{:S(2)}, u32[]{:S(2)}) %collective-permute-start.1) | collective-permute-done | bytes 524320 | tf_op jit(solution)/shard_map/ppermute | solution.py:22
  18.3 5.0 %collective-permute-done = bf16[512,512]{1,0:T(8,128)(2,1)S(1)} collective-permute-done((bf16[512,512]{1,0:T(8,128)(2,1)S(1)}, bf16[512,512]{1,0:T(8,128)(2,1)S(1)}, u32[]{:S(2)}, u32[]{:S(2)}) %collective-permute-start) | collective-permute-done | bytes 524320 | tf_op jit(solution)/shard_map/ppermute | solution.py:22
  23.3 0.1 pad_maximum_fusion.k_ref.v_ref
  23.4 0.0 copy-done.1
  23.4 0.0 copy-done.2
  23.5 10.3 %shard_map.101 = (bf16[512,512]{1,0:T(8,128)(2,1)}, bf16[512,512]{1,0:T(8,128)(2,1)}, f32[1536,256]{1,0:T(8,128)S(1)}, f32[1536,256]{1,0:T(8,128)S(1)}) custom-call(s32[4]{0:T(128)S(1)} %subtract_clamp_fusion.need_ref, bf16[512,512]{1,0:T(8,128)(2,1)S(1)} %copy-done.1, bf16[1536,512]{1,0:T(8,128)(2,1)S(1)} %pad_maximum_fusion.k_ref.v_ref, ...), custom_call_target="tpu_custom_call" | custom-call | flops 3623878656 | bytes 6815744 | tf_op jit(solution)/shard_map/pallas_call | solution.py:123
  33.7 0.1 slice.30
  33.8 0.1 slice.31
  33.8 0.1 maximum_convert_fusion
  33.9 0.0 copy-start.3
  33.9 0.1 fusion.3
  34.0 5.1 %collective-permute-start.2 = (bf16[512,512]{1,0:T(8,128)(2,1)S(1)}, bf16[512,512]{1,0:T(8,128)(2,1)S(1)}, u32[]{:S(2)}, u32[]{:S(2)}) collective-permute-start(bf16[512,512]{1,0:T(8,128)(2,1)S(1)} %get-tuple-element.13), channel_id=1, source_target_pairs={{1,0},{2,1},{3,2},{4,3},{5,4},{6,5},{7,6},{8,7},{9,8},{10,9},{11,1... | collective-permute-start | bytes 1572872 | tf_op jit(solution)/shard_map/ppermute | solution.py:22
  39.1 9.5 %collective-permute-start.3 = (bf16[512,512]{1,0:T(8,128)(2,1)S(1)}, bf16[512,512]{1,0:T(8,128)(2,1)S(1)}, u32[]{:S(2)}, u32[]{:S(2)}) collective-permute-start(bf16[512,512]{1,0:T(8,128)(2,1)S(1)} %get-tuple-element.14), channel_id=1, source_target_pairs={{2,0},{3,1},{4,2},{5,3},{6,4},{7,5},{8,6},{9,7},{10,8},{11,9},{12,... | collective-permute-start | bytes 1572872 | tf_op jit(solution)/shard_map/ppermute | solution.py:22
  48.6 0.0 copy-done
  48.6 0.0 copy-done.3
  48.6 0.2 fusion.5
  48.8 3.3 %collective-permute-start.4 = (f32[512,16]{0,1:T(8,128)S(1)}, f32[512,16]{0,1:T(8,128)S(1)}, u32[]{:S(2)}, u32[]{:S(2)}) collective-permute-start(f32[512,16]{0,1:T(8,128)S(1)} %fusion.5), channel_id=1, source_target_pairs={{0,64},{32,96},{64,0},{96,32},{128,192},{160,224},{192,128},{224,1... | collective-permute-start | bytes 98312 | tf_op jit(solution)/shard_map/ppermute | solution.py:40
  52.2 1.9 %collective-permute-done.4 = f32[512,16]{0,1:T(8,128)S(1)} collective-permute-done((f32[512,16]{0,1:T(8,128)S(1)}, f32[512,16]{0,1:T(8,128)S(1)}, u32[]{:S(2)}, u32[]{:S(2)}) %collective-permute-start.4) | collective-permute-done | bytes 32800 | tf_op jit(solution)/shard_map/ppermute | solution.py:40
  54.0 6.0 %collective-permute-start.5 = (f32[512,16]{0,1:T(8,128)S(1)}, f32[512,16]{0,1:T(8,128)S(1)}, u32[]{:S(2)}, u32[]{:S(2)}) collective-permute-start(f32[512,16]{0,1:T(8,128)S(1)} %add.97), channel_id=1, source_target_pairs={{0,192},{32,224},{64,128},{96,160},{128,64},{160,96},{192,0},{224,... | collective-permute-start | bytes 98312 | tf_op jit(solution)/shard_map/ppermute | solution.py:40
  60.1 1.9 %collective-permute-done.5 = f32[512,16]{0,1:T(8,128)S(1)} collective-permute-done((f32[512,16]{0,1:T(8,128)S(1)}, f32[512,16]{0,1:T(8,128)S(1)}, u32[]{:S(2)}, u32[]{:S(2)}) %collective-permute-start.5) | collective-permute-done | bytes 32800 | tf_op jit(solution)/shard_map/ppermute | solution.py:40
  62.0 0.9 %collective-permute-start.6 = (f32[512,16]{0,1:T(8,128)S(1)}, f32[512,16]{0,1:T(8,128)S(1)}, u32[]{:S(2)}, u32[]{:S(2)}) collective-permute-start(f32[512,16]{0,1:T(8,128)S(1)} %add.98), channel_id=1, source_target_pairs={{0,32},{32,0},{64,96},{96,64},{128,160},{160,128},{192,224},{224,1... | collective-permute-start | bytes 98312 | tf_op jit(solution)/shard_map/ppermute | solution.py:40
  63.0 2.9 %collective-permute-done.6 = f32[512,16]{0,1:T(8,128)S(1)} collective-permute-done((f32[512,16]{0,1:T(8,128)S(1)}, f32[512,16]{0,1:T(8,128)S(1)}, u32[]{:S(2)}, u32[]{:S(2)}) %collective-permute-start.6) | collective-permute-done | bytes 32800 | tf_op jit(solution)/shard_map/ppermute | solution.py:40
  65.9 0.6 add.99
  66.5 0.0 collective-permute-done.2
  66.5 0.0 collective-permute-done.3
  66.5 0.2 fusion
  66.7 0.8 %fusion.4 = (bf16[512,256]{1,0:T(8,128)(2,1)}, bf16[512,256]{1,0:T(8,128)(2,1)}) fusion(bf16[512,512]{1,0:T(8,128)(2,1)S(1)} %fusion), kind=kLoop, calls=%fused_computation.27 | loop fusion | bytes 1048576 | tf_op jit(solution)/shard_map/slice | solution.py:213
  (12 shorter events, 0.2 us)
Async XLA Ops:
  0.6 48.0 %copy-start = (bf16[16,512]{1,0:T(8,128)(2,1)S(1)}, bf16[16,512]{1,0:T(8,128)(2,1)}, u32[]{:S(2)}) copy-start(bf16[16,512]{1,0:T(8,128)(2,1)} %param.10) | copy-start | bytes 49156
  2.6 15.7 %collective-permute-start.1 = (bf16[512,512]{1,0:T(8,128)(2,1)S(1)}, bf16[512,512]{1,0:T(8,128)(2,1)S(1)}, u32[]{:S(2)}, u32[]{:S(2)}) collective-permute-start(bf16[512,512]{1,0:T(8,128)(2,1)S(1)} %constant_dynamic-update-slice_fusion), channel_id=1, source_target_pairs={{0,1},{1,2},{2,3},{3,4},{4,5},{5,6},{6,7},{7,8},{8,9},{9,10},{10,1... | collective-permute-start | bytes 1572872 | tf_op jit(solution)/shard_map/ppermute | solution.py:22
  4.5 18.8 %collective-permute-start = (bf16[512,512]{1,0:T(8,128)(2,1)S(1)}, bf16[512,512]{1,0:T(8,128)(2,1)S(1)}, u32[]{:S(2)}, u32[]{:S(2)}) collective-permute-start(bf16[512,512]{1,0:T(8,128)(2,1)S(1)} %constant_dynamic-update-slice_fusion), channel_id=1, source_target_pairs={{0,2},{1,3},{2,4},{3,5},{4,6},{5,7},{6,8},{7,9},{8,10},{9,11},{10,... | collective-permute-start | bytes 1572872 | tf_op jit(solution)/shard_map/ppermute | solution.py:22
  10.3 13.2 %copy-start.1 = (bf16[512,512]{1,0:T(8,128)(2,1)S(1)}, bf16[512,512]{1,0:T(8,128)(2,1)}, u32[]{:S(2)}) copy-start(bf16[512,512]{1,0:T(8,128)(2,1)} %q_ref.1) | copy-start | bytes 1572868
  10.3 13.2 %copy-start.2 = (bf16[512,512]{1,0:T(8,128)(2,1)S(1)}, bf16[512,512]{1,0:T(8,128)(2,1)}, u32[]{:S(2)}) copy-start(bf16[512,512]{1,0:T(8,128)(2,1)} %do_ref.1) | copy-start | bytes 1572868
  33.9 14.7 %copy-start.3 = (bf16[512,512]{1,0:T(8,128)(2,1)S(1)}, bf16[512,512]{1,0:T(8,128)(2,1)}, u32[]{:S(2)}) copy-start(bf16[512,512]{1,0:T(8,128)(2,1)} %get-tuple-element.5) | copy-start | bytes 1572868
  34.0 32.5 %collective-permute-start.2 = (bf16[512,512]{1,0:T(8,128)(2,1)S(1)}, bf16[512,512]{1,0:T(8,128)(2,1)S(1)}, u32[]{:S(2)}, u32[]{:S(2)}) collective-permute-start(bf16[512,512]{1,0:T(8,128)(2,1)S(1)} %get-tuple-element.13), channel_id=1, source_target_pairs={{1,0},{2,1},{3,2},{4,3},{5,4},{6,5},{7,6},{8,7},{9,8},{10,9},{11,1... | collective-permute-start | bytes 1572872 | tf_op jit(solution)/shard_map/ppermute | solution.py:22
  39.1 27.4 %collective-permute-start.3 = (bf16[512,512]{1,0:T(8,128)(2,1)S(1)}, bf16[512,512]{1,0:T(8,128)(2,1)S(1)}, u32[]{:S(2)}, u32[]{:S(2)}) collective-permute-start(bf16[512,512]{1,0:T(8,128)(2,1)S(1)} %get-tuple-element.14), channel_id=1, source_target_pairs={{2,0},{3,1},{4,2},{5,3},{6,4},{7,5},{8,6},{9,7},{10,8},{11,9},{12,... | collective-permute-start | bytes 1572872 | tf_op jit(solution)/shard_map/ppermute | solution.py:22
  48.8 5.2 %collective-permute-start.4 = (f32[512,16]{0,1:T(8,128)S(1)}, f32[512,16]{0,1:T(8,128)S(1)}, u32[]{:S(2)}, u32[]{:S(2)}) collective-permute-start(f32[512,16]{0,1:T(8,128)S(1)} %fusion.5), channel_id=1, source_target_pairs={{0,64},{32,96},{64,0},{96,32},{128,192},{160,224},{192,128},{224,1... | collective-permute-start | bytes 98312 | tf_op jit(solution)/shard_map/ppermute | solution.py:40
  54.0 7.9 %collective-permute-start.5 = (f32[512,16]{0,1:T(8,128)S(1)}, f32[512,16]{0,1:T(8,128)S(1)}, u32[]{:S(2)}, u32[]{:S(2)}) collective-permute-start(f32[512,16]{0,1:T(8,128)S(1)} %add.97), channel_id=1, source_target_pairs={{0,192},{32,224},{64,128},{96,160},{128,64},{160,96},{192,0},{224,... | collective-permute-start | bytes 98312 | tf_op jit(solution)/shard_map/ppermute | solution.py:40
  62.0 3.9 %collective-permute-start.6 = (f32[512,16]{0,1:T(8,128)S(1)}, f32[512,16]{0,1:T(8,128)S(1)}, u32[]{:S(2)}, u32[]{:S(2)}) collective-permute-start(f32[512,16]{0,1:T(8,128)S(1)} %add.98), channel_id=1, source_target_pairs={{0,32},{32,0},{64,96},{96,64},{128,160},{160,128},{192,224},{224,1... | collective-permute-start | bytes 98312 | tf_op jit(solution)/shard_map/ppermute | solution.py:40

commit v12 on v8

--- a/solution.py
+++ b/solution.py
@@ -37,6 +37,17 @@
         route = [(i, partner[i]) for i in range(len(partner))]
         total = total + lax.ppermute(total, axis, route)
     return total
+
+
+def halo_blocks(joined, axis, hop_count):
+    count = lax.axis_size(axis)
+    near = passed_along(joined, axis, 1)
+    if hop_count != 2 or count % 2:
+        return [near] + [passed_along(joined, axis, hop + 1) for hop in range(1, hop_count)]
+    far_even = lax.ppermute(joined, axis, [(i - 2, i) for i in range(2, count, 2)])
+    far_odd = lax.ppermute(near, axis, [(i, i + 1) for i in range(0, count, 2)])
+    even = lax.rem(lax.axis_index(axis), 2) == 0
+    return [near, jnp.where(even, far_even, far_odd)]
 
 
 def doc_index(positions, doc_ends):
@@ -166,9 +177,7 @@
     lowest = first_pos - WIN
     doc_ends = jnp.cumsum(document_block_counts) * BLK
     joined = jnp.concatenate([key_head_tensor, value_head_tensor], axis=1)
-    arrived = []
-    for hop_num in range(hop_count):
-        arrived.append(passed_along(joined, "ctx", hop_num + 1))
+    arrived = halo_blocks(joined, "ctx", hop_count)
     extended = jnp.concatenate(arrived[::-1] + [joined], axis=0)
     qdoc = doc_index(first_pos + jnp.arange(tokens_here, dtype=jnp.int32), doc_ends)
     kdoc = doc_index(lowest + jnp.arange(WIN + tokens_here, dtype=jnp.int32), doc_ends)

time: 66.2 us -> 62.3 us (0.941)
  waiting for transfers between devices: 18.7 us -> 15.5 us
  starting transfers between devices: 23.3 us -> 21.6 us
  local copies, waits for them, and re-layouts: 3.93 us -> 4.93 us
    ppermute x4 -> x3, starting transfers between devices: 13.3 us -> 6.58 us  [passed_along(): return lax.ppermute(block, axis, route)]
    ppermute x0 -> x2, starting transfers between devices: none -> 4.71 us  [the longest x1 3.4 us: halo_blocks(): lax.ppermute(joined, axis, [(i - 2, i) for i in range(2, count, 2)])]
    ppermute x4 -> x3, waiting for transfers between devices: 11.8 us -> 8.99 us  [passed_along(): return lax.ppermute(block, axis, route)]
    unnamed x9, local copies, waits for them, and re-layouts: 1 us -> 2 us
  transfers between devices with their start and end apart: 7 -> 8, of which waited for: 5 -> 4; matrix products, arithmetic and copies ran while one was open for 7% -> 7% of each run, Pallas kernels for 0% -> 0%
where the time goes in v12:
time: 62.3 us; the launch traced here: 62 us
  starting transfers between devices  21.6 us (35%)
  waiting for transfers between devices  15.5 us (25%)
  Pallas kernels  15.2 us (24%)
  local copies, waits for them, and re-layouts  4.93 us (8%)
  other arithmetic  3.62 us (6%)
  between operations  0.86 us (1%)
    pallas_call x1, Pallas kernels, fused_attention(): pl.pallas_call(attention_kernel, grid=(groups, blocks), in_specs=[pl.Bloc...  15.2 us
    ppermute x3, starting transfers between devices, gathered_sum(): total = total + lax.ppermute(total, axis, route)  10.3 us
    ppermute x3, waiting for transfers between devices, passed_along(): return lax.ppermute(block, axis, route)  8.99 us
    ppermute x3, starting transfers between devices, passed_along(): return lax.ppermute(block, axis, route)  6.58 us
    ppermute x3, waiting for transfers between devices, gathered_sum(): total = total + lax.ppermute(total, axis, route)  6.55 us
    ppermute x1, starting transfers between devices, halo_blocks(): lax.ppermute(joined, axis, [(i - 2, i) for i in range(2, count, 2)])  3.4 us
    select_n x1, other arithmetic, window_bias(): return jnp.where(inside, 0.0, masked_value).astype(jnp.float32)  2.13 us
    unnamed x9, local copies, waits for them, and re-layouts  2 us
  transfers between devices with their start and end apart: 8, of which 4 were waited for; matrix products, arithmetic and copies ran while one was open for 7% of the time, Pallas kernels for 0%

profile of v12, /device:TPU:24, one launch (start us, length us, event | category | flops | bytes accessed | tf_op | source)
XLA Modules:
  0.0 62.0 jit_solution(11549064830804419241)
XLA Ops:
  0.6 0.0 copy-start
  0.6 1.0 %constant_dynamic-update-slice_fusion.1 = bf16[512,512]{1,0:T(8,128)(2,1)S(1)} fusion(bf16[512,256]{1,0:T(8,128)(2,1)} %param.7), kind=kLoop, calls=%fused_computation.18 | loop fusion | bytes 524288
  1.6 1.0 %constant_dynamic-update-slice_fusion = bf16[512,512]{1,0:T(8,128)(2,1)S(1)} fusion(bf16[512,512]{1,0:T(8,128)(2,1)S(1)} %constant_dynamic-update-slice_fusion.1, bf16[512,256]{1,0:T(8,128)(2,1)} %param.8), kind=kLoop, calls=%fused_computation.17 | loop fusion | bytes 524288 | tf_op jit(solution)/shard_map/concatenate | solution.py:179
  2.6 1.9 %collective-permute-start.1 = (bf16[512,512]{1,0:T(8,128)(2,1)S(1)}, bf16[512,512]{1,0:T(8,128)(2,1)S(1)}, u32[]{:S(2)}, u32[]{:S(2)}) collective-permute-start(bf16[512,512]{1,0:T(8,128)(2,1)S(1)} %constant_dynamic-update-slice_fusion), channel_id=1, source_target_pairs={{0,1},{1,2},{2,3},{3,4},{4,5},{5,6},{6,7},{7,8},{8,9},{9,10},{10,1... | collective-permute-start | bytes 1572872 | tf_op jit(solution)/shard_map/ppermute | solution.py:20
  4.5 3.4 %collective-permute-start = (bf16[512,512]{1,0:T(8,128)(2,1)S(1)}, bf16[512,512]{1,0:T(8,128)(2,1)S(1)}, u32[]{:S(2)}, u32[]{:S(2)}) collective-permute-start(bf16[512,512]{1,0:T(8,128)(2,1)S(1)} %constant_dynamic-update-slice_fusion), channel_id=1, source_target_pairs={{0,2},{2,4},{4,6},{6,8},{8,10},{10,12},{12,14},{14,16},{16,18},{18... | collective-permute-start | bytes 1572872 | tf_op jit(solution)/shard_map/ppermute | solution.py:47
  8.0 0.7 %copy.14 = s32[32,1]{1,0:T(8,128)S(1)} copy(s32[32,1]{0,1:T(1,128)} %bitcast.5) | data formatting | bytes 256 | tf_op jit(solution)/shard_map/reshape.64
  8.7 0.1 reduce-window.8
  8.8 0.1 multiply_reduce_fusion
  8.9 0.1 convert_reduce_fusion
  9.0 0.1 convert_reduce_fusion.1
  9.1 0.1 copy.15
  9.3 9.0 %collective-permute-done.1 = bf16[512,512]{1,0:T(8,128)(2,1)S(1)} collective-permute-done((bf16[512,512]{1,0:T(8,128)(2,1)S(1)}, bf16[512,512]{1,0:T(8,128)(2,1)S(1)}, u32[]{:S(2)}, u32[]{:S(2)}) %collective-permute-start.1) | collective-permute-done | bytes 524320 | tf_op jit(solution)/shard_map/ppermute | solution.py:20
  18.3 1.3 %collective-permute-start.2 = (bf16[512,512]{1,0:T(8,128)(2,1)S(1)}, bf16[512,512]{1,0:T(8,128)(2,1)S(1)}, u32[]{:S(2)}, u32[]{:S(2)}) collective-permute-start(bf16[512,512]{1,0:T(8,128)(2,1)S(1)} %collective-permute-done.1), channel_id=1, source_target_pairs={{0,1},{2,3},{4,5},{6,7},{8,9},{10,11},{12,13},{14,15},{16,17},{18,... | collective-permute-start | bytes 1572872 | tf_op jit(solution)/shard_map/ppermute | solution.py:48
  19.6 2.1 %fusion.3.bias_ref = f32[512,1280]{1,0:T(8,128)} fusion(s32[512]{0:T(512)S(1)} %get-tuple-element.17, s32[512]{0:T(512)S(1)} %get-tuple-element.18, pred[512]{0:T(512)(128)(4,1)S(1)} %fusion.9), kind=kLoop, calls=%fused_computation.4 | loop fusion | flops 4587520 | bytes 2626048 | tf_op jit(solution)/shard_map/jit(_where)/select_n | solution.py:160
  21.8 0.0 copy-start.1
  21.8 0.0 copy-start.2
  21.8 0.0 collective-permute-done
  21.8 0.0 collective-permute-done.2
  21.8 0.1 broadcast_select_fusion
  21.8 0.1 pad_maximum_fusion.k_ref.v_ref
  22.0 0.9 %copy-done.1 = bf16[512,512]{1,0:T(8,128)(2,1)S(1)} copy-done((bf16[512,512]{1,0:T(8,128)(2,1)S(1)}, bf16[512,512]{1,0:T(8,128)(2,1)}, u32[]{:S(2)}) %copy-start.1) | copy-done | bytes 524312
  22.8 0.2 copy-done.2
  23.0 15.2 %shard_map.101 = (bf16[512,512]{1,0:T(8,128)(2,1)}, bf16[512,512]{1,0:T(8,128)(2,1)}, f32[1536,256]{1,0:T(8,128)S(1)}, f32[1536,256]{1,0:T(8,128)S(1)}) custom-call(bf16[512,512]{1,0:T(8,128)(2,1)S(1)} %copy-done.1, bf16[1536,512]{1,0:T(8,128)(2,1)S(1)} %pad_maximum_fusion.k_ref.v_ref, bf16[1536,512]{1,0:T(8,128)(2,1)S(1)} %pad_maximum_fusion.k_ref.v_ref, ...), custom_call_target="tpu_custom_call" | custom-call | flops 4026531840 | bytes 6815744 | tf_op jit(solution)/shard_map/pallas_call | solution.py:116
  38.2 0.1 slice.30
  38.2 0.0 copy-start.3
  38.2 0.1 slice.31
  38.3 0.1 maximum_convert_fusion
  38.4 0.1 fusion.10
  38.5 1.9 %collective-permute-start.3 = (bf16[512,512]{1,0:T(8,128)(2,1)S(1)}, bf16[512,512]{1,0:T(8,128)(2,1)S(1)}, u32[]{:S(2)}, u32[]{:S(2)}) collective-permute-start(bf16[512,512]{1,0:T(8,128)(2,1)S(1)} %get-tuple-element.13), channel_id=1, source_target_pairs={{1,0},{2,1},{3,2},{4,3},{5,4},{6,5},{7,6},{8,7},{9,8},{10,9},{11,1... | collective-permute-start | bytes 1572872 | tf_op jit(solution)/shard_map/ppermute | solution.py:20
  40.4 2.7 %collective-permute-start.4 = (bf16[512,512]{1,0:T(8,128)(2,1)S(1)}, bf16[512,512]{1,0:T(8,128)(2,1)S(1)}, u32[]{:S(2)}, u32[]{:S(2)}) collective-permute-start(bf16[512,512]{1,0:T(8,128)(2,1)S(1)} %get-tuple-element.14), channel_id=1, source_target_pairs={{2,0},{3,1},{4,2},{5,3},{6,4},{7,5},{8,6},{9,7},{10,8},{11,9},{12,... | collective-permute-start | bytes 1572872 | tf_op jit(solution)/shard_map/ppermute | solution.py:20
  43.1 0.0 copy-done
  43.2 0.0 copy-done.3
  43.2 0.2 fusion.12
  43.4 3.3 %collective-permute-start.5 = (f32[512,16]{0,1:T(8,128)S(1)}, f32[512,16]{0,1:T(8,128)S(1)}, u32[]{:S(2)}, u32[]{:S(2)}) collective-permute-start(f32[512,16]{0,1:T(8,128)S(1)} %fusion.12), channel_id=1, source_target_pairs={{0,64},{32,96},{64,0},{96,32},{128,192},{160,224},{192,128},{224,1... | collective-permute-start | bytes 98312 | tf_op jit(solution)/shard_map/ppermute | solution.py:38
  46.7 1.9 %collective-permute-done.5 = f32[512,16]{0,1:T(8,128)S(1)} collective-permute-done((f32[512,16]{0,1:T(8,128)S(1)}, f32[512,16]{0,1:T(8,128)S(1)}, u32[]{:S(2)}, u32[]{:S(2)}) %collective-permute-start.5) | collective-permute-done | bytes 32800 | tf_op jit(solution)/shard_map/ppermute | solution.py:38
  48.6 6.0 %collective-permute-start.6 = (f32[512,16]{0,1:T(8,128)S(1)}, f32[512,16]{0,1:T(8,128)S(1)}, u32[]{:S(2)}, u32[]{:S(2)}) collective-permute-start(f32[512,16]{0,1:T(8,128)S(1)} %add.79), channel_id=1, source_target_pairs={{0,192},{32,224},{64,128},{96,160},{128,64},{160,96},{192,0},{224,... | collective-permute-start | bytes 98312 | tf_op jit(solution)/shard_map/ppermute | solution.py:38
  54.5 1.9 %collective-permute-done.6 = f32[512,16]{0,1:T(8,128)S(1)} collective-permute-done((f32[512,16]{0,1:T(8,128)S(1)}, f32[512,16]{0,1:T(8,128)S(1)}, u32[]{:S(2)}, u32[]{:S(2)}) %collective-permute-start.6) | collective-permute-done | bytes 32800 | tf_op jit(solution)/shard_map/ppermute | solution.py:38
  56.4 1.1 %collective-permute-start.7 = (f32[512,16]{0,1:T(8,128)S(1)}, f32[512,16]{0,1:T(8,128)S(1)}, u32[]{:S(2)}, u32[]{:S(2)}) collective-permute-start(f32[512,16]{0,1:T(8,128)S(1)} %add.80), channel_id=1, source_target_pairs={{0,32},{32,0},{64,96},{96,64},{128,160},{160,128},{192,224},{224,1... | collective-permute-start | bytes 98312 | tf_op jit(solution)/shard_map/ppermute | solution.py:38
  57.6 2.8 %collective-permute-done.7 = f32[512,16]{0,1:T(8,128)S(1)} collective-permute-done((f32[512,16]{0,1:T(8,128)S(1)}, f32[512,16]{0,1:T(8,128)S(1)}, u32[]{:S(2)}, u32[]{:S(2)}) %collective-permute-start.7) | collective-permute-done | bytes 32800 | tf_op jit(solution)/shard_map/ppermute | solution.py:38
  60.3 0.6 %add.81 = f32[512,16]{0,1:T(8,128)} add(f32[512,16]{0,1:T(8,128)S(1)} %add.80, f32[512,16]{0,1:T(8,128)S(1)} %collective-permute-done.7) | non-fusion elementwise | flops 8192 | bytes 98304 | tf_op jit(solution)/shard_map/add | solution.py:38
  61.0 0.0 collective-permute-done.3
  61.0 0.0 collective-permute-done.4
  61.0 0.2 fusion.4
  61.2 0.8 %fusion.11 = (bf16[512,256]{1,0:T(8,128)(2,1)}, bf16[512,256]{1,0:T(8,128)(2,1)}) fusion(bf16[512,512]{1,0:T(8,128)(2,1)S(1)} %fusion.4), kind=kLoop, calls=%fused_computation.26 | loop fusion | bytes 1048576 | tf_op jit(solution)/shard_map/slice | solution.py:200
  (10 shorter events, 0.2 us)
Async XLA Ops:
  0.6 42.5 %copy-start = (bf16[16,512]{1,0:T(8,128)(2,1)S(1)}, bf16[16,512]{1,0:T(8,128)(2,1)}, u32[]{:S(2)}) copy-start(bf16[16,512]{1,0:T(8,128)(2,1)} %param.10) | copy-start | bytes 49156
  2.6 15.7 %collective-permute-start.1 = (bf16[512,512]{1,0:T(8,128)(2,1)S(1)}, bf16[512,512]{1,0:T(8,128)(2,1)S(1)}, u32[]{:S(2)}, u32[]{:S(2)}) collective-permute-start(bf16[512,512]{1,0:T(8,128)(2,1)S(1)} %constant_dynamic-update-slice_fusion), channel_id=1, source_target_pairs={{0,1},{1,2},{2,3},{3,4},{4,5},{5,6},{6,7},{7,8},{8,9},{9,10},{10,1... | collective-permute-start | bytes 1572872 | tf_op jit(solution)/shard_map/ppermute | solution.py:20
  4.5 17.2 %collective-permute-start = (bf16[512,512]{1,0:T(8,128)(2,1)S(1)}, bf16[512,512]{1,0:T(8,128)(2,1)S(1)}, u32[]{:S(2)}, u32[]{:S(2)}) collective-permute-start(bf16[512,512]{1,0:T(8,128)(2,1)S(1)} %constant_dynamic-update-slice_fusion), channel_id=1, source_target_pairs={{0,2},{2,4},{4,6},{6,8},{8,10},{10,12},{12,14},{14,16},{16,18},{18... | collective-permute-start | bytes 1572872 | tf_op jit(solution)/shard_map/ppermute | solution.py:47
  18.3 3.5 %collective-permute-start.2 = (bf16[512,512]{1,0:T(8,128)(2,1)S(1)}, bf16[512,512]{1,0:T(8,128)(2,1)S(1)}, u32[]{:S(2)}, u32[]{:S(2)}) collective-permute-start(bf16[512,512]{1,0:T(8,128)(2,1)S(1)} %collective-permute-done.1), channel_id=1, source_target_pairs={{0,1},{2,3},{4,5},{6,7},{8,9},{10,11},{12,13},{14,15},{16,17},{18,... | collective-permute-start | bytes 1572872 | tf_op jit(solution)/shard_map/ppermute | solution.py:48
  21.8 1.0 %copy-start.1 = (bf16[512,512]{1,0:T(8,128)(2,1)S(1)}, bf16[512,512]{1,0:T(8,128)(2,1)}, u32[]{:S(2)}) copy-start(bf16[512,512]{1,0:T(8,128)(2,1)} %q_ref.1) | copy-start | bytes 1572868
  21.8 1.2 %copy-start.2 = (bf16[512,512]{1,0:T(8,128)(2,1)S(1)}, bf16[512,512]{1,0:T(8,128)(2,1)}, u32[]{:S(2)}) copy-start(bf16[512,512]{1,0:T(8,128)(2,1)} %do_ref.1) | copy-start | bytes 1572868
  38.2 4.9 %copy-start.3 = (bf16[512,512]{1,0:T(8,128)(2,1)S(1)}, bf16[512,512]{1,0:T(8,128)(2,1)}, u32[]{:S(2)}) copy-start(bf16[512,512]{1,0:T(8,128)(2,1)} %get-tuple-element.5) | copy-start | bytes 1572868
  38.5 22.5 %collective-permute-start.3 = (bf16[512,512]{1,0:T(8,128)(2,1)S(1)}, bf16[512,512]{1,0:T(8,128)(2,1)S(1)}, u32[]{:S(2)}, u32[]{:S(2)}) collective-permute-start(bf16[512,512]{1,0:T(8,128)(2,1)S(1)} %get-tuple-element.13), channel_id=1, source_target_pairs={{1,0},{2,1},{3,2},{4,3},{5,4},{6,5},{7,6},{8,7},{9,8},{10,9},{11,1... | collective-permute-start | bytes 1572872 | tf_op jit(solution)/shard_map/ppermute | solution.py:20
  40.4 20.6 %collective-permute-start.4 = (bf16[512,512]{1,0:T(8,128)(2,1)S(1)}, bf16[512,512]{1,0:T(8,128)(2,1)S(1)}, u32[]{:S(2)}, u32[]{:S(2)}) collective-permute-start(bf16[512,512]{1,0:T(8,128)(2,1)S(1)} %get-tuple-element.14), channel_id=1, source_target_pairs={{2,0},{3,1},{4,2},{5,3},{6,4},{7,5},{8,6},{9,7},{10,8},{11,9},{12,... | collective-permute-start | bytes 1572872 | tf_op jit(solution)/shard_map/ppermute | solution.py:20
  43.4 5.2 %collective-permute-start.5 = (f32[512,16]{0,1:T(8,128)S(1)}, f32[512,16]{0,1:T(8,128)S(1)}, u32[]{:S(2)}, u32[]{:S(2)}) collective-permute-start(f32[512,16]{0,1:T(8,128)S(1)} %fusion.12), channel_id=1, source_target_pairs={{0,64},{32,96},{64,0},{96,32},{128,192},{160,224},{192,128},{224,1... | collective-permute-start | bytes 98312 | tf_op jit(solution)/shard_map/ppermute | solution.py:38
  48.6 7.8 %collective-permute-start.6 = (f32[512,16]{0,1:T(8,128)S(1)}, f32[512,16]{0,1:T(8,128)S(1)}, u32[]{:S(2)}, u32[]{:S(2)}) collective-permute-start(f32[512,16]{0,1:T(8,128)S(1)} %add.79), channel_id=1, source_target_pairs={{0,192},{32,224},{64,128},{96,160},{128,64},{160,96},{192,0},{224,... | collective-permute-start | bytes 98312 | tf_op jit(solution)/shard_map/ppermute | solution.py:38
  56.4 3.9 %collective-permute-start.7 = (f32[512,16]{0,1:T(8,128)S(1)}, f32[512,16]{0,1:T(8,128)S(1)}, u32[]{:S(2)}, u32[]{:S(2)}) collective-permute-start(f32[512,16]{0,1:T(8,128)S(1)} %add.80), channel_id=1, source_target_pairs={{0,32},{32,0},{64,96},{96,64},{128,160},{160,128},{192,224},{224,1... | collective-permute-start | bytes 98312 | tf_op jit(solution)/shard_map/ppermute | solution.py:38

commit v13 on v10

--- a/solution.py
+++ b/solution.py
@@ -37,6 +37,17 @@
         route = [(i, partner[i]) for i in range(len(partner))]
         total = total + lax.ppermute(total, axis, route)
     return total
+
+
+def halo_blocks(joined, axis, hop_count):
+    count = lax.axis_size(axis)
+    near = passed_along(joined, axis, 1)
+    if hop_count != 2 or count % 2:
+        return [near] + [passed_along(joined, axis, hop + 1) for hop in range(1, hop_count)]
+    far_even = lax.ppermute(joined, axis, [(i - 2, i) for i in range(2, count, 2)])
+    far_odd = lax.ppermute(near, axis, [(i, i + 1) for i in range(0, count, 2)])
+    even = lax.rem(lax.axis_index(axis), 2) == 0
+    return [near, jnp.where(even, far_even, far_odd)]
 
 
 def doc_index(positions, doc_ends):
@@ -160,9 +171,7 @@
     lowest = first_pos - WIN
     doc_ends = jnp.cumsum(document_block_counts) * BLK
     joined = jnp.concatenate([key_head_tensor, value_head_tensor], axis=1)
-    arrived = []
-    for hop_num in range(hop_count):
-        arrived.append(passed_along(joined, "ctx", hop_num + 1))
+    arrived = halo_blocks(joined, "ctx", hop_count)
     extended = jnp.concatenate(arrived[::-1] + [joined], axis=0)
     qdoc = doc_index(first_pos + jnp.arange(tokens_here, dtype=jnp.int32), doc_ends)
     kdoc = doc_index(lowest + jnp.arange(WIN + tokens_here, dtype=jnp.int32), doc_ends)

time: 66.4 us -> 62.8 us (0.946)
  waiting for transfers between devices: 20.9 us -> 17.5 us
  starting transfers between devices: 23.4 us -> 22.1 us
  local copies, waits for them, and re-layouts: 3.94 us -> 5 us
    ppermute x4 -> x3, starting transfers between devices: 13.5 us -> 7.51 us  [passed_along(): return lax.ppermute(block, axis, route)]
    ppermute x4 -> x3, waiting for transfers between devices: 14 us -> 9.2 us  [passed_along(): return lax.ppermute(block, axis, route)]
    ppermute x0 -> x2, starting transfers between devices: none -> 4.71 us  [the longest x1 3.4 us: halo_blocks(): lax.ppermute(joined, axis, [(i - 2, i) for i in range(2, count, 2)])]
    ppermute x0 -> x2, waiting for transfers between devices: none -> 1.31 us  [the longest x1 1.01 us: halo_blocks(): lax.ppermute(joined, axis, [(i - 2, i) for i in range(2, count, 2)])]
    unnamed x9, local copies, waits for them, and re-layouts: 1 us -> 2.07 us
  transfers between devices with their start and end apart: 7 -> 8, of which waited for: 5 -> 6; matrix products, arithmetic and copies ran while one was open for 3% -> 4% of each run, Pallas kernels for 0% -> 0%
where the time goes in v13:
time: 62.8 us; the launch traced here: 62.5 us
  starting transfers between devices  22.1 us (35%)
  waiting for transfers between devices  17.5 us (28%)
  Pallas kernels  15.4 us (25%)
  local copies, waits for them, and re-layouts  5 us (8%)
  other arithmetic  1.49 us (2%)
  between operations  0.83 us (1%)
    pallas_call x1, Pallas kernels, fused_attention(): pl.pallas_call(attention_kernel, grid=(groups, blocks), in_specs=[pl.Bloc...  15.4 us
    ppermute x3, starting transfers between devices, gathered_sum(): total = total + lax.ppermute(total, axis, route)  9.91 us
    ppermute x3, waiting for transfers between devices, passed_along(): return lax.ppermute(block, axis, route)  9.2 us
    ppermute x3, starting transfers between devices, passed_along(): return lax.ppermute(block, axis, route)  7.51 us
    ppermute x3, waiting for transfers between devices, gathered_sum(): total = total + lax.ppermute(total, axis, route)  6.95 us
    ppermute x1, starting transfers between devices, halo_blocks(): lax.ppermute(joined, axis, [(i - 2, i) for i in range(2, count, 2)])  3.4 us
    unnamed x9, local copies, waits for them, and re-layouts  2.07 us
    ppermute x1, starting transfers between devices, halo_blocks(): far_odd = lax.ppermute(near, axis, [(i, i + 1) for i in range(0, count, 2)])  1.31 us
  transfers between devices with their start and end apart: 8, of which 6 were waited for; matrix products, arithmetic and copies ran while one was open for 4% of the time, Pallas kernels for 0%

profile of v13, /device:TPU:24, one launch (start us, length us, event | category | flops | bytes accessed | tf_op | source)
XLA Modules:
  0.0 62.5 jit_solution(16590646321650205969)
XLA Ops:
  0.6 0.0 copy-start
  0.6 1.0 %constant_dynamic-update-slice_fusion.1 = bf16[512,512]{1,0:T(8,128)(2,1)S(1)} fusion(bf16[512,256]{1,0:T(8,128)(2,1)} %param.7), kind=kLoop, calls=%fused_computation.13 | loop fusion | bytes 524288
  1.6 1.0 %constant_dynamic-update-slice_fusion = bf16[512,512]{1,0:T(8,128)(2,1)S(1)} fusion(bf16[512,512]{1,0:T(8,128)(2,1)S(1)} %constant_dynamic-update-slice_fusion.1, bf16[512,256]{1,0:T(8,128)(2,1)} %param.8), kind=kLoop, calls=%fused_computation.12 | loop fusion | bytes 524288 | tf_op jit(solution)/shard_map/concatenate | solution.py:173
  2.6 1.9 %collective-permute-start.1 = (bf16[512,512]{1,0:T(8,128)(2,1)S(1)}, bf16[512,512]{1,0:T(8,128)(2,1)S(1)}, u32[]{:S(2)}, u32[]{:S(2)}) collective-permute-start(bf16[512,512]{1,0:T(8,128)(2,1)S(1)} %constant_dynamic-update-slice_fusion), channel_id=1, source_target_pairs={{0,1},{1,2},{2,3},{3,4},{4,5},{5,6},{6,7},{7,8},{8,9},{9,10},{10,1... | collective-permute-start | bytes 1572872 | tf_op jit(solution)/shard_map/ppermute | solution.py:20
  4.5 3.4 %collective-permute-start = (bf16[512,512]{1,0:T(8,128)(2,1)S(1)}, bf16[512,512]{1,0:T(8,128)(2,1)S(1)}, u32[]{:S(2)}, u32[]{:S(2)}) collective-permute-start(bf16[512,512]{1,0:T(8,128)(2,1)S(1)} %constant_dynamic-update-slice_fusion), channel_id=1, source_target_pairs={{0,2},{2,4},{4,6},{6,8},{8,10},{10,12},{12,14},{14,16},{16,18},{18... | collective-permute-start | bytes 1572872 | tf_op jit(solution)/shard_map/ppermute | solution.py:47
  7.9 0.7 %copy.14 = s32[32,1]{1,0:T(8,128)S(1)} copy(s32[32,1]{0,1:T(1,128)} %bitcast.5) | data formatting | bytes 256 | tf_op jit(solution)/shard_map/reshape.64
  8.7 0.1 reduce-window.8
  8.7 0.1 multiply_reduce_fusion
  8.8 0.1 convert_reduce_fusion.1
  8.9 0.2 copy.15
  9.1 9.2 %collective-permute-done.1 = bf16[512,512]{1,0:T(8,128)(2,1)S(1)} collective-permute-done((bf16[512,512]{1,0:T(8,128)(2,1)S(1)}, bf16[512,512]{1,0:T(8,128)(2,1)S(1)}, u32[]{:S(2)}, u32[]{:S(2)}) %collective-permute-start.1) | collective-permute-done | bytes 524320 | tf_op jit(solution)/shard_map/ppermute | solution.py:20
  18.3 1.3 %collective-permute-start.2 = (bf16[512,512]{1,0:T(8,128)(2,1)S(1)}, bf16[512,512]{1,0:T(8,128)(2,1)S(1)}, u32[]{:S(2)}, u32[]{:S(2)}) collective-permute-start(bf16[512,512]{1,0:T(8,128)(2,1)S(1)} %collective-permute-done.1), channel_id=1, source_target_pairs={{0,1},{2,3},{4,5},{6,7},{8,9},{10,11},{12,13},{14,15},{16,17},{18,... | collective-permute-start | bytes 1572872 | tf_op jit(solution)/shard_map/ppermute | solution.py:48
  19.6 0.1 convert_reduce_fusion
  19.8 1.0 %collective-permute-done = bf16[512,512]{1,0:T(8,128)(2,1)S(1)} collective-permute-done((bf16[512,512]{1,0:T(8,128)(2,1)S(1)}, bf16[512,512]{1,0:T(8,128)(2,1)S(1)}, u32[]{:S(2)}, u32[]{:S(2)}) %collective-permute-start) | collective-permute-done | bytes 524320 | tf_op jit(solution)/shard_map/ppermute | solution.py:47
  20.8 0.3 collective-permute-done.2
  21.1 0.1 broadcast_select_fusion
  21.2 0.0 copy-start.1
  21.2 0.0 copy-start.2
  21.2 0.1 pad_maximum_fusion.k_ref.v_ref
  21.3 0.9 %copy-done.1 = bf16[512,512]{1,0:T(8,128)(2,1)S(1)} copy-done((bf16[512,512]{1,0:T(8,128)(2,1)S(1)}, bf16[512,512]{1,0:T(8,128)(2,1)}, u32[]{:S(2)}) %copy-start.1) | copy-done | bytes 524312
  22.2 0.2 copy-done.2
  22.4 15.4 %shard_map.101 = (bf16[512,512]{1,0:T(8,128)(2,1)}, bf16[512,512]{1,0:T(8,128)(2,1)}, f32[1536,256]{1,0:T(8,128)S(1)}, f32[1536,256]{1,0:T(8,128)S(1)}) custom-call(bf16[512,512]{1,0:T(8,128)(2,1)S(1)} %copy-done.1, bf16[1536,512]{1,0:T(8,128)(2,1)S(1)} %pad_maximum_fusion.k_ref.v_ref, bf16[1536,512]{1,0:T(8,128)(2,1)S(1)} %pad_maximum_fusion.k_ref.v_ref, ...), custom_call_target="tpu_custom_call" | custom-call | flops 4026531840 | bytes 6815744 | tf_op jit(solution)/shard_map/pallas_call | solution.py:120
  37.8 0.1 slice.30
  37.8 0.1 slice.31
  37.9 0.1 maximum_convert_fusion
  38.0 0.0 copy-start.3
  38.0 0.1 fusion.2
  38.1 2.8 %collective-permute-start.3 = (bf16[512,512]{1,0:T(8,128)(2,1)S(1)}, bf16[512,512]{1,0:T(8,128)(2,1)S(1)}, u32[]{:S(2)}, u32[]{:S(2)}) collective-permute-start(bf16[512,512]{1,0:T(8,128)(2,1)S(1)} %get-tuple-element.13), channel_id=1, source_target_pairs={{1,0},{2,1},{3,2},{4,3},{5,4},{6,5},{7,6},{8,7},{9,8},{10,9},{11,1... | collective-permute-start | bytes 1572872 | tf_op jit(solution)/shard_map/ppermute | solution.py:20
  40.9 2.7 %collective-permute-start.4 = (bf16[512,512]{1,0:T(8,128)(2,1)S(1)}, bf16[512,512]{1,0:T(8,128)(2,1)S(1)}, u32[]{:S(2)}, u32[]{:S(2)}) collective-permute-start(bf16[512,512]{1,0:T(8,128)(2,1)S(1)} %get-tuple-element.14), channel_id=1, source_target_pairs={{2,0},{3,1},{4,2},{5,3},{6,4},{7,5},{8,6},{9,7},{10,8},{11,9},{12,... | collective-permute-start | bytes 1572872 | tf_op jit(solution)/shard_map/ppermute | solution.py:20
  43.7 0.0 copy-done
  43.7 0.0 copy-done.3
  43.7 0.2 fusion.4
  43.9 3.3 %collective-permute-start.5 = (f32[512,16]{0,1:T(8,128)S(1)}, f32[512,16]{0,1:T(8,128)S(1)}, u32[]{:S(2)}, u32[]{:S(2)}) collective-permute-start(f32[512,16]{0,1:T(8,128)S(1)} %fusion.4), channel_id=1, source_target_pairs={{0,64},{32,96},{64,0},{96,32},{128,192},{160,224},{192,128},{224,1... | collective-permute-start | bytes 98312 | tf_op jit(solution)/shard_map/ppermute | solution.py:38
  47.2 2.2 %collective-permute-done.5 = f32[512,16]{0,1:T(8,128)S(1)} collective-permute-done((f32[512,16]{0,1:T(8,128)S(1)}, f32[512,16]{0,1:T(8,128)S(1)}, u32[]{:S(2)}, u32[]{:S(2)}) %collective-permute-start.5) | collective-permute-done | bytes 32800 | tf_op jit(solution)/shard_map/ppermute | solution.py:38
  49.5 5.6 %collective-permute-start.6 = (f32[512,16]{0,1:T(8,128)S(1)}, f32[512,16]{0,1:T(8,128)S(1)}, u32[]{:S(2)}, u32[]{:S(2)}) collective-permute-start(f32[512,16]{0,1:T(8,128)S(1)} %add.67), channel_id=1, source_target_pairs={{0,192},{32,224},{64,128},{96,160},{128,64},{160,96},{192,0},{224,... | collective-permute-start | bytes 98312 | tf_op jit(solution)/shard_map/ppermute | solution.py:38
  55.1 1.9 %collective-permute-done.6 = f32[512,16]{0,1:T(8,128)S(1)} collective-permute-done((f32[512,16]{0,1:T(8,128)S(1)}, f32[512,16]{0,1:T(8,128)S(1)}, u32[]{:S(2)}, u32[]{:S(2)}) %collective-permute-start.6) | collective-permute-done | bytes 32800 | tf_op jit(solution)/shard_map/ppermute | solution.py:38
  57.0 1.0 %collective-permute-start.7 = (f32[512,16]{0,1:T(8,128)S(1)}, f32[512,16]{0,1:T(8,128)S(1)}, u32[]{:S(2)}, u32[]{:S(2)}) collective-permute-start(f32[512,16]{0,1:T(8,128)S(1)} %add.68), channel_id=1, source_target_pairs={{0,32},{32,0},{64,96},{96,64},{128,160},{160,128},{192,224},{224,1... | collective-permute-start | bytes 98312 | tf_op jit(solution)/shard_map/ppermute | solution.py:38
  58.0 2.8 %collective-permute-done.7 = f32[512,16]{0,1:T(8,128)S(1)} collective-permute-done((f32[512,16]{0,1:T(8,128)S(1)}, f32[512,16]{0,1:T(8,128)S(1)}, u32[]{:S(2)}, u32[]{:S(2)}) %collective-permute-start.7) | collective-permute-done | bytes 32800 | tf_op jit(solution)/shard_map/ppermute | solution.py:38
  60.9 0.6 add.69
  61.5 0.0 collective-permute-done.3
  61.5 0.0 collective-permute-done.4
  61.5 0.2 fusion
  61.7 0.8 %fusion.3 = (bf16[512,256]{1,0:T(8,128)(2,1)}, bf16[512,256]{1,0:T(8,128)(2,1)}) fusion(bf16[512,512]{1,0:T(8,128)(2,1)S(1)} %fusion), kind=kLoop, calls=%fused_computation.16 | loop fusion | bytes 1048576 | tf_op jit(solution)/shard_map/slice | solution.py:194
  (8 shorter events, 0.1 us)
Async XLA Ops:
  0.6 43.0 %copy-start = (bf16[16,512]{1,0:T(8,128)(2,1)S(1)}, bf16[16,512]{1,0:T(8,128)(2,1)}, u32[]{:S(2)}) copy-start(bf16[16,512]{1,0:T(8,128)(2,1)} %param.10) | copy-start | bytes 49156
  2.6 15.7 %collective-permute-start.1 = (bf16[512,512]{1,0:T(8,128)(2,1)S(1)}, bf16[512,512]{1,0:T(8,128)(2,1)S(1)}, u32[]{:S(2)}, u32[]{:S(2)}) collective-permute-start(bf16[512,512]{1,0:T(8,128)(2,1)S(1)} %constant_dynamic-update-slice_fusion), channel_id=1, source_target_pairs={{0,1},{1,2},{2,3},{3,4},{4,5},{5,6},{6,7},{7,8},{8,9},{9,10},{10,1... | collective-permute-start | bytes 1572872 | tf_op jit(solution)/shard_map/ppermute | solution.py:20
  4.5 16.3 %collective-permute-start = (bf16[512,512]{1,0:T(8,128)(2,1)S(1)}, bf16[512,512]{1,0:T(8,128)(2,1)S(1)}, u32[]{:S(2)}, u32[]{:S(2)}) collective-permute-start(bf16[512,512]{1,0:T(8,128)(2,1)S(1)} %constant_dynamic-update-slice_fusion), channel_id=1, source_target_pairs={{0,2},{2,4},{4,6},{6,8},{8,10},{10,12},{12,14},{14,16},{16,18},{18... | collective-permute-start | bytes 1572872 | tf_op jit(solution)/shard_map/ppermute | solution.py:47
  18.3 2.8 %collective-permute-start.2 = (bf16[512,512]{1,0:T(8,128)(2,1)S(1)}, bf16[512,512]{1,0:T(8,128)(2,1)S(1)}, u32[]{:S(2)}, u32[]{:S(2)}) collective-permute-start(bf16[512,512]{1,0:T(8,128)(2,1)S(1)} %collective-permute-done.1), channel_id=1, source_target_pairs={{0,1},{2,3},{4,5},{6,7},{8,9},{10,11},{12,13},{14,15},{16,17},{18,... | collective-permute-start | bytes 1572872 | tf_op jit(solution)/shard_map/ppermute | solution.py:48
  21.2 1.0 %copy-start.1 = (bf16[512,512]{1,0:T(8,128)(2,1)S(1)}, bf16[512,512]{1,0:T(8,128)(2,1)}, u32[]{:S(2)}) copy-start(bf16[512,512]{1,0:T(8,128)(2,1)} %q_ref.1) | copy-start | bytes 1572868
  21.2 1.2 %copy-start.2 = (bf16[512,512]{1,0:T(8,128)(2,1)S(1)}, bf16[512,512]{1,0:T(8,128)(2,1)}, u32[]{:S(2)}) copy-start(bf16[512,512]{1,0:T(8,128)(2,1)} %do_ref.1) | copy-start | bytes 1572868
  38.0 5.7 %copy-start.3 = (bf16[512,512]{1,0:T(8,128)(2,1)S(1)}, bf16[512,512]{1,0:T(8,128)(2,1)}, u32[]{:S(2)}) copy-start(bf16[512,512]{1,0:T(8,128)(2,1)} %get-tuple-element.5) | copy-start | bytes 1572868
  38.1 23.4 %collective-permute-start.3 = (bf16[512,512]{1,0:T(8,128)(2,1)S(1)}, bf16[512,512]{1,0:T(8,128)(2,1)S(1)}, u32[]{:S(2)}, u32[]{:S(2)}) collective-permute-start(bf16[512,512]{1,0:T(8,128)(2,1)S(1)} %get-tuple-element.13), channel_id=1, source_target_pairs={{1,0},{2,1},{3,2},{4,3},{5,4},{6,5},{7,6},{8,7},{9,8},{10,9},{11,1... | collective-permute-start | bytes 1572872 | tf_op jit(solution)/shard_map/ppermute | solution.py:20
  40.9 20.6 %collective-permute-start.4 = (bf16[512,512]{1,0:T(8,128)(2,1)S(1)}, bf16[512,512]{1,0:T(8,128)(2,1)S(1)}, u32[]{:S(2)}, u32[]{:S(2)}) collective-permute-start(bf16[512,512]{1,0:T(8,128)(2,1)S(1)} %get-tuple-element.14), channel_id=1, source_target_pairs={{2,0},{3,1},{4,2},{5,3},{6,4},{7,5},{8,6},{9,7},{10,8},{11,9},{12,... | collective-permute-start | bytes 1572872 | tf_op jit(solution)/shard_map/ppermute | solution.py:20
  43.9 5.5 %collective-permute-start.5 = (f32[512,16]{0,1:T(8,128)S(1)}, f32[512,16]{0,1:T(8,128)S(1)}, u32[]{:S(2)}, u32[]{:S(2)}) collective-permute-start(f32[512,16]{0,1:T(8,128)S(1)} %fusion.4), channel_id=1, source_target_pairs={{0,64},{32,96},{64,0},{96,32},{128,192},{160,224},{192,128},{224,1... | collective-permute-start | bytes 98312 | tf_op jit(solution)/shard_map/ppermute | solution.py:38
  49.5 7.5 %collective-permute-start.6 = (f32[512,16]{0,1:T(8,128)S(1)}, f32[512,16]{0,1:T(8,128)S(1)}, u32[]{:S(2)}, u32[]{:S(2)}) collective-permute-start(f32[512,16]{0,1:T(8,128)S(1)} %add.67), channel_id=1, source_target_pairs={{0,192},{32,224},{64,128},{96,160},{128,64},{160,96},{192,0},{224,... | collective-permute-start | bytes 98312 | tf_op jit(solution)/shard_map/ppermute | solution.py:38
  57.0 3.9 %collective-permute-start.7 = (f32[512,16]{0,1:T(8,128)S(1)}, f32[512,16]{0,1:T(8,128)S(1)}, u32[]{:S(2)}, u32[]{:S(2)}) collective-permute-start(f32[512,16]{0,1:T(8,128)S(1)} %add.68), channel_id=1, source_target_pairs={{0,32},{32,0},{64,96},{96,64},{128,160},{160,128},{192,224},{224,1... | collective-permute-start | bytes 98312 | tf_op jit(solution)/shard_map/ppermute | solution.py:38

commit v14 on v12

--- a/solution.py
+++ b/solution.py
@@ -21,8 +21,6 @@
 
 
 def pairings(count):
-    if count == 8:
-        return [[i ^ 2 for i in range(8)], [(6 - i) % 8 if i % 2 == 0 else (8 - i) % 8 for i in range(8)], [i ^ 1 for i in range(8)]]
     rounds = []
     stride = 1
     while stride < count:

time: 62.3 us -> 63.2 us (1.014)
  starting transfers between devices: 21.6 us -> 23.3 us
  waiting for transfers between devices: 15.5 us -> 14.8 us
    ppermute x3, starting transfers between devices: 10.3 us -> 12 us  [gathered_sum(): total = total + lax.ppermute(total, axis, route)]
    ppermute x3, waiting for transfers between devices: 6.55 us -> 5.79 us  [gathered_sum(): total = total + lax.ppermute(total, axis, route)]
where the time goes in v14:
time: 63.2 us; the launch traced here: 62.9 us
  starting transfers between devices  23.3 us (37%)
  Pallas kernels  15.2 us (24%)
  waiting for transfers between devices  14.8 us (23%)
  local copies, waits for them, and re-layouts  4.93 us (8%)
  other arithmetic  3.62 us (6%)
  between operations  0.86 us (1%)
    pallas_call x1, Pallas kernels, fused_attention(): pl.pallas_call(attention_kernel, grid=(groups, blocks), in_specs=[pl.Bloc...  15.2 us
    ppermute x3, starting transfers between devices, gathered_sum(): total = total + lax.ppermute(total, axis, route)  12 us
    ppermute x3, waiting for transfers between devices, passed_along(): return lax.ppermute(block, axis, route)  8.99 us
    ppermute x3, starting transfers between devices, passed_along(): return lax.ppermute(block, axis, route)  6.58 us
    ppermute x3, waiting for transfers between devices, gathered_sum(): total = total + lax.ppermute(total, axis, route)  5.79 us
    ppermute x1, starting transfers between devices, halo_blocks(): lax.ppermute(joined, axis, [(i - 2, i) for i in range(2, count, 2)])  3.4 us
    select_n x1, other arithmetic, window_bias(): return jnp.where(inside, 0.0, masked_value).astype(jnp.float32)  2.13 us
    unnamed x9, local copies, waits for them, and re-layouts  2 us
  transfers between devices with their start and end apart: 8, of which 4 were waited for; matrix products, arithmetic and copies ran while one was open for 7% of the time, Pallas kernels for 0%

profile of v14, /device:TPU:24, one launch (start us, length us, event | category | flops | bytes accessed | tf_op | source)
XLA Modules:
  0.0 62.9 jit_solution(8340437118276633527)
XLA Ops:
  0.6 0.0 copy-start
  0.6 1.0 %constant_dynamic-update-slice_fusion.1 = bf16[512,512]{1,0:T(8,128)(2,1)S(1)} fusion(bf16[512,256]{1,0:T(8,128)(2,1)} %param.7), kind=kLoop, calls=%fused_computation.18 | loop fusion | bytes 524288
  1.6 1.0 %constant_dynamic-update-slice_fusion = bf16[512,512]{1,0:T(8,128)(2,1)S(1)} fusion(bf16[512,512]{1,0:T(8,128)(2,1)S(1)} %constant_dynamic-update-slice_fusion.1, bf16[512,256]{1,0:T(8,128)(2,1)} %param.8), kind=kLoop, calls=%fused_computation.17 | loop fusion | bytes 524288 | tf_op jit(solution)/shard_map/concatenate | solution.py:177
  2.6 1.9 %collective-permute-start.1 = (bf16[512,512]{1,0:T(8,128)(2,1)S(1)}, bf16[512,512]{1,0:T(8,128)(2,1)S(1)}, u32[]{:S(2)}, u32[]{:S(2)}) collective-permute-start(bf16[512,512]{1,0:T(8,128)(2,1)S(1)} %constant_dynamic-update-slice_fusion), channel_id=1, source_target_pairs={{0,1},{1,2},{2,3},{3,4},{4,5},{5,6},{6,7},{7,8},{8,9},{9,10},{10,1... | collective-permute-start | bytes 1572872 | tf_op jit(solution)/shard_map/ppermute | solution.py:20
  4.5 3.4 %collective-permute-start = (bf16[512,512]{1,0:T(8,128)(2,1)S(1)}, bf16[512,512]{1,0:T(8,128)(2,1)S(1)}, u32[]{:S(2)}, u32[]{:S(2)}) collective-permute-start(bf16[512,512]{1,0:T(8,128)(2,1)S(1)} %constant_dynamic-update-slice_fusion), channel_id=1, source_target_pairs={{0,2},{2,4},{4,6},{6,8},{8,10},{10,12},{12,14},{14,16},{16,18},{18... | collective-permute-start | bytes 1572872 | tf_op jit(solution)/shard_map/ppermute | solution.py:45
  8.0 0.7 %copy.14 = s32[32,1]{1,0:T(8,128)S(1)} copy(s32[32,1]{0,1:T(1,128)} %bitcast.5) | data formatting | bytes 256 | tf_op jit(solution)/shard_map/reshape.64
  8.7 0.1 reduce-window.8
  8.8 0.1 multiply_reduce_fusion
  8.9 0.1 convert_reduce_fusion
  9.0 0.1 convert_reduce_fusion.1
  9.1 0.1 copy.15
  9.3 9.0 %collective-permute-done.1 = bf16[512,512]{1,0:T(8,128)(2,1)S(1)} collective-permute-done((bf16[512,512]{1,0:T(8,128)(2,1)S(1)}, bf16[512,512]{1,0:T(8,128)(2,1)S(1)}, u32[]{:S(2)}, u32[]{:S(2)}) %collective-permute-start.1) | collective-permute-done | bytes 524320 | tf_op jit(solution)/shard_map/ppermute | solution.py:20
  18.3 1.3 %collective-permute-start.2 = (bf16[512,512]{1,0:T(8,128)(2,1)S(1)}, bf16[512,512]{1,0:T(8,128)(2,1)S(1)}, u32[]{:S(2)}, u32[]{:S(2)}) collective-permute-start(bf16[512,512]{1,0:T(8,128)(2,1)S(1)} %collective-permute-done.1), channel_id=1, source_target_pairs={{0,1},{2,3},{4,5},{6,7},{8,9},{10,11},{12,13},{14,15},{16,17},{18,... | collective-permute-start | bytes 1572872 | tf_op jit(solution)/shard_map/ppermute | solution.py:46
  19.6 2.1 %fusion.3.bias_ref = f32[512,1280]{1,0:T(8,128)} fusion(s32[512]{0:T(512)S(1)} %get-tuple-element.17, s32[512]{0:T(512)S(1)} %get-tuple-element.18, pred[512]{0:T(512)(128)(4,1)S(1)} %fusion.9), kind=kLoop, calls=%fused_computation.4 | loop fusion | flops 4587520 | bytes 2626048 | tf_op jit(solution)/shard_map/jit(_where)/select_n | solution.py:158
  21.8 0.0 copy-start.1
  21.8 0.0 copy-start.2
  21.8 0.0 collective-permute-done
  21.8 0.0 collective-permute-done.2
  21.8 0.1 broadcast_select_fusion
  21.8 0.1 pad_maximum_fusion.k_ref.v_ref
  22.0 0.9 %copy-done.1 = bf16[512,512]{1,0:T(8,128)(2,1)S(1)} copy-done((bf16[512,512]{1,0:T(8,128)(2,1)S(1)}, bf16[512,512]{1,0:T(8,128)(2,1)}, u32[]{:S(2)}) %copy-start.1) | copy-done | bytes 524312
  22.8 0.2 copy-done.2
  23.0 15.2 %shard_map.101 = (bf16[512,512]{1,0:T(8,128)(2,1)}, bf16[512,512]{1,0:T(8,128)(2,1)}, f32[1536,256]{1,0:T(8,128)S(1)}, f32[1536,256]{1,0:T(8,128)S(1)}) custom-call(bf16[512,512]{1,0:T(8,128)(2,1)S(1)} %copy-done.1, bf16[1536,512]{1,0:T(8,128)(2,1)S(1)} %pad_maximum_fusion.k_ref.v_ref, bf16[1536,512]{1,0:T(8,128)(2,1)S(1)} %pad_maximum_fusion.k_ref.v_ref, ...), custom_call_target="tpu_custom_call" | custom-call | flops 4026531840 | bytes 6815744 | tf_op jit(solution)/shard_map/pallas_call | solution.py:114
  38.2 0.1 slice.30
  38.2 0.0 copy-start.3
  38.2 0.1 slice.31
  38.3 0.1 maximum_convert_fusion
  38.4 0.1 fusion.10
  38.5 1.9 %collective-permute-start.3 = (bf16[512,512]{1,0:T(8,128)(2,1)S(1)}, bf16[512,512]{1,0:T(8,128)(2,1)S(1)}, u32[]{:S(2)}, u32[]{:S(2)}) collective-permute-start(bf16[512,512]{1,0:T(8,128)(2,1)S(1)} %get-tuple-element.13), channel_id=1, source_target_pairs={{1,0},{2,1},{3,2},{4,3},{5,4},{6,5},{7,6},{8,7},{9,8},{10,9},{11,1... | collective-permute-start | bytes 1572872 | tf_op jit(solution)/shard_map/ppermute | solution.py:20
  40.4 2.7 %collective-permute-start.4 = (bf16[512,512]{1,0:T(8,128)(2,1)S(1)}, bf16[512,512]{1,0:T(8,128)(2,1)S(1)}, u32[]{:S(2)}, u32[]{:S(2)}) collective-permute-start(bf16[512,512]{1,0:T(8,128)(2,1)S(1)} %get-tuple-element.14), channel_id=1, source_target_pairs={{2,0},{3,1},{4,2},{5,3},{6,4},{7,5},{8,6},{9,7},{10,8},{11,9},{12,... | collective-permute-start | bytes 1572872 | tf_op jit(solution)/shard_map/ppermute | solution.py:20
  43.1 0.0 copy-done
  43.2 0.0 copy-done.3
  43.2 0.2 fusion.12
  43.4 1.9 %collective-permute-start.5 = (f32[512,16]{0,1:T(8,128)S(1)}, f32[512,16]{0,1:T(8,128)S(1)}, u32[]{:S(2)}, u32[]{:S(2)}) collective-permute-start(f32[512,16]{0,1:T(8,128)S(1)} %fusion.12), channel_id=1, source_target_pairs={{0,32},{32,0},{64,96},{96,64},{128,160},{160,128},{192,224},{224,1... | collective-permute-start | bytes 98312 | tf_op jit(solution)/shard_map/ppermute | solution.py:36
  45.3 2.0 %collective-permute-done.5 = f32[512,16]{0,1:T(8,128)S(1)} collective-permute-done((f32[512,16]{0,1:T(8,128)S(1)}, f32[512,16]{0,1:T(8,128)S(1)}, u32[]{:S(2)}, u32[]{:S(2)}) %collective-permute-start.5) | collective-permute-done | bytes 32800 | tf_op jit(solution)/shard_map/ppermute | solution.py:36
  47.3 3.3 %collective-permute-start.6 = (f32[512,16]{0,1:T(8,128)S(1)}, f32[512,16]{0,1:T(8,128)S(1)}, u32[]{:S(2)}, u32[]{:S(2)}) collective-permute-start(f32[512,16]{0,1:T(8,128)S(1)} %add.79), channel_id=1, source_target_pairs={{0,64},{32,96},{64,0},{96,32},{128,192},{160,224},{192,128},{224,1... | collective-permute-start | bytes 98312 | tf_op jit(solution)/shard_map/ppermute | solution.py:36
  50.6 2.0 %collective-permute-done.6 = f32[512,16]{0,1:T(8,128)S(1)} collective-permute-done((f32[512,16]{0,1:T(8,128)S(1)}, f32[512,16]{0,1:T(8,128)S(1)}, u32[]{:S(2)}, u32[]{:S(2)}) %collective-permute-start.6) | collective-permute-done | bytes 32800 | tf_op jit(solution)/shard_map/ppermute | solution.py:36
  52.6 6.8 %collective-permute-start.7 = (f32[512,16]{0,1:T(8,128)S(1)}, f32[512,16]{0,1:T(8,128)S(1)}, u32[]{:S(2)}, u32[]{:S(2)}) collective-permute-start(f32[512,16]{0,1:T(8,128)S(1)} %add.80), channel_id=1, source_target_pairs={{0,128},{32,160},{64,192},{96,224},{128,0},{160,32},{192,64},{224,... | collective-permute-start | bytes 98312 | tf_op jit(solution)/shard_map/ppermute | solution.py:36
  59.4 1.8 %collective-permute-done.7 = f32[512,16]{0,1:T(8,128)S(1)} collective-permute-done((f32[512,16]{0,1:T(8,128)S(1)}, f32[512,16]{0,1:T(8,128)S(1)}, u32[]{:S(2)}, u32[]{:S(2)}) %collective-permute-start.7) | collective-permute-done | bytes 32800 | tf_op jit(solution)/shard_map/ppermute | solution.py:36
  61.3 0.6 add.81
  61.9 0.0 collective-permute-done.3
  61.9 0.0 collective-permute-done.4
  61.9 0.2 fusion.4
  62.1 0.8 %fusion.11 = (bf16[512,256]{1,0:T(8,128)(2,1)}, bf16[512,256]{1,0:T(8,128)(2,1)}) fusion(bf16[512,512]{1,0:T(8,128)(2,1)S(1)} %fusion.4), kind=kLoop, calls=%fused_computation.26 | loop fusion | bytes 1048576 | tf_op jit(solution)/shard_map/slice | solution.py:198
  (10 shorter events, 0.2 us)
Async XLA Ops:
  0.6 42.5 %copy-start = (bf16[16,512]{1,0:T(8,128)(2,1)S(1)}, bf16[16,512]{1,0:T(8,128)(2,1)}, u32[]{:S(2)}) copy-start(bf16[16,512]{1,0:T(8,128)(2,1)} %param.10) | copy-start | bytes 49156
  2.6 15.7 %collective-permute-start.1 = (bf16[512,512]{1,0:T(8,128)(2,1)S(1)}, bf16[512,512]{1,0:T(8,128)(2,1)S(1)}, u32[]{:S(2)}, u32[]{:S(2)}) collective-permute-start(bf16[512,512]{1,0:T(8,128)(2,1)S(1)} %constant_dynamic-update-slice_fusion), channel_id=1, source_target_pairs={{0,1},{1,2},{2,3},{3,4},{4,5},{5,6},{6,7},{7,8},{8,9},{9,10},{10,1... | collective-permute-start | bytes 1572872 | tf_op jit(solution)/shard_map/ppermute | solution.py:20
  4.5 17.2 %collective-permute-start = (bf16[512,512]{1,0:T(8,128)(2,1)S(1)}, bf16[512,512]{1,0:T(8,128)(2,1)S(1)}, u32[]{:S(2)}, u32[]{:S(2)}) collective-permute-start(bf16[512,512]{1,0:T(8,128)(2,1)S(1)} %constant_dynamic-update-slice_fusion), channel_id=1, source_target_pairs={{0,2},{2,4},{4,6},{6,8},{8,10},{10,12},{12,14},{14,16},{16,18},{18... | collective-permute-start | bytes 1572872 | tf_op jit(solution)/shard_map/ppermute | solution.py:45
  18.3 3.5 %collective-permute-start.2 = (bf16[512,512]{1,0:T(8,128)(2,1)S(1)}, bf16[512,512]{1,0:T(8,128)(2,1)S(1)}, u32[]{:S(2)}, u32[]{:S(2)}) collective-permute-start(bf16[512,512]{1,0:T(8,128)(2,1)S(1)} %collective-permute-done.1), channel_id=1, source_target_pairs={{0,1},{2,3},{4,5},{6,7},{8,9},{10,11},{12,13},{14,15},{16,17},{18,... | collective-permute-start | bytes 1572872 | tf_op jit(solution)/shard_map/ppermute | solution.py:46
  21.8 1.0 %copy-start.1 = (bf16[512,512]{1,0:T(8,128)(2,1)S(1)}, bf16[512,512]{1,0:T(8,128)(2,1)}, u32[]{:S(2)}) copy-start(bf16[512,512]{1,0:T(8,128)(2,1)} %q_ref.1) | copy-start | bytes 1572868
  21.8 1.2 %copy-start.2 = (bf16[512,512]{1,0:T(8,128)(2,1)S(1)}, bf16[512,512]{1,0:T(8,128)(2,1)}, u32[]{:S(2)}) copy-start(bf16[512,512]{1,0:T(8,128)(2,1)} %do_ref.1) | copy-start | bytes 1572868
  38.2 4.9 %copy-start.3 = (bf16[512,512]{1,0:T(8,128)(2,1)S(1)}, bf16[512,512]{1,0:T(8,128)(2,1)}, u32[]{:S(2)}) copy-start(bf16[512,512]{1,0:T(8,128)(2,1)} %get-tuple-element.5) | copy-start | bytes 1572868
  38.5 23.4 %collective-permute-start.3 = (bf16[512,512]{1,0:T(8,128)(2,1)S(1)}, bf16[512,512]{1,0:T(8,128)(2,1)S(1)}, u32[]{:S(2)}, u32[]{:S(2)}) collective-permute-start(bf16[512,512]{1,0:T(8,128)(2,1)S(1)} %get-tuple-element.13), channel_id=1, source_target_pairs={{1,0},{2,1},{3,2},{4,3},{5,4},{6,5},{7,6},{8,7},{9,8},{10,9},{11,1... | collective-permute-start | bytes 1572872 | tf_op jit(solution)/shard_map/ppermute | solution.py:20
  40.4 21.5 %collective-permute-start.4 = (bf16[512,512]{1,0:T(8,128)(2,1)S(1)}, bf16[512,512]{1,0:T(8,128)(2,1)S(1)}, u32[]{:S(2)}, u32[]{:S(2)}) collective-permute-start(bf16[512,512]{1,0:T(8,128)(2,1)S(1)} %get-tuple-element.14), channel_id=1, source_target_pairs={{2,0},{3,1},{4,2},{5,3},{6,4},{7,5},{8,6},{9,7},{10,8},{11,9},{12,... | collective-permute-start | bytes 1572872 | tf_op jit(solution)/shard_map/ppermute | solution.py:20
  43.4 3.9 %collective-permute-start.5 = (f32[512,16]{0,1:T(8,128)S(1)}, f32[512,16]{0,1:T(8,128)S(1)}, u32[]{:S(2)}, u32[]{:S(2)}) collective-permute-start(f32[512,16]{0,1:T(8,128)S(1)} %fusion.12), channel_id=1, source_target_pairs={{0,32},{32,0},{64,96},{96,64},{128,160},{160,128},{192,224},{224,1... | collective-permute-start | bytes 98312 | tf_op jit(solution)/shard_map/ppermute | solution.py:36
  47.3 5.2 %collective-permute-start.6 = (f32[512,16]{0,1:T(8,128)S(1)}, f32[512,16]{0,1:T(8,128)S(1)}, u32[]{:S(2)}, u32[]{:S(2)}) collective-permute-start(f32[512,16]{0,1:T(8,128)S(1)} %add.79), channel_id=1, source_target_pairs={{0,64},{32,96},{64,0},{96,32},{128,192},{160,224},{192,128},{224,1... | collective-permute-start | bytes 98312 | tf_op jit(solution)/shard_map/ppermute | solution.py:36
  52.6 8.7 %collective-permute-start.7 = (f32[512,16]{0,1:T(8,128)S(1)}, f32[512,16]{0,1:T(8,128)S(1)}, u32[]{:S(2)}, u32[]{:S(2)}) collective-permute-start(f32[512,16]{0,1:T(8,128)S(1)} %add.80), channel_id=1, source_target_pairs={{0,128},{32,160},{64,192},{96,224},{128,0},{160,32},{192,64},{224,... | collective-permute-start | bytes 98312 | tf_op jit(solution)/shard_map/ppermute | solution.py:36

commit v15 on v12

--- a/solution.py
+++ b/solution.py
@@ -143,7 +143,7 @@
         ],
         compiler_params=pltpu.CompilerParams(
             dimension_semantics=("arbitrary", "arbitrary"),
-            vmem_limit_bytes=48 * 1024 * 1024,
+            vmem_limit_bytes=62 * 1024 * 1024,
         ),
         cost_estimate=pl.CostEstimate(
             flops=flops, transcendentals=groups * blocks * 2 * rows * span,

time: 62.3 us -> 66 us (1.059)
  local copies, waits for them, and re-layouts: 4.93 us -> 8.5 us
  waiting for transfers between devices: 15.5 us -> 12.2 us
  other arithmetic: 3.62 us -> 6.08 us
  Pallas kernels: 15.2 us -> 16 us
    slice x2, local copies, waits for them, and re-layouts: 0.11 us -> 2.61 us  [body(): halo_grads = jnp.concatenate([key_grads[:WIN], value_grads[:WIN]], axis=1)]
    slice x2, local copies, waits for them, and re-layouts: 0.07 us -> 2.15 us  [body(): own = jnp.concatenate([key_grads[WIN:], value_grads[WIN:]], axis=1)]
    ppermute x3, waiting for transfers between devices: 6.55 us -> 4.52 us  [gathered_sum(): total = total + lax.ppermute(total, axis, route)]
    select_n x2, other arithmetic: 0.05 us -> 1.35 us  [doc_index(): return jnp.where(positions < 0, -1, counted)]
    ppermute x3, waiting for transfers between devices: 8.99 us -> 7.71 us  [passed_along(): return lax.ppermute(block, axis, route)]
    concatenate x1, other arithmetic: 0.1 us -> 1.25 us  [body(): extended = jnp.concatenate(arrived[::-1] + [joined], axis=0)]
    unnamed x9 -> x5, local copies, waits for them, and re-layouts: 2 us -> 0.99 us
    pallas_call x1, Pallas kernels: 15.2 us -> 16 us  [fused_attention(): pl.pallas_call(attention_kernel, grid=(groups, blocks), in_specs=[pl.Bloc...]
  transfers between devices with their start and end apart: 8 -> 8, of which waited for: 4 -> 4; matrix products, arithmetic and copies ran while one was open for 7% -> 12% of each run, Pallas kernels for 0% -> 0%
where the time goes in v15:
time: 66 us; the launch traced here: 65.5 us
  starting transfers between devices  21.7 us (33%)
  Pallas kernels  16 us (24%)
  waiting for transfers between devices  12.2 us (18%)
  local copies, waits for them, and re-layouts  8.5 us (13%)
  other arithmetic  6.08 us (9%)
  between operations  0.82 us (1%)
    pallas_call x1, Pallas kernels, fused_attention(): pl.pallas_call(attention_kernel, grid=(groups, blocks), in_specs=[pl.Bloc...  16 us
    ppermute x3, starting transfers between devices, gathered_sum(): total = total + lax.ppermute(total, axis, route)  10.3 us
    ppermute x3, waiting for transfers between devices, passed_along(): return lax.ppermute(block, axis, route)  7.71 us
    ppermute x3, starting transfers between devices, passed_along(): return lax.ppermute(block, axis, route)  6.71 us
    ppermute x3, waiting for transfers between devices, gathered_sum(): total = total + lax.ppermute(total, axis, route)  4.52 us
    ppermute x1, starting transfers between devices, halo_blocks(): lax.ppermute(joined, axis, [(i - 2, i) for i in range(2, count, 2)])  3.4 us
    slice x2, local copies, waits for them, and re-layouts, body(): halo_grads = jnp.concatenate([key_grads[:WIN], value_grads[:WIN]], axis=1)  2.61 us
    slice x2, local copies, waits for them, and re-layouts, body(): own = jnp.concatenate([key_grads[WIN:], value_grads[WIN:]], axis=1)  2.15 us
  transfers between devices with their start and end apart: 8, of which 4 were waited for; matrix products, arithmetic and copies ran while one was open for 12% of the time, Pallas kernels for 0%

profile of v15, /device:TPU:24, one launch (start us, length us, event | category | flops | bytes accessed | tf_op | source)
XLA Modules:
  0.0 65.5 jit_solution(11619352903908363974)
XLA Ops:
  0.6 0.0 copy-start
  0.6 1.0 %constant_dynamic-update-slice_fusion.1 = bf16[512,512]{1,0:T(8,128)(2,1)S(1)} fusion(bf16[512,256]{1,0:T(8,128)(2,1)} %param.7), kind=kLoop, calls=%fused_computation.18 | loop fusion | bytes 524288
  1.6 1.0 %constant_dynamic-update-slice_fusion = bf16[512,512]{1,0:T(8,128)(2,1)S(1)} fusion(bf16[512,512]{1,0:T(8,128)(2,1)S(1)} %constant_dynamic-update-slice_fusion.1, bf16[512,256]{1,0:T(8,128)(2,1)} %param.8), kind=kLoop, calls=%fused_computation.17 | loop fusion | bytes 524288 | tf_op jit(solution)/shard_map/concatenate | solution.py:179
  2.6 1.9 %collective-permute-start.1 = (bf16[512,512]{1,0:T(8,128)(2,1)S(1)}, bf16[512,512]{1,0:T(8,128)(2,1)S(1)}, u32[]{:S(2)}, u32[]{:S(2)}) collective-permute-start(bf16[512,512]{1,0:T(8,128)(2,1)S(1)} %constant_dynamic-update-slice_fusion), channel_id=1, source_target_pairs={{0,1},{1,2},{2,3},{3,4},{4,5},{5,6},{6,7},{7,8},{8,9},{9,10},{10,1... | collective-permute-start | bytes 1572872 | tf_op jit(solution)/shard_map/ppermute | solution.py:20
  4.5 3.4 %collective-permute-start = (bf16[512,512]{1,0:T(8,128)(2,1)S(1)}, bf16[512,512]{1,0:T(8,128)(2,1)S(1)}, u32[]{:S(2)}, u32[]{:S(2)}) collective-permute-start(bf16[512,512]{1,0:T(8,128)(2,1)S(1)} %constant_dynamic-update-slice_fusion), channel_id=1, source_target_pairs={{0,2},{2,4},{4,6},{6,8},{8,10},{10,12},{12,14},{14,16},{16,18},{18... | collective-permute-start | bytes 1572872 | tf_op jit(solution)/shard_map/ppermute | solution.py:47
  8.0 0.7 %copy.14 = s32[32,1]{1,0:T(8,128)S(1)} copy(s32[32,1]{0,1:T(1,128)} %bitcast.5) | data formatting | bytes 256 | tf_op jit(solution)/shard_map/reshape.64
  8.7 0.1 reduce-window.8
  8.8 0.1 multiply_reduce_fusion
  8.9 0.1 convert_reduce_fusion
  9.0 0.1 convert_reduce_fusion.1
  9.1 0.1 copy.15
  9.3 0.6 compare_select_fusion.kdoc_ref
  9.9 0.7 %fusion.5.qdoc_ref = s32[512,1]{1,0:T(8,128)} fusion(s32[512,1]{1,0:T(8,128)S(1)} %copy.15, s32[]{:T(128)S(6)} %mul.16), kind=kLoop, calls=%fused_computation.11 | loop fusion | flops 1536 | bytes 4100 | tf_op jit(solution)/shard_map/jit(_where)/select_n | solution.py:55
  10.6 7.7 %collective-permute-done.1 = bf16[512,512]{1,0:T(8,128)(2,1)S(1)} collective-permute-done((bf16[512,512]{1,0:T(8,128)(2,1)S(1)}, bf16[512,512]{1,0:T(8,128)(2,1)S(1)}, u32[]{:S(2)}, u32[]{:S(2)}) %collective-permute-start.1) | collective-permute-done | bytes 524320 | tf_op jit(solution)/shard_map/ppermute | solution.py:20
  18.3 1.3 %collective-permute-start.2 = (bf16[512,512]{1,0:T(8,128)(2,1)S(1)}, bf16[512,512]{1,0:T(8,128)(2,1)S(1)}, u32[]{:S(2)}, u32[]{:S(2)}) collective-permute-start(bf16[512,512]{1,0:T(8,128)(2,1)S(1)} %collective-permute-done.1), channel_id=1, source_target_pairs={{0,1},{2,3},{4,5},{6,7},{8,9},{10,11},{12,13},{14,15},{16,17},{18,... | collective-permute-start | bytes 1572872 | tf_op jit(solution)/shard_map/ppermute | solution.py:48
  19.6 2.1 %fusion.3.bias_ref = f32[512,1280]{1,0:T(8,128)} fusion(s32[512]{0:T(512)S(1)} %get-tuple-element.17, s32[512]{0:T(512)S(1)} %get-tuple-element.18, pred[512]{0:T(512)(128)(4,1)S(1)} %fusion.9), kind=kLoop, calls=%fused_computation.4 | loop fusion | flops 4587520 | bytes 2626048 | tf_op jit(solution)/shard_map/jit(_where)/select_n | solution.py:160
  21.8 0.0 collective-permute-done
  21.8 0.0 collective-permute-done.2
  21.8 0.1 broadcast_select_fusion
  21.8 1.3 %pad_maximum_fusion.k_ref.v_ref = bf16[1536,512]{1,0:T(8,128)(2,1)} fusion(bf16[512,512]{1,0:T(8,128)(2,1)S(1)} %constant_dynamic-update-slice_fusion, bf16[512,512]{1,0:T(8,128)(2,1)S(1)} %collective-permute-done.1, bf16[512,512]{1,0:T(8,128)(2,1)S(1)} %broadcast_select_fusion), kind=kLoop, calls=%fused_computation.6 | loop fusion | flops 4718592 | bytes 3145728 | tf_op jit(solution)/shard_map/concatenate | solution.py:181
  23.1 16.0 %shard_map.101 = (bf16[512,512]{1,0:T(8,128)(2,1)}, bf16[512,512]{1,0:T(8,128)(2,1)}, f32[1536,256]{1,0:T(8,128)}, f32[1536,256]{1,0:T(8,128)}) custom-call(bf16[512,512]{1,0:T(8,128)(2,1)} %q_ref.1, bf16[1536,512]{1,0:T(8,128)(2,1)} %pad_maximum_fusion.k_ref.v_ref, bf16[1536,512]{1,0:T(8,128)(2,1)} %pad_maximum_fusion.k_ref.v_ref, bf16[512,512]{1,0:T(8,128)(2,1)} %do_ref.1, ...), custom_call_target="tpu_custom_call" | custom-call | flops 4026531840 | bytes 6815744 | tf_op jit(solution)/shard_map/pallas_call | solution.py:116
  39.1 1.3 %slice.30 = bf16[1024,256]{1,0:T(8,128)(2,1)S(1)} slice(f32[1536,256]{1,0:T(8,128)} %get-tuple-element.11), slice={[0:1024], [0:256]} | slice | bytes 1048576 | tf_op jit(solution)/shard_map/slice | solution.py:187
  40.3 0.0 copy-start.1
  40.4 1.3 %slice.31 = bf16[1024,256]{1,0:T(8,128)(2,1)S(1)} slice(f32[1536,256]{1,0:T(8,128)} %get-tuple-element.12), slice={[0:1024], [0:256]} | slice | bytes 1048576 | tf_op jit(solution)/shard_map/slice | solution.py:187
  41.7 0.1 maximum_convert_fusion
  41.8 0.1 fusion.10
  41.9 2.1 %collective-permute-start.3 = (bf16[512,512]{1,0:T(8,128)(2,1)S(1)}, bf16[512,512]{1,0:T(8,128)(2,1)S(1)}, u32[]{:S(2)}, u32[]{:S(2)}) collective-permute-start(bf16[512,512]{1,0:T(8,128)(2,1)S(1)} %get-tuple-element.13), channel_id=1, source_target_pairs={{1,0},{2,1},{3,2},{4,3},{5,4},{6,5},{7,6},{8,7},{9,8},{10,9},{11,1... | collective-permute-start | bytes 1572872 | tf_op jit(solution)/shard_map/ppermute | solution.py:20
  43.9 2.7 %collective-permute-start.4 = (bf16[512,512]{1,0:T(8,128)(2,1)S(1)}, bf16[512,512]{1,0:T(8,128)(2,1)S(1)}, u32[]{:S(2)}, u32[]{:S(2)}) collective-permute-start(bf16[512,512]{1,0:T(8,128)(2,1)S(1)} %get-tuple-element.14), channel_id=1, source_target_pairs={{2,0},{3,1},{4,2},{5,3},{6,4},{7,5},{8,6},{9,7},{10,8},{11,9},{12,... | collective-permute-start | bytes 1572872 | tf_op jit(solution)/shard_map/ppermute | solution.py:20
  46.7 0.0 copy-done
  46.7 0.0 copy-done.1
  46.7 0.2 fusion.12
  46.9 3.3 %collective-permute-start.5 = (f32[512,16]{0,1:T(8,128)S(1)}, f32[512,16]{0,1:T(8,128)S(1)}, u32[]{:S(2)}, u32[]{:S(2)}) collective-permute-start(f32[512,16]{0,1:T(8,128)S(1)} %fusion.12), channel_id=1, source_target_pairs={{0,64},{32,96},{64,0},{96,32},{128,192},{160,224},{192,128},{224,1... | collective-permute-start | bytes 98312 | tf_op jit(solution)/shard_map/ppermute | solution.py:38
  50.2 1.9 %collective-permute-done.5 = f32[512,16]{0,1:T(8,128)S(1)} collective-permute-done((f32[512,16]{0,1:T(8,128)S(1)}, f32[512,16]{0,1:T(8,128)S(1)}, u32[]{:S(2)}, u32[]{:S(2)}) %collective-permute-start.5) | collective-permute-done | bytes 32800 | tf_op jit(solution)/shard_map/ppermute | solution.py:38
  52.1 6.0 %collective-permute-start.6 = (f32[512,16]{0,1:T(8,128)S(1)}, f32[512,16]{0,1:T(8,128)S(1)}, u32[]{:S(2)}, u32[]{:S(2)}) collective-permute-start(f32[512,16]{0,1:T(8,128)S(1)} %add.79), channel_id=1, source_target_pairs={{0,192},{32,224},{64,128},{96,160},{128,64},{160,96},{192,0},{224,... | collective-permute-start | bytes 98312 | tf_op jit(solution)/shard_map/ppermute | solution.py:38
  58.1 1.9 %collective-permute-done.6 = f32[512,16]{0,1:T(8,128)S(1)} collective-permute-done((f32[512,16]{0,1:T(8,128)S(1)}, f32[512,16]{0,1:T(8,128)S(1)}, u32[]{:S(2)}, u32[]{:S(2)}) %collective-permute-start.6) | collective-permute-done | bytes 32800 | tf_op jit(solution)/shard_map/ppermute | solution.py:38
  60.0 1.0 %collective-permute-start.7 = (f32[512,16]{0,1:T(8,128)S(1)}, f32[512,16]{0,1:T(8,128)S(1)}, u32[]{:S(2)}, u32[]{:S(2)}) collective-permute-start(f32[512,16]{0,1:T(8,128)S(1)} %add.80), channel_id=1, source_target_pairs={{0,32},{32,0},{64,96},{96,64},{128,160},{160,128},{192,224},{224,1... | collective-permute-start | bytes 98312 | tf_op jit(solution)/shard_map/ppermute | solution.py:38
  61.0 1.1 %slice.28 = f32[512,256]{1,0:T(8,128)S(1)} slice(f32[1536,256]{1,0:T(8,128)} %get-tuple-element.11), slice={[1024:1536], [0:256]} | slice | bytes 1048576 | tf_op jit(solution)/shard_map/slice | solution.py:197
  62.1 1.1 %slice.29 = f32[512,256]{1,0:T(8,128)S(1)} slice(f32[1536,256]{1,0:T(8,128)} %get-tuple-element.12), slice={[1024:1536], [0:256]} | slice | bytes 1048576 | tf_op jit(solution)/shard_map/slice | solution.py:197
  63.1 0.7 %collective-permute-done.7 = f32[512,16]{0,1:T(8,128)S(1)} collective-permute-done((f32[512,16]{0,1:T(8,128)S(1)}, f32[512,16]{0,1:T(8,128)S(1)}, u32[]{:S(2)}, u32[]{:S(2)}) %collective-permute-start.7) | collective-permute-done | bytes 32800 | tf_op jit(solution)/shard_map/ppermute | solution.py:38
  63.9 0.6 add.81
  64.5 0.0 collective-permute-done.3
  64.5 0.0 collective-permute-done.4
  64.5 0.2 fusion.4
  64.7 0.8 %fusion.11 = (bf16[512,256]{1,0:T(8,128)(2,1)}, bf16[512,256]{1,0:T(8,128)(2,1)}) fusion(bf16[512,512]{1,0:T(8,128)(2,1)S(1)} %fusion.4), kind=kLoop, calls=%fused_computation.26 | loop fusion | bytes 1048576 | tf_op jit(solution)/shard_map/slice | solution.py:200
  (6 shorter events, 0.0 us)
Async XLA Ops:
  0.6 46.0 %copy-start = (bf16[16,512]{1,0:T(8,128)(2,1)S(1)}, bf16[16,512]{1,0:T(8,128)(2,1)}, u32[]{:S(2)}) copy-start(bf16[16,512]{1,0:T(8,128)(2,1)} %param.10) | copy-start | bytes 49156
  2.6 15.7 %collective-permute-start.1 = (bf16[512,512]{1,0:T(8,128)(2,1)S(1)}, bf16[512,512]{1,0:T(8,128)(2,1)S(1)}, u32[]{:S(2)}, u32[]{:S(2)}) collective-permute-start(bf16[512,512]{1,0:T(8,128)(2,1)S(1)} %constant_dynamic-update-slice_fusion), channel_id=1, source_target_pairs={{0,1},{1,2},{2,3},{3,4},{4,5},{5,6},{6,7},{7,8},{8,9},{9,10},{10,1... | collective-permute-start | bytes 1572872 | tf_op jit(solution)/shard_map/ppermute | solution.py:20
  4.5 17.3 %collective-permute-start = (bf16[512,512]{1,0:T(8,128)(2,1)S(1)}, bf16[512,512]{1,0:T(8,128)(2,1)S(1)}, u32[]{:S(2)}, u32[]{:S(2)}) collective-permute-start(bf16[512,512]{1,0:T(8,128)(2,1)S(1)} %constant_dynamic-update-slice_fusion), channel_id=1, source_target_pairs={{0,2},{2,4},{4,6},{6,8},{8,10},{10,12},{12,14},{14,16},{16,18},{18... | collective-permute-start | bytes 1572872 | tf_op jit(solution)/shard_map/ppermute | solution.py:47
  18.3 3.5 %collective-permute-start.2 = (bf16[512,512]{1,0:T(8,128)(2,1)S(1)}, bf16[512,512]{1,0:T(8,128)(2,1)S(1)}, u32[]{:S(2)}, u32[]{:S(2)}) collective-permute-start(bf16[512,512]{1,0:T(8,128)(2,1)S(1)} %collective-permute-done.1), channel_id=1, source_target_pairs={{0,1},{2,3},{4,5},{6,7},{8,9},{10,11},{12,13},{14,15},{16,17},{18,... | collective-permute-start | bytes 1572872 | tf_op jit(solution)/shard_map/ppermute | solution.py:48
  40.3 6.3 %copy-start.1 = (bf16[512,512]{1,0:T(8,128)(2,1)S(1)}, bf16[512,512]{1,0:T(8,128)(2,1)}, u32[]{:S(2)}) copy-start(bf16[512,512]{1,0:T(8,128)(2,1)} %get-tuple-element.5) | copy-start | bytes 1572868
  41.9 22.6 %collective-permute-start.3 = (bf16[512,512]{1,0:T(8,128)(2,1)S(1)}, bf16[512,512]{1,0:T(8,128)(2,1)S(1)}, u32[]{:S(2)}, u32[]{:S(2)}) collective-permute-start(bf16[512,512]{1,0:T(8,128)(2,1)S(1)} %get-tuple-element.13), channel_id=1, source_target_pairs={{1,0},{2,1},{3,2},{4,3},{5,4},{6,5},{7,6},{8,7},{9,8},{10,9},{11,1... | collective-permute-start | bytes 1572872 | tf_op jit(solution)/shard_map/ppermute | solution.py:20
  43.9 20.6 %collective-permute-start.4 = (bf16[512,512]{1,0:T(8,128)(2,1)S(1)}, bf16[512,512]{1,0:T(8,128)(2,1)S(1)}, u32[]{:S(2)}, u32[]{:S(2)}) collective-permute-start(bf16[512,512]{1,0:T(8,128)(2,1)S(1)} %get-tuple-element.14), channel_id=1, source_target_pairs={{2,0},{3,1},{4,2},{5,3},{6,4},{7,5},{8,6},{9,7},{10,8},{11,9},{12,... | collective-permute-start | bytes 1572872 | tf_op jit(solution)/shard_map/ppermute | solution.py:20
  46.9 5.2 %collective-permute-start.5 = (f32[512,16]{0,1:T(8,128)S(1)}, f32[512,16]{0,1:T(8,128)S(1)}, u32[]{:S(2)}, u32[]{:S(2)}) collective-permute-start(f32[512,16]{0,1:T(8,128)S(1)} %fusion.12), channel_id=1, source_target_pairs={{0,64},{32,96},{64,0},{96,32},{128,192},{160,224},{192,128},{224,1... | collective-permute-start | bytes 98312 | tf_op jit(solution)/shard_map/ppermute | solution.py:38
  52.1 7.8 %collective-permute-start.6 = (f32[512,16]{0,1:T(8,128)S(1)}, f32[512,16]{0,1:T(8,128)S(1)}, u32[]{:S(2)}, u32[]{:S(2)}) collective-permute-start(f32[512,16]{0,1:T(8,128)S(1)} %add.79), channel_id=1, source_target_pairs={{0,192},{32,224},{64,128},{96,160},{128,64},{160,96},{192,0},{224,... | collective-permute-start | bytes 98312 | tf_op jit(solution)/shard_map/ppermute | solution.py:38
  60.0 3.9 %collective-permute-start.7 = (f32[512,16]{0,1:T(8,128)S(1)}, f32[512,16]{0,1:T(8,128)S(1)}, u32[]{:S(2)}, u32[]{:S(2)}) collective-permute-start(f32[512,16]{0,1:T(8,128)S(1)} %add.80), channel_id=1, source_target_pairs={{0,32},{32,0},{64,96},{96,64},{128,160},{160,128},{192,224},{224,1... | collective-permute-start | bytes 98312 | tf_op jit(solution)/shard_map/ppermute | solution.py:38
